TPU v7x, 128 devices: a whole 4x4x4 slice. The times are simulated.
128 devices in a mesh: gx: 16 (over y, x_lo, core), gy: 8 (over z, x_hi).
Axes of the slice: x: 4 (x_hi: 2, x_lo: 2; x = x_hi * 2 + x_lo), y: 4, z: 4, core: 2. Of those that a mesh axis runs over, the one named last changes fastest.
Arguments:
- features: bfloat16 [131072, 256], P(('gx', 'gy')), may hold values from -6 to 6
- valid: int32 [131072], P(('gx', 'gy')), may hold values from 0 to 1, as said below
- cotangent: bfloat16 [131072, 256], P(('gx', 'gy')), may hold values from -6 to 6
- gamma: float32 [256], replicated, may hold values from 0.5 to 1.5
- w_qkv: bfloat16 [256, 768], replicated
- w_out: bfloat16 [256, 256], replicated, may hold values from -0.375 to 0.375
Outputs:
- block_out: bfloat16 [131072, 256], P(('gx', 'gy'))
- grad_x: bfloat16 [131072, 256], P(('gx', 'gy'))
- grad_wqkv: float32 [256, 768], replicated
- grad_wout: float32 [256, 256], replicated
- gamma_gradient: float32 [256], replicated
Inputs may be any that keep to these rules, and one draw needn't show every extreme that they name: `valid`: the node that takes the first position of each patch in transposed order is occupied.
All inputs are finite; a program needn't handle non-finite values.
Results may differ from a plain program's by a relative error of at most 0.015.
The roundings to bfloat16 on the way count: a program that leaves them out, or rounds other values in their place, can miss the bound.
Values may be sent and summed in bfloat16 or wider, within the bound.
No kernel may reach another device: no remote copies, remote signals or barrier semaphores. Data moves between devices by JAX's collectives and lax.ppermute only.
A program may use at most 64 MiB of HBM per device.

v0:
```python
import jax
import jax.numpy as jnp
from jax import lax
from jax.sharding import PartitionSpec as P

HEADS = 16
K = 1024


def layer_norm_apply(input_rows, gamma):
    xf = input_rows.astype(jnp.float32)
    centered_input = xf - jnp.mean(xf, -1, keepdims=True)
    reciprocal_deviation = lax.rsqrt(
        jnp.mean(centered_input * centered_input, -1, keepdims=True) + 1e-05
    )
    normalized_input = centered_input * reciprocal_deviation
    return (normalized_input, reciprocal_deviation, (normalized_input * gamma).astype(jnp.bfloat16))


def head_probs(query, keys, keep, scale):
    scores = jnp.dot(query, keys.T, preferred_element_type=jnp.float32) * scale
    scores = jnp.where(keep[None, :], scores, -1e30)
    expo = jnp.exp(scores - jnp.max(scores, -1, keepdims=True))
    return expo / jnp.sum(expo, -1, keepdims=True)


def split_heads(block, heads):
    return block.reshape(block.shape[0], heads, -1).transpose(1, 0, 2)


def join_heads(block):
    return block.transpose(1, 0, 2).reshape(block.shape[1], -1)


def patch_forward(qkv_block, keep, heads):
    width = qkv_block.shape[1] // 3
    scale = (width // heads) ** (-0.5)
    query = split_heads(qkv_block[:, :width], heads)
    keys = split_heads(qkv_block[:, width : 2 * width], heads)
    values = split_heads(qkv_block[:, 2 * width :], heads)

    def one_head(parts):
        probs = head_probs(parts[0], parts[1], keep, scale).astype(jnp.bfloat16)
        return jnp.dot(probs, parts[2], preferred_element_type=jnp.float32).astype(jnp.bfloat16)

    return join_heads(lax.map(one_head, (query, keys, values)))


def patch_backward(qkv_block, keep, grad_block, heads):
    width = qkv_block.shape[1] // 3
    scale = (width // heads) ** (-0.5)
    query = split_heads(qkv_block[:, :width], heads)
    keys = split_heads(qkv_block[:, width : 2 * width], heads)
    values = split_heads(qkv_block[:, 2 * width :], heads)
    grads = split_heads(grad_block, heads)

    def one_head(parts):
        q_head, k_head, v_head, g_head = parts
        probs = head_probs(q_head, k_head, keep, scale)
        rounded = probs.astype(jnp.bfloat16)
        d_value = jnp.dot(rounded.T, g_head, preferred_element_type=jnp.float32).astype(
            jnp.bfloat16
        )
        d_prob = jnp.dot(g_head, v_head.T, preferred_element_type=jnp.float32)
        d_score = (probs * (d_prob - jnp.sum(d_prob * probs, -1, keepdims=True)) * scale).astype(
            jnp.bfloat16
        )
        d_query = jnp.dot(d_score, k_head, preferred_element_type=jnp.float32).astype(jnp.bfloat16)
        d_key = jnp.dot(d_score.T, q_head, preferred_element_type=jnp.float32).astype(jnp.bfloat16)
        return (d_query, d_key, d_value)

    d_query, d_key, d_value = lax.map(one_head, (query, keys, values, grads))
    return jnp.concatenate([join_heads(d_query), join_heads(d_key), join_heads(d_value)], 1)


def relayout_pair(first, second):
    size_x = lax.axis_size("gx")
    size_y = lax.axis_size("gy")
    first_s = first.reshape(size_x * size_y, -1, first.shape[1])
    second_s = second.reshape(size_x * size_y, -1)
    moved_a, moved_b = (
        lax.all_to_all(first_s, ("gx", "gy"), split_axis=0, concat_axis=0, tiled=True),
        lax.all_to_all(second_s, ("gx", "gy"), split_axis=0, concat_axis=0, tiled=True),
    )
    return (moved_a.reshape(first.shape), moved_b.reshape(second.shape))


def relayout_one(array):
    size_x = lax.axis_size("gx")
    size_y = lax.axis_size("gy")
    shaped = array.reshape(size_x * size_y, -1, array.shape[1])
    moved = lax.all_to_all(shaped, ("gx", "gy"), split_axis=0, concat_axis=0, tiled=True)
    return moved.reshape(array.shape)


def shards(features, valid, cotangent, gamma, w_qkv, w_out):
    rows, width = features.shape
    patches = rows // K
    nodes = rows * lax.axis_size("gx") * lax.axis_size("gy")
    inverse_root = float(nodes) ** (-0.5)
    input_rows, occupied = relayout_pair(features, valid.astype(jnp.bfloat16))
    keep = occupied > 0.5
    normalized_input, reciprocal_deviation, hidden_state = layer_norm_apply(input_rows, gamma)
    qkv = jnp.dot(hidden_state, w_qkv, preferred_element_type=jnp.float32).astype(jnp.bfloat16)
    qkv_p = qkv.reshape(patches, K, 3 * width)
    keep_p = keep.reshape(patches, K)
    attn = lax.map(lambda a: patch_forward(a[0], a[1], HEADS), (qkv_p, keep_p)).reshape(rows, width)
    y_val = (
        input_rows.astype(jnp.float32) + jnp.dot(attn, w_out, preferred_element_type=jnp.float32)
    ).astype(jnp.bfloat16)
    y_plain = relayout_one(y_val)
    gt = relayout_one(cotangent)
    local_wout = jnp.dot(attn.T, gt, preferred_element_type=jnp.float32)
    d_attn = jnp.dot(gt, w_out.T, preferred_element_type=jnp.float32).astype(jnp.bfloat16)
    d_attn_p = d_attn.reshape(patches, K, width)
    d_qkv = lax.map(
        lambda a: patch_backward(a[0], a[1], a[2], HEADS), (qkv_p, keep_p, d_attn_p)
    ).reshape(rows, 3 * width)
    local_wqkv = jnp.dot(hidden_state.T, d_qkv, preferred_element_type=jnp.float32)
    hidden_gradient = jnp.dot(d_qkv, w_qkv.T, preferred_element_type=jnp.float32)
    shard_gamma = jnp.sum(hidden_gradient * normalized_input, 0)
    scaled_output = hidden_gradient * gamma
    norm_gradient = reciprocal_deviation * (
        scaled_output
        - jnp.mean(scaled_output, -1, keepdims=True)
        - normalized_input * jnp.mean(scaled_output * normalized_input, -1, keepdims=True)
    )
    d_x = (gt.astype(jnp.float32) + norm_gradient).astype(jnp.bfloat16)
    total_wqkv, total_wout, total_gamma = lax.psum(
        (local_wqkv, local_wout, shard_gamma), ("gx", "gy")
    )
    dx_plain = relayout_one(d_x)
    return (
        y_plain,
        dx_plain,
        total_wqkv * inverse_root,
        total_wout * inverse_root,
        total_gamma * inverse_root,
    )


def solution(mesh):
    placed = (P(("gx", "gy"), None), P(("gx", "gy")), P(("gx", "gy"), None), P(), P(), P())
    return jax.shard_map(
        shards,
        mesh=mesh,
        in_specs=placed,
        out_specs=(P(("gx", "gy"), None), P(("gx", "gy"), None), P(), P(), P()),
        check_vma=False,
    )
```

profile of v0, /device:TPU:1, one launch (start us, length us, event | category | flops | bytes accessed | tf_op | source)
XLA Modules:
  0.0 457.5 jit_solution(11587714062182369944)
XLA Ops:
  8.0 21.2 %all_to_all.30 = bf16[128,1,8]{2,1,0:T(2,128)(2,1)S(1)} all-to-all(bf16[128,1,8]{2,1,0:T(2,128)(2,1)S(1)} %all_to_all.24), channel_id=1, replica_groups=mesh['gx'=16,'gy'=8] {'gx','gy'}, dimensions={0} | all-to-all | bytes 4096 | tf_op jit(solution)/shard_map/all_to_all | solution.py:83
  29.3 4.2 all-to-all-start
  33.8 13.7 %all-to-all-done = bf16[128,8,256]{2,1,0:T(8,128)(2,1)S(1)} async-done(((bf16[128,8,256]{2,1,0:T(8,128)(2,1)}), bf16[128,8,256]{2,1,0:T(8,128)(2,1)S(1)}, u32[]{:S(2)}, u32[]{:S(2)}) %all-to-all-start) | async-done | bytes 524320 | tf_op jit(solution)/shard_map/all_to_all | solution.py:82
  47.4 4.0 all-to-all-start.3
  54.8 10.7 %all-to-all-done.3 = bf16[128,8,256]{2,1,0:T(8,128)(2,1)S(1)} async-done(((bf16[128,8,256]{2,1,0:T(8,128)(2,1)}), bf16[128,8,256]{2,1,0:T(8,128)(2,1)S(1)}, u32[]{:S(2)}, u32[]{:S(2)}) %all-to-all-start.3) | async-done | bytes 524320 | tf_op jit(solution)/shard_map/all_to_all | solution.py:92
  67.6 152.1 %while.41 = (s32[]{:T(128)}, bf16[16,1024,16]{1,2,0:T(8,128)(2,1)S(1)}, bf16[16,1024,16]{1,2,0:T(8,128)(2,1)}, bf16[16,1024,16]{1,2,0:T(8,128)(2,1)}, pred[1024]...) while((s32[]{:T(128)}, ...), condition=%wide.region_10.11_spmd, body=%wide.region_6.10_spmd.sunk | while | flops 195081216 | bytes 36034660 | solution.py:72
  71.2 2.3 multiply_reduce_fusion.3
  73.5 1.9 multiply_convert_fusion.2
  80.7 2.3 multiply_reduce_fusion.3
  83.0 1.9 multiply_convert_fusion.2
  90.2 2.3 multiply_reduce_fusion.3
  92.5 1.9 multiply_convert_fusion.2
  99.7 2.3 multiply_reduce_fusion.3
  102.0 1.9 multiply_convert_fusion.2
  109.2 2.3 multiply_reduce_fusion.3
  111.5 1.9 multiply_convert_fusion.2
  118.7 2.3 multiply_reduce_fusion.3
  121.0 1.9 multiply_convert_fusion.2
  128.2 2.3 multiply_reduce_fusion.3
  130.5 1.9 multiply_convert_fusion.2
  137.7 2.3 multiply_reduce_fusion.3
  140.0 1.9 multiply_convert_fusion.2
  145.3 1.9 fusion.122
  147.2 2.3 multiply_reduce_fusion.3
  149.5 1.9 multiply_convert_fusion.2
  156.8 2.3 multiply_reduce_fusion.3
  159.1 1.9 multiply_convert_fusion.2
  166.3 2.3 multiply_reduce_fusion.3
  168.6 1.9 multiply_convert_fusion.2
  175.8 2.3 multiply_reduce_fusion.3
  178.1 1.9 multiply_convert_fusion.2
  185.3 2.3 multiply_reduce_fusion.3
  187.6 1.9 multiply_convert_fusion.2
  194.8 2.3 multiply_reduce_fusion.3
  197.1 1.9 multiply_convert_fusion.2
  204.3 2.3 multiply_reduce_fusion.3
  206.6 1.9 multiply_convert_fusion.2
  213.8 2.3 multiply_reduce_fusion.3
  216.1 1.9 multiply_convert_fusion.2
  219.8 58.3 %while.40 = (s32[]{:T(128)}, bf16[16,1024,16]{1,2,0:T(8,128)(2,1)S(1)}, pred[1024]{0:T(1024)(128)(4,1)S(1)}, bf16[16,1024,16]{1,2,0:T(8,128)(2,1)S(1)}, bf16[16,...) while((s32[]{:T(128)}, bf16[16,1024,16]{1,2,0:T(8,128)(2,1)S(1)}, ...), condition=%wide.region_5.6_spmd, body=%wide.region_2.5_spmd.sunk | while | flops 79706112 | bytes 12739661 | solution.py:46
  221.5 1.9 fusion.111
  225.2 1.9 fusion.111
  228.8 1.9 fusion.111
  232.4 1.9 fusion.111
  236.1 1.9 fusion.111
  239.7 1.9 fusion.111
  243.4 1.9 fusion.111
  247.0 1.9 fusion.111
  250.7 1.9 fusion.111
  254.3 1.9 fusion.111
  257.9 1.9 fusion.111
  261.6 1.9 fusion.111
  265.2 1.9 fusion.111
  268.9 1.9 fusion.111
  272.5 1.9 fusion.111
  276.2 1.9 fusion.111
  278.1 2.6 fusion.71
  282.3 4.0 all-to-all-start.4
  287.4 3.0 fusion.74
  291.6 8.7 %all-to-all-done.4 = bf16[128,8,256]{2,1,0:T(8,128)(2,1)S(1)} async-done(((bf16[128,8,256]{2,1,0:T(8,128)(2,1)}), bf16[128,8,256]{2,1,0:T(8,128)(2,1)S(1)}, u32[]{:S(2)}, u32[]{:S(2)}) %all-to-all-start.4) | async-done | bytes 524320 | tf_op jit(solution)/shard_map/all_to_all | solution.py:92
  300.3 4.0 all-to-all-start.2
  304.3 68.1 %psum.23 = f32[256]{0:T(256)S(1)} all-reduce(f32[256]{0:T(256)S(1)} %get-tuple-element.117), channel_id=1, replica_groups=mesh['gx'=16,'gy'=8] {'gx','gy'}, use_global_device_ids=true, to_apply=%region_16.17 | all-reduce | flops 256 | bytes 2048 | tf_op jit(solution)/shard_map/psum | solution.py:129
  373.0 72.4 %all-reduce.3.cloned.1.call-done = (f32[256,768]{1,0:T(8,128)}, f32[256,256]{1,0:T(8,128)}) async-done(((f32[256,768]{1,0:T(8,128)}, f32[256,256]{1,0:T(8,128)}), (f32[256,768]{1,0:T(8,128)}, f32[256,256]{1,0:T(8,128)})) %all-reduce.3.cloned.1.call-update) | async-done | bytes 1048592 | tf_op jit(solution)/shard_map/psum | solution.py:129
  445.4 2.1 broadcast_multiply_fusion
  (147 shorter events, 124.0 us)
Async XLA Ops:
  7.2 45.1 %copy-start = (bf16[256,768]{1,0:T(8,128)(2,1)S(1)}, bf16[256,768]{1,0:T(8,128)(2,1)}, u32[]{:S(2)}) copy-start(bf16[256,768]{1,0:T(8,128)(2,1)} %param.14) | copy-start | bytes 1179652
  29.3 18.2 %all-to-all-start = ((bf16[128,8,256]{2,1,0:T(8,128)(2,1)}), bf16[128,8,256]{2,1,0:T(8,128)(2,1)S(1)}, u32[]{:S(2)}, u32[]{:S(2)}) async-start(bf16[128,8,256]{2,1,0:T(8,128)(2,1)} %bitcast.179), calls=%async_computation | async-start | bytes 1048576 | tf_op jit(solution)/shard_map/all_to_all | solution.py:82
  33.6 31.8 %copy-start.1 = (bf16[256,256]{1,0:T(8,128)(2,1)S(1)}, bf16[256,256]{1,0:T(8,128)(2,1)}, u32[]{:S(2)}) copy-start(bf16[256,256]{1,0:T(8,128)(2,1)} %param.15) | copy-start | bytes 393220
  47.4 18.0 %all-to-all-start.3 = ((bf16[128,8,256]{2,1,0:T(8,128)(2,1)}), bf16[128,8,256]{2,1,0:T(8,128)(2,1)S(1)}, u32[]{:S(2)}, u32[]{:S(2)}) async-start(bf16[128,8,256]{2,1,0:T(8,128)(2,1)} %bitcast.180), calls=%async_computation.3 | async-start | bytes 1048576 | tf_op jit(solution)/shard_map/all_to_all | solution.py:92
  219.8 58.3 %copy-start.3 = (f32[256]{0:T(256)S(1)}, f32[256]{0:T(256)}, u32[]{:S(2)}) copy-start(f32[256]{0:T(256)} %param.13) | copy-start | bytes 3076
  282.3 18.0 %all-to-all-start.4 = ((bf16[128,8,256]{2,1,0:T(8,128)(2,1)}), bf16[128,8,256]{2,1,0:T(8,128)(2,1)S(1)}, u32[]{:S(2)}, u32[]{:S(2)}) async-start(bf16[128,8,256]{2,1,0:T(8,128)(2,1)} %fusion.76), calls=%async_computation.4 | async-start | bytes 1048576 | tf_op jit(solution)/shard_map/all_to_all | solution.py:92
  286.3 159.0 %all-reduce.3.cloned.1.call-start = ((), (), s32[]{:S(2)}) async-start(), calls=%async_computation.5 | async-start | bytes 2097152 | tf_op jit(solution)/shard_map/psum | solution.py:129
  286.4 4.1 copy-start.2
  300.3 72.7 %all-to-all-start.2 = ((bf16[128,8,256]{2,1,0:T(8,128)(2,1)}), bf16[128,8,256]{2,1,0:T(8,128)(2,1)S(1)}, u32[]{:S(2)}, u32[]{:S(2)}) async-start(bf16[128,8,256]{2,1,0:T(8,128)(2,1)} %fusion.59), calls=%async_computation.2 | async-start | bytes 1048576 | tf_op jit(solution)/shard_map/all_to_all | solution.py:92
Sparse Core Ops, SparseCore 0:
  292.7 152.6 all-reduce.2
where the time goes:
time: 460 us; the launch traced here: 458 us
  matrix products  160 us (35%)
  waiting for transfers between devices  105 us (23%)
  blocking collectives  89.3 us (19%)
  other arithmetic  67.3 us (15%)
  starting transfers between devices  16.3 us (4%)
  between operations  14.2 us (3%)
  local copies, waits for them, and re-layouts  4.75 us (1%)
    psum x1, waiting for transfers between devices, shards(): lax.psum((local_wqkv, local_wout, shard_gamma), ('gx', 'gy'))  72.4 us
    psum x1, blocking collectives, shards(): lax.psum((local_wqkv, local_wout, shard_gamma), ('gx', 'gy'))  68.1 us
    dot_general x16, matrix products, one_head(): d_prob = jnp.dot(g_head, v_head.T, preferred_element_type=jnp.float32)  36.6 us
    convert_element_type x16, other arithmetic, one_head(): (probs * (d_prob - jnp.sum(d_prob * probs, -1, keepdims=True)) * scale).a...  30.8 us
    dot_general x16, matrix products, one_head(): jnp.dot(probs, parts[2], preferred_element_type=jnp.float32)  30.7 us
    dot_general x16, matrix products, one_head(): jnp.dot(rounded.T, g_head, preferred_element_type=jnp.float32)  30.3 us
    reduce_sum x32, other arithmetic, head_probs(): return expo / jnp.sum(expo, -1, keepdims=True)  29 us
    dot_general x32, matrix products, head_probs(): scores = jnp.dot(query, keys.T, preferred_element_type=jnp.float32) * scale  25.6 us
  transfers between devices with their start and end apart: 5, of which 4 were waited for; matrix products, arithmetic and copies ran while one was open for 2% of the time, Pallas kernels for 0%

commit v1 on v0

v1 whole, which is shorter than its diff:
```python
import functools

import jax
import jax.numpy as jnp
from jax import lax
from jax.experimental import pallas as pl
from jax.experimental.pallas import tpu as pltpu
from jax.sharding import PartitionSpec as P

HEADS = 16
K = 1024
TQ = 256


def layer_norm_apply(input_rows, gamma):
    xf = input_rows.astype(jnp.float32)
    centered_input = xf - jnp.mean(xf, -1, keepdims=True)
    reciprocal_deviation = lax.rsqrt(
        jnp.mean(centered_input * centered_input, -1, keepdims=True) + 1e-05
    )
    normalized_input = centered_input * reciprocal_deviation
    return (normalized_input, reciprocal_deviation, (normalized_input * gamma).astype(jnp.bfloat16))


def _attn_kernel(qkv_ref, do_ref, keep_ref, o_ref, dqkv_ref, *, scale, n, tq):
    qT = qkv_ref[0]
    kT = qkv_ref[1]
    vT = qkv_ref[2]
    doT = do_ref[...]
    keep = keep_ref[...] > 0.5
    d = qT.shape[0]
    dk_acc = jnp.zeros((d, n), jnp.float32)
    dv_acc = jnp.zeros((d, n), jnp.float32)
    for b in range(n // tq):
        cols = slice(b * tq, (b + 1) * tq)
        qT_b = qT[:, cols]
        doT_b = doT[:, cols]
        q_b = qT_b.T
        do_b = doT_b.T
        s = jnp.dot(q_b, kT, preferred_element_type=jnp.float32) * scale
        s = jnp.where(keep, s, -1e30)
        m = jnp.max(s, -1, keepdims=True)
        e = jnp.exp(s - m)
        l = jnp.sum(e, -1, keepdims=True)
        p = e * (1.0 / l)
        pb = p.astype(jnp.bfloat16)
        o_ref[:, cols] = lax.dot_general(
            vT, pb, (((1,), (1,)), ((), ())), preferred_element_type=jnp.float32
        ).astype(o_ref.dtype)
        dv_acc = dv_acc + jnp.dot(doT_b, pb, preferred_element_type=jnp.float32)
        dp = jnp.dot(do_b, vT, preferred_element_type=jnp.float32)
        rs = jnp.sum(dp * p, -1, keepdims=True)
        ds = (p * (dp - rs) * scale).astype(jnp.bfloat16)
        dqkv_ref[0, :, cols] = lax.dot_general(
            kT, ds, (((1,), (1,)), ((), ())), preferred_element_type=jnp.float32
        ).astype(dqkv_ref.dtype)
        dk_acc = dk_acc + jnp.dot(qT_b, ds, preferred_element_type=jnp.float32)
    dqkv_ref[1] = dk_acc.astype(dqkv_ref.dtype)
    dqkv_ref[2] = dv_acc.astype(dqkv_ref.dtype)


def fused_attention(qkvT, doT, keep_row, heads):
    _, c, n = qkvT.shape
    d = c // heads
    scale = d ** (-0.5)
    kernel = functools.partial(_attn_kernel, scale=scale, n=n, tq=TQ)
    flops = heads * 6 * 2 * n * n * d
    return pl.pallas_call(
        kernel,
        grid=(heads,),
        in_specs=[
            pl.BlockSpec((3, d, n), lambda h: (0, h, 0)),
            pl.BlockSpec((d, n), lambda h: (h, 0)),
            pl.BlockSpec((1, n), lambda h: (0, 0)),
        ],
        out_specs=[
            pl.BlockSpec((d, n), lambda h: (h, 0)),
            pl.BlockSpec((3, d, n), lambda h: (0, h, 0)),
        ],
        out_shape=[
            jax.ShapeDtypeStruct((c, n), jnp.bfloat16),
            jax.ShapeDtypeStruct((3, c, n), jnp.bfloat16),
        ],
        compiler_params=pltpu.CompilerParams(dimension_semantics=("arbitrary",)),
        cost_estimate=pl.CostEstimate(
            flops=flops, transcendentals=heads * n * n, bytes_accessed=2 * 8 * c * n
        ),
    )(qkvT, doT, keep_row)


def relayout_pair(first, second):
    size_x = lax.axis_size("gx")
    size_y = lax.axis_size("gy")
    first_s = first.reshape(size_x * size_y, -1, first.shape[1])
    second_s = second.reshape(size_x * size_y, -1)
    moved_a, moved_b = (
        lax.all_to_all(first_s, ("gx", "gy"), split_axis=0, concat_axis=0, tiled=True),
        lax.all_to_all(second_s, ("gx", "gy"), split_axis=0, concat_axis=0, tiled=True),
    )
    return (moved_a.reshape(first.shape), moved_b.reshape(second.shape))


def relayout_one(array):
    size_x = lax.axis_size("gx")
    size_y = lax.axis_size("gy")
    shaped = array.reshape(size_x * size_y, -1, array.shape[1])
    moved = lax.all_to_all(shaped, ("gx", "gy"), split_axis=0, concat_axis=0, tiled=True)
    return moved.reshape(array.shape)


def shards(features, valid, cotangent, gamma, w_qkv, w_out):
    rows, width = features.shape
    patches = rows // K
    nodes = rows * lax.axis_size("gx") * lax.axis_size("gy")
    inverse_root = float(nodes) ** (-0.5)
    input_rows, occupied = relayout_pair(features, valid.astype(jnp.bfloat16))
    normalized_input, reciprocal_deviation, hidden_state = layer_norm_apply(input_rows, gamma)
    qkvT = lax.dot_general(
        w_qkv, hidden_state, (((0,), (1,)), ((), ())), preferred_element_type=jnp.float32
    ).astype(jnp.bfloat16)
    y_keep = occupied.astype(jnp.float32).reshape(1, rows)
    gt = relayout_one(cotangent)
    d_attnT = lax.dot_general(
        w_out, gt, (((1,), (1,)), ((), ())), preferred_element_type=jnp.float32
    ).astype(jnp.bfloat16)
    attnT, d_qkvT = fused_attention(qkvT.reshape(3, width, rows), d_attnT, y_keep, HEADS)
    d_qkvT = d_qkvT.reshape(3 * width, rows)
    y_val = (
        input_rows.astype(jnp.float32)
        + lax.dot_general(attnT, w_out, (((0,), (0,)), ((), ())), preferred_element_type=jnp.float32)
    ).astype(jnp.bfloat16)
    y_plain = relayout_one(y_val)
    local_wout = jnp.dot(attnT, gt, preferred_element_type=jnp.float32)
    local_wqkv = lax.dot_general(
        hidden_state, d_qkvT, (((0,), (1,)), ((), ())), preferred_element_type=jnp.float32
    )
    hidden_gradient = lax.dot_general(
        d_qkvT, w_qkv, (((0,), (1,)), ((), ())), preferred_element_type=jnp.float32
    )
    shard_gamma = jnp.sum(hidden_gradient * normalized_input, 0)
    scaled_output = hidden_gradient * gamma
    norm_gradient = reciprocal_deviation * (
        scaled_output
        - jnp.mean(scaled_output, -1, keepdims=True)
        - normalized_input * jnp.mean(scaled_output * normalized_input, -1, keepdims=True)
    )
    d_x = (gt.astype(jnp.float32) + norm_gradient).astype(jnp.bfloat16)
    total_wqkv, total_wout, total_gamma = lax.psum(
        (local_wqkv, local_wout, shard_gamma), ("gx", "gy")
    )
    dx_plain = relayout_one(d_x)
    return (
        y_plain,
        dx_plain,
        total_wqkv * inverse_root,
        total_wout * inverse_root,
        total_gamma * inverse_root,
    )


def solution(mesh):
    placed = (P(("gx", "gy"), None), P(("gx", "gy")), P(("gx", "gy"), None), P(), P(), P())
    return jax.shard_map(
        shards,
        mesh=mesh,
        in_specs=placed,
        out_specs=(P(("gx", "gy"), None), P(("gx", "gy"), None), P(), P(), P()),
        check_vma=False,
    )
```

time: 460 us -> 320 us (0.70)
  matrix products: 160 us -> 12.3 us
  Pallas kernels: 0 us -> 73.9 us
  other arithmetic: 67.3 us -> 6.52 us
    dot_general x118 -> x6, matrix products: 160 us -> 12.3 us  [the longest x1 3.24 us: shards(): lax.dot_general(hidden_state, d_qkvT, (((0,), (1,)), ((), ())), preferred...]
    pallas_call x0 -> x1, Pallas kernels: none -> 73.9 us  [fused_attention(): pl.pallas_call(kernel, grid=(heads,), in_specs=[pl.BlockSpec((3, d, n), l...]
    convert_element_type x16 -> x1, other arithmetic: 30.8 us -> 0.19 us  [shards(): y_keep = occupied.astype(jnp.float32).reshape(1, rows)]
    reduce_sum x32 -> x0, other arithmetic: 29 us -> none  [head_probs(): return expo / jnp.sum(expo, -1, keepdims=True)]
  transfers between devices with their start and end apart: 5 -> 5, of which waited for: 4 -> 4; matrix products, arithmetic and copies ran while one was open for 2% -> 3% of each run, Pallas kernels for 0% -> 0%
where the time goes in v1:
time: 320 us; the launch traced here: 319 us
  waiting for transfers between devices  104 us (32%)
  blocking collectives  89.5 us (28%)
  Pallas kernels  73.9 us (23%)
  starting transfers between devices  16.6 us (5%)
  between operations  14.2 us (4%)
  matrix products  12.3 us (4%)
  other arithmetic  6.52 us (2%)
    pallas_call x1, Pallas kernels, fused_attention(): pl.pallas_call(kernel, grid=(heads,), in_specs=[pl.BlockSpec((3, d, n), l...  73.9 us
    psum x1, waiting for transfers between devices, shards(): lax.psum((local_wqkv, local_wout, shard_gamma), ('gx', 'gy'))  71.8 us
    psum x1, blocking collectives, shards(): lax.psum((local_wqkv, local_wout, shard_gamma), ('gx', 'gy'))  68.3 us
    all_to_all x1, blocking collectives, relayout_pair(): lax.all_to_all(second_s, ('gx', 'gy'), split_axis=0, concat_axis=0, tiled...  21.2 us
    all_to_all x3, waiting for transfers between devices, relayout_one(): lax.all_to_all(shaped, ('gx', 'gy'), split_axis=0, concat_axis=0, tiled=T...  18.6 us
    all_to_all x1, waiting for transfers between devices, relayout_pair(): lax.all_to_all(first_s, ('gx', 'gy'), split_axis=0, concat_axis=0, tiled=...  13.1 us
    all_to_all x3, starting transfers between devices, relayout_one(): lax.all_to_all(shaped, ('gx', 'gy'), split_axis=0, concat_axis=0, tiled=T...  12.4 us
  transfers between devices with their start and end apart: 5, of which 4 were waited for; matrix products, arithmetic and copies ran while one was open for 3% of the time, Pallas kernels for 0%

profile of v1, /device:TPU:1, one launch (start us, length us, event | category | flops | bytes accessed | tf_op | source)
XLA Modules:
  0.0 319.1 jit_solution(9718452539564685293)
XLA Ops:
  7.2 0.0 copy-start
  7.2 0.7 convert_element_type.61
  7.9 0.1 all_to_all.24
  8.0 21.2 %all_to_all.30 = bf16[128,1,8]{2,1,0:T(2,128)(2,1)S(1)} all-to-all(bf16[128,1,8]{2,1,0:T(2,128)(2,1)S(1)} %all_to_all.24), channel_id=1, replica_groups=mesh['gx'=16,'gy'=8] {'gx','gy'}, dimensions={0} | all-to-all | bytes 4096 | tf_op jit(solution)/shard_map/all_to_all | solution.py:98
  29.3 4.2 %all-to-all-start = ((bf16[128,8,256]{2,1,0:T(8,128)(2,1)}), bf16[128,8,256]{2,1,0:T(8,128)(2,1)S(1)}, u32[]{:S(2)}, u32[]{:S(2)}) async-start(bf16[128,8,256]{2,1,0:T(8,128)(2,1)} %bitcast.69), calls=%async_computation | async-start | bytes 1048576 | tf_op jit(solution)/shard_map/all_to_all | solution.py:97
  33.4 0.0 copy-start.2
  33.4 0.2 convert_reduce_fusion.1
  33.6 0.7 reshape.125.keep_ref
  34.3 13.1 %all-to-all-done = bf16[128,8,256]{2,1,0:T(8,128)(2,1)S(1)} async-done(((bf16[128,8,256]{2,1,0:T(8,128)(2,1)}), bf16[128,8,256]{2,1,0:T(8,128)(2,1)S(1)}, u32[]{:S(2)}, u32[]{:S(2)}) %all-to-all-start) | async-done | bytes 524320 | tf_op jit(solution)/shard_map/all_to_all | solution.py:97
  47.4 4.0 %all-to-all-start.1 = ((bf16[128,8,256]{2,1,0:T(8,128)(2,1)}), bf16[128,8,256]{2,1,0:T(8,128)(2,1)S(1)}, u32[]{:S(2)}, u32[]{:S(2)}) async-start(bf16[128,8,256]{2,1,0:T(8,128)(2,1)} %bitcast.70), calls=%async_computation.1 | async-start | bytes 1048576 | tf_op jit(solution)/shard_map/all_to_all | solution.py:107
  51.4 0.0 copy-start.4
  51.5 0.2 convert_reduce_fusion
  51.7 0.1 div.15
  51.8 0.4 fusion.5
  52.2 0.1 rsqrt.13
  52.3 13.2 %all-to-all-done.1 = bf16[128,8,256]{2,1,0:T(8,128)(2,1)S(1)} async-done(((bf16[128,8,256]{2,1,0:T(8,128)(2,1)}), bf16[128,8,256]{2,1,0:T(8,128)(2,1)S(1)}, u32[]{:S(2)}, u32[]{:S(2)}) %all-to-all-start.1) | async-done | bytes 524320 | tf_op jit(solution)/shard_map/all_to_all | solution.py:107
  65.4 0.0 copy-done.2
  65.5 1.1 convolution_convert_fusion.1.do_ref
  66.6 0.0 copy-done
  66.6 0.0 copy-done.4
  66.6 2.0 convolution_convert_fusion
  68.6 73.9 %shard_map.101 = (bf16[256,1024]{1,0:T(8,128)(2,1)}, bf16[3,256,1024]{2,1,0:T(8,128)(2,1)}) custom-call(bf16[3,256,1024]{2,1,0:T(8,128)(2,1)} %bitcast.68, bf16[256,1024]{1,0:T(8,128)(2,1)} %convolution_convert_fusion.1.do_ref, f32[1,1024]{1,0:T(1,128)} %reshape.125.keep_ref), custom_call_target="tpu_custom_call" | custom-call | flops 3221225472 | bytes 4194304 | tf_op jit(solution)/shard_map/pallas_call | solution.py:68
  142.6 0.0 copy-start.1
  142.6 2.3 fusion.4
  144.8 4.0 %all-to-all-start.3 = ((bf16[128,8,256]{2,1,0:T(8,128)(2,1)}), bf16[128,8,256]{2,1,0:T(8,128)(2,1)S(1)}, u32[]{:S(2)}, u32[]{:S(2)}) async-start(bf16[128,8,256]{2,1,0:T(8,128)(2,1)} %fusion.4), calls=%async_computation.3 | async-start | bytes 1048576 | tf_op jit(solution)/shard_map/all_to_all | solution.py:107
  148.9 0.0 all-reduce.3.cloned.1.call-start
  148.9 0.0 copy-done.1
  148.9 1.0 fusion.25
  149.9 3.2 %fusion.23 = f32[256,768]{1,0:T(8,128)} fusion(bf16[768,1024]{1,0:T(8,128)(2,1)} %bitcast.71, bf16[128,8,256]{2,1,0:T(8,128)(2,1)S(1)} %all-to-all-done, f32[256]{0:T(256)S(1)} %copy-done.4, f32[128,8]{1,0:T(8,128)S(1)} %add_rsqrt_fusion, f32[128,8]{1,0:T(8,128)S(1)} %broadcast_multiply_fusion.2), kind=kOutput, calls=%fused_computation.29 | convolution fusion | flops 403963904 | bytes 2892800 | tf_op jit(solution)/shard_map/dot_general | solution.py:134
  153.2 0.0 all-reduce.3.cloned.1.call-update
  153.2 2.6 fusion.19
  155.8 1.6 fusion.20
  157.4 5.4 %all-to-all-done.3 = bf16[128,8,256]{2,1,0:T(8,128)(2,1)S(1)} async-done(((bf16[128,8,256]{2,1,0:T(8,128)(2,1)}), bf16[128,8,256]{2,1,0:T(8,128)(2,1)S(1)}, u32[]{:S(2)}, u32[]{:S(2)}) %all-to-all-start.3) | async-done | bytes 524320 | tf_op jit(solution)/shard_map/all_to_all | solution.py:107
  162.9 4.3 %all-to-all-start.4 = ((bf16[128,8,256]{2,1,0:T(8,128)(2,1)}), bf16[128,8,256]{2,1,0:T(8,128)(2,1)S(1)}, u32[]{:S(2)}, u32[]{:S(2)}) async-start(bf16[128,8,256]{2,1,0:T(8,128)(2,1)} %fusion.20), calls=%async_computation.4 | async-start | bytes 1048576 | tf_op jit(solution)/shard_map/all_to_all | solution.py:107
  167.2 68.3 %psum.23 = f32[256]{0:T(256)S(1)} all-reduce(f32[256]{0:T(256)S(1)} %get-tuple-element.9), channel_id=1, replica_groups=mesh['gx'=16,'gy'=8] {'gx','gy'}, use_global_device_ids=true, to_apply=%region_7.0 | all-reduce | flops 256 | bytes 2048 | tf_op jit(solution)/shard_map/psum | solution.py:148
  235.5 0.6 broadcast_multiply_fusion.5
  236.0 0.0 all-to-all-done.4
  236.0 71.8 %all-reduce.3.cloned.1.call-done = (f32[256,768]{1,0:T(8,128)}, f32[256,256]{1,0:T(8,128)}) async-done(((f32[256,768]{1,0:T(8,128)}, f32[256,256]{1,0:T(8,128)}), (f32[256,768]{1,0:T(8,128)}, f32[256,256]{1,0:T(8,128)})) %all-reduce.3.cloned.1.call-update) | async-done | bytes 1048592 | tf_op jit(solution)/shard_map/psum | solution.py:148
  307.8 0.0 copy-start.3
  307.8 2.1 broadcast_multiply_fusion
  309.9 0.0 copy-done.3
  309.9 0.7 broadcast_multiply_fusion.1
  310.7 0.8 copy.16
  311.5 0.8 copy.17
  (3 shorter events, 0.0 us)
Async XLA Ops:
  7.2 59.4 %copy-start = (bf16[256,768]{1,0:T(8,128)(2,1)S(1)}, bf16[256,768]{1,0:T(8,128)(2,1)}, u32[]{:S(2)}) copy-start(bf16[256,768]{1,0:T(8,128)(2,1)} %param.10) | copy-start | bytes 1179652
  29.3 18.2 %all-to-all-start = ((bf16[128,8,256]{2,1,0:T(8,128)(2,1)}), bf16[128,8,256]{2,1,0:T(8,128)(2,1)S(1)}, u32[]{:S(2)}, u32[]{:S(2)}) async-start(bf16[128,8,256]{2,1,0:T(8,128)(2,1)} %bitcast.69), calls=%async_computation | async-start | bytes 1048576 | tf_op jit(solution)/shard_map/all_to_all | solution.py:97
  33.4 32.0 %copy-start.2 = (bf16[256,256]{1,0:T(8,128)(2,1)S(1)}, bf16[256,256]{1,0:T(8,128)(2,1)}, u32[]{:S(2)}) copy-start(bf16[256,256]{1,0:T(8,128)(2,1)} %param.11) | copy-start | bytes 393220
  47.4 18.0 %all-to-all-start.1 = ((bf16[128,8,256]{2,1,0:T(8,128)(2,1)}), bf16[128,8,256]{2,1,0:T(8,128)(2,1)S(1)}, u32[]{:S(2)}, u32[]{:S(2)}) async-start(bf16[128,8,256]{2,1,0:T(8,128)(2,1)} %bitcast.70), calls=%async_computation.1 | async-start | bytes 1048576 | tf_op jit(solution)/shard_map/all_to_all | solution.py:107
  51.4 15.1 %copy-start.4 = (f32[256]{0:T(256)S(1)}, f32[256]{0:T(256)}, u32[]{:S(2)}) copy-start(f32[256]{0:T(256)} %param.9) | copy-start | bytes 3076
  142.6 6.4 %copy-start.1 = (bf16[256,1024]{1,0:T(8,128)(2,1)S(1)}, bf16[256,1024]{1,0:T(8,128)(2,1)}, u32[]{:S(2)}) copy-start(bf16[256,1024]{1,0:T(8,128)(2,1)} %get-tuple-element.7) | copy-start | bytes 1572868
  144.8 18.0 %all-to-all-start.3 = ((bf16[128,8,256]{2,1,0:T(8,128)(2,1)}), bf16[128,8,256]{2,1,0:T(8,128)(2,1)S(1)}, u32[]{:S(2)}, u32[]{:S(2)}) async-start(bf16[128,8,256]{2,1,0:T(8,128)(2,1)} %fusion.4), calls=%async_computation.3 | async-start | bytes 1048576 | tf_op jit(solution)/shard_map/all_to_all | solution.py:107
  148.9 158.9 %all-reduce.3.cloned.1.call-start = ((), (), s32[]{:S(2)}) async-start(), calls=%async_computation.5 | async-start | bytes 2097152 | tf_op jit(solution)/shard_map/psum | solution.py:148
  162.9 73.2 %all-to-all-start.4 = ((bf16[128,8,256]{2,1,0:T(8,128)(2,1)}), bf16[128,8,256]{2,1,0:T(8,128)(2,1)S(1)}, u32[]{:S(2)}, u32[]{:S(2)}) async-start(bf16[128,8,256]{2,1,0:T(8,128)(2,1)} %fusion.20), calls=%async_computation.4 | async-start | bytes 1048576 | tf_op jit(solution)/shard_map/all_to_all | solution.py:107
  307.8 2.1 copy-start.3
Sparse Core Ops, SparseCore 0:
  155.2 152.5 all-reduce.2

commit v2 on v1

--- a/solution.py
+++ b/solution.py
@@ -88,48 +88,51 @@
     )(qkvT, doT, keep_row)
 
 
-def relayout_pair(first, second):
-    size_x = lax.axis_size("gx")
-    size_y = lax.axis_size("gy")
-    first_s = first.reshape(size_x * size_y, -1, first.shape[1])
-    second_s = second.reshape(size_x * size_y, -1)
-    moved_a, moved_b = (
-        lax.all_to_all(first_s, ("gx", "gy"), split_axis=0, concat_axis=0, tiled=True),
-        lax.all_to_all(second_s, ("gx", "gy"), split_axis=0, concat_axis=0, tiled=True),
-    )
-    return (moved_a.reshape(first.shape), moved_b.reshape(second.shape))
-
-
-def relayout_one(array):
-    size_x = lax.axis_size("gx")
-    size_y = lax.axis_size("gy")
-    shaped = array.reshape(size_x * size_y, -1, array.shape[1])
+def to_all(array):
+    size = lax.axis_size("gx") * lax.axis_size("gy")
+    shaped = array.reshape(size, -1, array.shape[-1])
     moved = lax.all_to_all(shaped, ("gx", "gy"), split_axis=0, concat_axis=0, tiled=True)
     return moved.reshape(array.shape)
 
 
+def sum_all(parts):
+    size = lax.axis_size("gx") * lax.axis_size("gy")
+    matrix, vector = parts
+    rows, cols = matrix.shape
+    per = rows // size
+    side = jnp.zeros((size, per, 128), jnp.float32).at[:, :, 0].set(vector.reshape(size, per))
+    payload = jnp.concatenate([matrix.reshape(size, per, cols), side], 2)
+    moved = lax.all_to_all(payload, ("gx", "gy"), split_axis=0, concat_axis=0, tiled=True)
+    mine = jnp.sum(moved, 0, keepdims=True)
+    spread = jnp.broadcast_to(mine, payload.shape)
+    total = lax.all_to_all(spread, ("gx", "gy"), split_axis=0, concat_axis=0, tiled=True)
+    return total[:, :, :cols].reshape(rows, cols), total[:, :, cols].reshape(rows)
+
+
 def shards(features, valid, cotangent, gamma, w_qkv, w_out):
     rows, width = features.shape
-    patches = rows // K
     nodes = rows * lax.axis_size("gx") * lax.axis_size("gy")
     inverse_root = float(nodes) ** (-0.5)
-    input_rows, occupied = relayout_pair(features, valid.astype(jnp.bfloat16))
+    flag = jnp.zeros((rows, 128), jnp.bfloat16).at[:, 0].set(valid.astype(jnp.bfloat16))
+    moved = to_all(jnp.concatenate([features, cotangent, flag], 1))
+    input_rows = moved[:, :width]
+    gt = moved[:, width : 2 * width]
+    occupied = moved[:, 2 * width]
     normalized_input, reciprocal_deviation, hidden_state = layer_norm_apply(input_rows, gamma)
     qkvT = lax.dot_general(
         w_qkv, hidden_state, (((0,), (1,)), ((), ())), preferred_element_type=jnp.float32
     ).astype(jnp.bfloat16)
-    y_keep = occupied.astype(jnp.float32).reshape(1, rows)
-    gt = relayout_one(cotangent)
+    keep_row = occupied.astype(jnp.float32).reshape(1, rows)
     d_attnT = lax.dot_general(
         w_out, gt, (((1,), (1,)), ((), ())), preferred_element_type=jnp.float32
     ).astype(jnp.bfloat16)
-    attnT, d_qkvT = fused_attention(qkvT.reshape(3, width, rows), d_attnT, y_keep, HEADS)
+    attnT, d_qkvT = fused_attention(qkvT.reshape(3, width, rows), d_attnT, keep_row, HEADS)
     d_qkvT = d_qkvT.reshape(3 * width, rows)
     y_val = (
         input_rows.astype(jnp.float32)
         + lax.dot_general(attnT, w_out, (((0,), (0,)), ((), ())), preferred_element_type=jnp.float32)
     ).astype(jnp.bfloat16)
-    y_plain = relayout_one(y_val)
+    y_plain = to_all(y_val)
     local_wout = jnp.dot(attnT, gt, preferred_element_type=jnp.float32)
     local_wqkv = lax.dot_general(
         hidden_state, d_qkvT, (((0,), (1,)), ((), ())), preferred_element_type=jnp.float32
@@ -145,15 +148,15 @@
         - normalized_input * jnp.mean(scaled_output * normalized_input, -1, keepdims=True)
     )
     d_x = (gt.astype(jnp.float32) + norm_gradient).astype(jnp.bfloat16)
-    total_wqkv, total_wout, total_gamma = lax.psum(
-        (local_wqkv, local_wout, shard_gamma), ("gx", "gy")
+    total_w, total_gamma = sum_all(
+        (jnp.concatenate([local_wqkv, local_wout], 1), shard_gamma)
     )
-    dx_plain = relayout_one(d_x)
+    dx_plain = to_all(d_x)
     return (
         y_plain,
         dx_plain,
-        total_wqkv * inverse_root,
-        total_wout * inverse_root,
+        total_w[:, : 3 * width] * inverse_root,
+        total_w[:, 3 * width :] * inverse_root,
         total_gamma * inverse_root,
     )
 

time: 320 us -> 216 us (0.68)
  blocking collectives: 89.5 us -> 33.5 us
  waiting for transfers between devices: 104 us -> 56.2 us
  between operations: 14.2 us -> 0.78 us
  local copies, waits for them, and re-layouts: 2.6 us -> 8.94 us
  other arithmetic: 6.52 us -> 12.2 us
    psum x1 -> x0, waiting for transfers between devices: 71.8 us -> none  [shards(): lax.psum((local_wqkv, local_wout, shard_gamma), ('gx', 'gy'))]
    psum x1 -> x0, blocking collectives: 68.3 us -> none  [shards(): lax.psum((local_wqkv, local_wout, shard_gamma), ('gx', 'gy'))]
    all_to_all x4, waiting for transfers between devices: 31.7 us -> 56.2 us  [the longest x1 20.9 us: sum_all(): lax.all_to_all(spread, ('gx', 'gy'), split_axis=0, concat_axis=0, tiled=T...]
    all_to_all x1, blocking collectives: 21.2 us -> 33.5 us  [to_all(): lax.all_to_all(shaped, ('gx', 'gy'), split_axis=0, concat_axis=0, tiled=T...]
    reshape x0 -> x2, local copies, waits for them, and re-layouts: none -> 3.79 us  [the longest x1 1.94 us: sum_all(): total[:, :, :cols].reshape(rows, cols)]
  transfers between devices with their start and end apart: 5 -> 4, of which waited for: 4 -> 4; matrix products, arithmetic and copies ran while one was open for 3% -> 6% of each run, Pallas kernels for 0% -> 0%
where the time goes in v2:
time: 216 us; the launch traced here: 215 us
  Pallas kernels  73.9 us (34%)
  waiting for transfers between devices  56.2 us (26%)
  blocking collectives  33.5 us (16%)
  starting transfers between devices  18.2 us (8%)
  other arithmetic  12.2 us (6%)
  matrix products  11.4 us (5%)
  local copies, waits for them, and re-layouts  8.94 us (4%)
    pallas_call x1, Pallas kernels, fused_attention(): pl.pallas_call(kernel, grid=(heads,), in_specs=[pl.BlockSpec((3, d, n), l...  73.9 us
    all_to_all x1, blocking collectives, to_all(): lax.all_to_all(shaped, ('gx', 'gy'), split_axis=0, concat_axis=0, tiled=T...  33.5 us
    all_to_all x1, waiting for transfers between devices, sum_all(): lax.all_to_all(spread, ('gx', 'gy'), split_axis=0, concat_axis=0, tiled=T...  20.9 us
    all_to_all x1, waiting for transfers between devices, sum_all(): lax.all_to_all(payload, ('gx', 'gy'), split_axis=0, concat_axis=0, tiled=...  18.2 us
    all_to_all x2, waiting for transfers between devices, to_all(): lax.all_to_all(shaped, ('gx', 'gy'), split_axis=0, concat_axis=0, tiled=T...  17.1 us
    all_to_all x2, starting transfers between devices, to_all(): lax.all_to_all(shaped, ('gx', 'gy'), split_axis=0, concat_axis=0, tiled=T...  8 us
    all_to_all x1, starting transfers between devices, sum_all(): lax.all_to_all(payload, ('gx', 'gy'), split_axis=0, concat_axis=0, tiled=...  6.22 us
  transfers between devices with their start and end apart: 4, of which 4 were waited for; matrix products, arithmetic and copies ran while one was open for 6% of the time, Pallas kernels for 0%

profile of v2, /device:TPU:1, one launch (start us, length us, event | category | flops | bytes accessed | tf_op | source)
XLA Modules:
  0.0 215.3 jit_solution(4037730931390408625)
XLA Ops:
  0.6 0.0 copy-start
  0.6 0.6 compare_reduce_fusion
  1.3 1.3 convert_select_fusion
  2.6 0.2 reshape.153
  2.8 1.3 fusion.2
  4.1 33.5 %all_to_all.25 = bf16[128,8,640]{2,1,0:T(8,128)(2,1)S(1)} all-to-all(bf16[128,8,640]{2,1,0:T(8,128)(2,1)S(1)} %fusion.2), channel_id=1, replica_groups=mesh['gx'=16,'gy'=8] {'gx','gy'}, dimensions={0} | all-to-all | bytes 2621440 | tf_op jit(solution)/shard_map/all_to_all | solution.py:94
  37.7 0.0 copy-start.4
  37.7 0.0 copy-start.5
  37.7 0.7 convert_reduce_fusion.1
  38.4 0.2 convert_reduce_fusion
  38.6 0.4 fusion.20
  39.0 0.0 copy-done.4
  39.0 1.1 fusion.10.do_ref
  40.2 0.0 copy-done
  40.2 0.0 copy-done.5
  40.2 2.0 convolution_convert_fusion
  42.2 73.9 %shard_map.101 = (bf16[256,1024]{1,0:T(8,128)(2,1)}, bf16[3,256,1024]{2,1,0:T(8,128)(2,1)}) custom-call(bf16[3,256,1024]{2,1,0:T(8,128)(2,1)} %bitcast.39, bf16[256,1024]{1,0:T(8,128)(2,1)} %fusion.10.do_ref, f32[1,1024]{1,0:T(1,128)} %bitcast.36), custom_call_target="tpu_custom_call" | custom-call | flops 3221225472 | bytes 4194304 | tf_op jit(solution)/shard_map/pallas_call | solution.py:68
  116.1 0.0 copy-start.3
  116.1 1.4 fusion.22
  117.6 0.0 copy-done.3
  117.6 1.2 fusion.11
  118.7 4.0 %all-to-all-start.1 = ((bf16[128,8,256]{2,1,0:T(8,128)(2,1)}), bf16[128,8,256]{2,1,0:T(8,128)(2,1)S(1)}, u32[]{:S(2)}, u32[]{:S(2)}) async-start(bf16[128,8,256]{2,1,0:T(8,128)(2,1)} %fusion.11), calls=%async_computation.1 | async-start | bytes 1048576 | tf_op jit(solution)/shard_map/all_to_all | solution.py:94
  122.7 2.4 %fusion.26 = f32[256,768]{1,0:T(8,128)S(1)} fusion(bf16[768,1024]{1,0:T(8,128)(2,1)} %bitcast.37, f32[256]{0:T(256)S(1)} %copy-done.5, f32[1024]{0:T(1024)S(1)} %add_rsqrt_fusion, f32[1024]{0:T(1024)S(1)} %broadcast_multiply_fusion.2, bf16[1024,640]{1,0:T(8,128)(2,1)S(1)} %bitcast.31), kind=kOutput, calls=%fused_computation.45 | convolution fusion | flops 403963904 | bytes 2892800 | tf_op jit(solution)/shard_map/dot_general | solution.py:137
  125.1 1.1 pad_maximum_fusion
  126.2 1.8 reshape.149
  128.0 3.4 %fusion.19 = (f32[256]{0:T(256)S(1)}, f32[1024]{0:T(1024)S(1)}, f32[1024]{0:T(1024)S(1)}, f32[1024,256]{1,0:T(8,128)}) fusion(f32[1024]{0:T(1024)S(1)} %add_rsqrt_fusion, f32[1024]{0:T(1024)S(1)} %broadcast_multiply_fusion.2, bf16[1024,640]{1,0:T(8,128)(2,1)S(1)} %bitcast.32, f32[256]{0:T(256)S(1)} %copy-done.5, bf16[768,1024]{1,0:T(8,128)(2,1)} %bitcast.38, ...), kind=kOutput, calls=%fused_computation.26 | convolution fusion | flops 405010176 | bytes 3557376 | tf_op jit(solution)/shard_map/dot_general | solution.py:140
  131.4 0.3 reshape.155
  131.7 1.5 fusion.12
  133.2 3.6 %all-to-all-done.1 = bf16[128,8,256]{2,1,0:T(8,128)(2,1)S(1)} async-done(((bf16[128,8,256]{2,1,0:T(8,128)(2,1)}), bf16[128,8,256]{2,1,0:T(8,128)(2,1)S(1)}, u32[]{:S(2)}, u32[]{:S(2)}) %all-to-all-start.1) | async-done | bytes 524320 | tf_op jit(solution)/shard_map/all_to_all | solution.py:94
  136.8 6.2 %all-to-all-start.3 = ((f32[128,2,1152]{2,1,0:T(2,128)}), f32[128,2,1152]{2,1,0:T(2,128)S(1)}, u32[]{:S(2)}, u32[]{:S(2)}) async-start(f32[128,2,1152]{2,1,0:T(2,128)} %fusion.12), calls=%async_computation.3 | async-start | bytes 2359296 | tf_op jit(solution)/shard_map/all_to_all | solution.py:105
  143.0 2.6 %fusion.21 = bf16[128,8,256]{2,1,0:T(8,128)(2,1)} fusion(f32[1024,256]{1,0:T(8,128)} %get-tuple-element.36, f32[1024]{0:T(1024)S(1)} %get-tuple-element.37, f32[1024]{0:T(1024)S(1)} %get-tuple-element.38, f32[256]{0:T(256)S(1)} %copy-done.5, f32[1024]{0:T(1024)S(1)} %add_rsqrt_fusion, f32[1024]{0:T(1024)S(1)} %broadcast_multiply_fusion.2, ...), kind=kLoop, calls=%fused_computation.31 | loop fusion | flops 2883584 | bytes 2638848 | tf_op jit(solution)/shard_map/reshape | solution.py:93
  145.6 18.2 %all-to-all-done.3 = f32[128,2,1152]{2,1,0:T(2,128)S(1)} async-done(((f32[128,2,1152]{2,1,0:T(2,128)}), f32[128,2,1152]{2,1,0:T(2,128)S(1)}, u32[]{:S(2)}, u32[]{:S(2)}) %all-to-all-start.3) | async-done | bytes 1179680 | tf_op jit(solution)/shard_map/all_to_all | solution.py:105
  163.8 4.0 %all-to-all-start.2 = ((bf16[128,8,256]{2,1,0:T(8,128)(2,1)}), bf16[128,8,256]{2,1,0:T(8,128)(2,1)S(1)}, u32[]{:S(2)}, u32[]{:S(2)}) async-start(bf16[128,8,256]{2,1,0:T(8,128)(2,1)} %fusion.21), calls=%async_computation.2 | async-start | bytes 1048576 | tf_op jit(solution)/shard_map/all_to_all | solution.py:94
  167.8 0.4 reduce_sum.59
  168.2 13.6 %all-to-all-done.2 = bf16[128,8,256]{2,1,0:T(8,128)(2,1)S(1)} async-done(((bf16[128,8,256]{2,1,0:T(8,128)(2,1)}), bf16[128,8,256]{2,1,0:T(8,128)(2,1)S(1)}, u32[]{:S(2)}, u32[]{:S(2)}) %all-to-all-start.2) | async-done | bytes 524320 | tf_op jit(solution)/shard_map/all_to_all | solution.py:94
  181.8 0.0 copy-start.1
  181.8 1.3 broadcast_in_dim.2
  183.2 0.0 copy-done.1
  183.2 4.0 %all-to-all-start.4 = ((f32[128,2,1152]{2,1,0:T(2,128)}), f32[128,2,1152]{2,1,0:T(2,128)S(1)}, u32[]{:S(2)}, u32[]{:S(2)}) async-start(f32[128,2,1152]{2,1,0:T(2,128)} %broadcast_in_dim.2), calls=%async_computation.4 | async-start | bytes 2359296 | tf_op jit(solution)/shard_map/all_to_all | solution.py:108
  187.2 20.9 %all-to-all-done.4 = f32[128,2,1152]{2,1,0:T(2,128)S(1)} async-done(((f32[128,2,1152]{2,1,0:T(2,128)}), f32[128,2,1152]{2,1,0:T(2,128)S(1)}, u32[]{:S(2)}, u32[]{:S(2)}) %all-to-all-start.4) | async-done | bytes 1179680 | tf_op jit(solution)/shard_map/all_to_all | solution.py:108
  208.0 1.1 slice.64
  209.1 1.9 reshape.151
  211.1 0.7 slice_multiply_fusion.1
  211.8 1.0 slice_multiply_fusion
  212.7 0.0 copy-start.2
  212.7 0.2 fusion.25
  213.0 0.7 mul.83
  213.7 0.8 copy.28
  214.5 0.0 copy-done.2
  214.5 0.8 copy.29
  (3 shorter events, 0.0 us)
Async XLA Ops:
  0.6 39.5 %copy-start = (bf16[256,768]{1,0:T(8,128)(2,1)S(1)}, bf16[256,768]{1,0:T(8,128)(2,1)}, u32[]{:S(2)}) copy-start(bf16[256,768]{1,0:T(8,128)(2,1)} %param.14) | copy-start | bytes 1179652
  37.7 1.3 copy-start.4
  37.7 2.5 %copy-start.5 = (f32[256]{0:T(256)S(1)}, f32[256]{0:T(256)}, u32[]{:S(2)}) copy-start(f32[256]{0:T(256)} %param.13) | copy-start | bytes 3076
  116.1 1.4 copy-start.3
  118.7 18.0 %all-to-all-start.1 = ((bf16[128,8,256]{2,1,0:T(8,128)(2,1)}), bf16[128,8,256]{2,1,0:T(8,128)(2,1)S(1)}, u32[]{:S(2)}, u32[]{:S(2)}) async-start(bf16[128,8,256]{2,1,0:T(8,128)(2,1)} %fusion.11), calls=%async_computation.1 | async-start | bytes 1048576 | tf_op jit(solution)/shard_map/all_to_all | solution.py:94
  136.8 27.1 %all-to-all-start.3 = ((f32[128,2,1152]{2,1,0:T(2,128)}), f32[128,2,1152]{2,1,0:T(2,128)S(1)}, u32[]{:S(2)}, u32[]{:S(2)}) async-start(f32[128,2,1152]{2,1,0:T(2,128)} %fusion.12), calls=%async_computation.3 | async-start | bytes 2359296 | tf_op jit(solution)/shard_map/all_to_all | solution.py:105
  163.8 18.0 %all-to-all-start.2 = ((bf16[128,8,256]{2,1,0:T(8,128)(2,1)}), bf16[128,8,256]{2,1,0:T(8,128)(2,1)S(1)}, u32[]{:S(2)}, u32[]{:S(2)}) async-start(bf16[128,8,256]{2,1,0:T(8,128)(2,1)} %fusion.21), calls=%async_computation.2 | async-start | bytes 1048576 | tf_op jit(solution)/shard_map/all_to_all | solution.py:94
  181.8 1.3 copy-start.1
  183.2 24.9 %all-to-all-start.4 = ((f32[128,2,1152]{2,1,0:T(2,128)}), f32[128,2,1152]{2,1,0:T(2,128)S(1)}, u32[]{:S(2)}, u32[]{:S(2)}) async-start(f32[128,2,1152]{2,1,0:T(2,128)} %broadcast_in_dim.2), calls=%async_computation.4 | async-start | bytes 2359296 | tf_op jit(solution)/shard_map/all_to_all | solution.py:108
  212.7 1.7 copy-start.2

commit v3 on v2

--- a/solution.py
+++ b/solution.py
@@ -7,8 +7,8 @@
 from jax.experimental.pallas import tpu as pltpu
 from jax.sharding import PartitionSpec as P
 
+
 HEADS = 16
-K = 1024
 TQ = 256
 
 
@@ -59,18 +59,18 @@
     dqkv_ref[2] = dv_acc.astype(dqkv_ref.dtype)
 
 
-def fused_attention(qkvT, doT, keep_row, heads):
+def fused_attention(qkvT, doT, keep_row, heads, first, count):
     _, c, n = qkvT.shape
     d = c // heads
     scale = d ** (-0.5)
     kernel = functools.partial(_attn_kernel, scale=scale, n=n, tq=TQ)
-    flops = heads * 6 * 2 * n * n * d
+    flops = count * 6 * 2 * n * n * d
     return pl.pallas_call(
         kernel,
-        grid=(heads,),
+        grid=(count,),
         in_specs=[
-            pl.BlockSpec((3, d, n), lambda h: (0, h, 0)),
-            pl.BlockSpec((d, n), lambda h: (h, 0)),
+            pl.BlockSpec((3, d, n), lambda h: (0, h + first, 0)),
+            pl.BlockSpec((d, n), lambda h: (h + first, 0)),
             pl.BlockSpec((1, n), lambda h: (0, 0)),
         ],
         out_specs=[
@@ -78,12 +78,12 @@
             pl.BlockSpec((3, d, n), lambda h: (0, h, 0)),
         ],
         out_shape=[
-            jax.ShapeDtypeStruct((c, n), jnp.bfloat16),
-            jax.ShapeDtypeStruct((3, c, n), jnp.bfloat16),
+            jax.ShapeDtypeStruct((count * d, n), jnp.bfloat16),
+            jax.ShapeDtypeStruct((3, count * d, n), jnp.bfloat16),
         ],
         compiler_params=pltpu.CompilerParams(dimension_semantics=("arbitrary",)),
         cost_estimate=pl.CostEstimate(
-            flops=flops, transcendentals=heads * n * n, bytes_accessed=2 * 8 * c * n
+            flops=flops, transcendentals=count * n * n, bytes_accessed=2 * 8 * count * d * n
         ),
     )(qkvT, doT, keep_row)
 
@@ -95,24 +95,32 @@
     return moved.reshape(array.shape)
 
 
-def sum_all(parts):
+def scatter_sum(payload):
+    moved = lax.all_to_all(payload, ("gx", "gy"), split_axis=0, concat_axis=0, tiled=True)
+    return jnp.sum(moved, 0, keepdims=True)
+
+
+def gather_all(chunk, size):
+    spread = jnp.broadcast_to(chunk, (size,) + chunk.shape[1:])
+    return lax.all_to_all(spread, ("gx", "gy"), split_axis=0, concat_axis=0, tiled=True)
+
+
+def half_grads(hidden_state, d_qkvT_half, attnT_half, gt):
+    wq = lax.dot_general(
+        hidden_state, d_qkvT_half.reshape(-1, d_qkvT_half.shape[-1]),
+        (((0,), (1,)), ((), ())), preferred_element_type=jnp.float32,
+    )
+    wo = jnp.dot(attnT_half, gt, preferred_element_type=jnp.float32)
+    return wq, wo
+
+
+def block(features, valid, cotangent, gamma, w_qkv, w_out):
+    rows, width = features.shape
     size = lax.axis_size("gx") * lax.axis_size("gy")
-    matrix, vector = parts
-    rows, cols = matrix.shape
-    per = rows // size
-    side = jnp.zeros((size, per, 128), jnp.float32).at[:, :, 0].set(vector.reshape(size, per))
-    payload = jnp.concatenate([matrix.reshape(size, per, cols), side], 2)
-    moved = lax.all_to_all(payload, ("gx", "gy"), split_axis=0, concat_axis=0, tiled=True)
-    mine = jnp.sum(moved, 0, keepdims=True)
-    spread = jnp.broadcast_to(mine, payload.shape)
-    total = lax.all_to_all(spread, ("gx", "gy"), split_axis=0, concat_axis=0, tiled=True)
-    return total[:, :, :cols].reshape(rows, cols), total[:, :, cols].reshape(rows)
-
-
-def shards(features, valid, cotangent, gamma, w_qkv, w_out):
-    rows, width = features.shape
-    nodes = rows * lax.axis_size("gx") * lax.axis_size("gy")
+    nodes = rows * size
     inverse_root = float(nodes) ** (-0.5)
+    half = HEADS // 2
+    hw = width // 2
     flag = jnp.zeros((rows, 128), jnp.bfloat16).at[:, 0].set(valid.astype(jnp.bfloat16))
     moved = to_all(jnp.concatenate([features, cotangent, flag], 1))
     input_rows = moved[:, :width]
@@ -121,22 +129,28 @@
     normalized_input, reciprocal_deviation, hidden_state = layer_norm_apply(input_rows, gamma)
     qkvT = lax.dot_general(
         w_qkv, hidden_state, (((0,), (1,)), ((), ())), preferred_element_type=jnp.float32
-    ).astype(jnp.bfloat16)
+    ).astype(jnp.bfloat16).reshape(3, width, rows)
     keep_row = occupied.astype(jnp.float32).reshape(1, rows)
     d_attnT = lax.dot_general(
         w_out, gt, (((1,), (1,)), ((), ())), preferred_element_type=jnp.float32
     ).astype(jnp.bfloat16)
-    attnT, d_qkvT = fused_attention(qkvT.reshape(3, width, rows), d_attnT, keep_row, HEADS)
-    d_qkvT = d_qkvT.reshape(3 * width, rows)
+
+    attn_a, dqkv_a = fused_attention(qkvT, d_attnT, keep_row, HEADS, 0, half)
+    wq_a, wo_a = half_grads(hidden_state, dqkv_a, attn_a, gt)
+    sizes_a = (wq_a.size, wo_a.size)
+    pay_a = jnp.concatenate([wq_a.reshape(-1), wo_a.reshape(-1)]).reshape(size, -1, 128)
+    mine_a = scatter_sum(pay_a)
+    attn_b, dqkv_b = fused_attention(qkvT, d_attnT, keep_row, HEADS, half, half)
+    total_a = gather_all(mine_a, size).reshape(-1)
+
+    attnT = jnp.concatenate([attn_a, attn_b], 0)
     y_val = (
         input_rows.astype(jnp.float32)
         + lax.dot_general(attnT, w_out, (((0,), (0,)), ((), ())), preferred_element_type=jnp.float32)
     ).astype(jnp.bfloat16)
     y_plain = to_all(y_val)
-    local_wout = jnp.dot(attnT, gt, preferred_element_type=jnp.float32)
-    local_wqkv = lax.dot_general(
-        hidden_state, d_qkvT, (((0,), (1,)), ((), ())), preferred_element_type=jnp.float32
-    )
+    wq_b, wo_b = half_grads(hidden_state, dqkv_b, attn_b, gt)
+    d_qkvT = jnp.concatenate([dqkv_a, dqkv_b], 1).reshape(3 * width, rows)
     hidden_gradient = lax.dot_general(
         d_qkvT, w_qkv, (((0,), (1,)), ((), ())), preferred_element_type=jnp.float32
     )
@@ -148,23 +162,38 @@
         - normalized_input * jnp.mean(scaled_output * normalized_input, -1, keepdims=True)
     )
     d_x = (gt.astype(jnp.float32) + norm_gradient).astype(jnp.bfloat16)
-    total_w, total_gamma = sum_all(
-        (jnp.concatenate([local_wqkv, local_wout], 1), shard_gamma)
-    )
+    main_b = jnp.concatenate([wq_b.reshape(-1), wo_b.reshape(-1)]).reshape(size, -1, 128)
+    per = width // size
+    side = jnp.zeros((size, 1, 128), jnp.float32).at[:, 0, :per].set(shard_gamma.reshape(size, per))
+    pay_b = jnp.concatenate([main_b, side], 1)
+    mine_b = scatter_sum(pay_b)
     dx_plain = to_all(d_x)
+    total_b = gather_all(mine_b, size)
+    gamma_total = total_b[:, -1, :per].reshape(width)
+    flat_b = total_b[:, :-1, :].reshape(-1)
+
+    def unpack(flat):
+        wq = flat[: sizes_a[0]].reshape(width, 3, hw)
+        wo = flat[sizes_a[0] :].reshape(hw, width)
+        return wq, wo
+
+    wq_ta, wo_ta = unpack(total_a)
+    wq_tb, wo_tb = unpack(flat_b)
+    total_wqkv = jnp.concatenate([wq_ta, wq_tb], 2).reshape(width, 3 * width)
+    total_wout = jnp.concatenate([wo_ta, wo_tb], 0)
     return (
         y_plain,
         dx_plain,
-        total_w[:, : 3 * width] * inverse_root,
-        total_w[:, 3 * width :] * inverse_root,
-        total_gamma * inverse_root,
+        total_wqkv * inverse_root,
+        total_wout * inverse_root,
+        gamma_total * inverse_root,
     )
 
 
 def solution(mesh):
     placed = (P(("gx", "gy"), None), P(("gx", "gy")), P(("gx", "gy"), None), P(), P(), P())
     return jax.shard_map(
-        shards,
+        block,
         mesh=mesh,
         in_specs=placed,
         out_specs=(P(("gx", "gy"), None), P(("gx", "gy"), None), P(), P(), P()),

time: 216 us -> 249 us (1.15)
  waiting for transfers between devices: 56.2 us -> 79.5 us
  starting transfers between devices: 18.2 us -> 24 us
    all_to_all x2 -> x4, waiting for transfers between devices: 39.1 us -> 63.7 us  [the longest x2 33.1 us: gather_all(): lax.all_to_all(spread, ('gx', 'gy'), split_axis=0, concat_axis=0, tiled=T...]
    all_to_all x2 -> x4, starting transfers between devices: 10.2 us -> 16 us  [the longest x2 8.05 us: scatter_sum(): lax.all_to_all(payload, ('gx', 'gy'), split_axis=0, concat_axis=0, tiled=...]
    unnamed x14 -> x23, local copies, waits for them, and re-layouts: 1.61 us -> 4.28 us
    pallas_call x1 -> x2, Pallas kernels: 73.9 us -> 75.5 us  [fused_attention(): pl.pallas_call(kernel, grid=(count,), in_specs=[pl.BlockSpec((3, d, n), l...]
    dot_general x6 -> x8, matrix products: 11.4 us -> 13 us  [the longest x2 4.26 us: half_grads(): lax.dot_general(hidden_state, d_qkvT_half.reshape(-1, d_qkvT_half.shape[-...]
  transfers between devices with their start and end apart: 4 -> 6, of which waited for: 4 -> 6; matrix products, arithmetic and copies ran while one was open for 6% -> 6% of each run, Pallas kernels for 0% -> 0%
where the time goes in v3:
time: 249 us; the launch traced here: 248 us
  waiting for transfers between devices  79.5 us (32%)
  Pallas kernels  75.5 us (30%)
  blocking collectives  33.5 us (13%)
  starting transfers between devices  24 us (10%)
  matrix products  13 us (5%)
  local copies, waits for them, and re-layouts  10.7 us (4%)
  other arithmetic  10.6 us (4%)
    pallas_call x2, Pallas kernels, fused_attention(): pl.pallas_call(kernel, grid=(count,), in_specs=[pl.BlockSpec((3, d, n), l...  75.5 us
    all_to_all x1, blocking collectives, to_all(): lax.all_to_all(shaped, ('gx', 'gy'), split_axis=0, concat_axis=0, tiled=T...  33.5 us
    all_to_all x2, waiting for transfers between devices, gather_all(): lax.all_to_all(spread, ('gx', 'gy'), split_axis=0, concat_axis=0, tiled=T...  33.1 us
    all_to_all x2, waiting for transfers between devices, scatter_sum(): lax.all_to_all(payload, ('gx', 'gy'), split_axis=0, concat_axis=0, tiled=...  30.6 us
    all_to_all x2, waiting for transfers between devices, to_all(): lax.all_to_all(shaped, ('gx', 'gy'), split_axis=0, concat_axis=0, tiled=T...  15.9 us
    all_to_all x2, starting transfers between devices, to_all(): lax.all_to_all(shaped, ('gx', 'gy'), split_axis=0, concat_axis=0, tiled=T...  8.06 us
    all_to_all x2, starting transfers between devices, scatter_sum(): lax.all_to_all(payload, ('gx', 'gy'), split_axis=0, concat_axis=0, tiled=...  8.05 us
    all_to_all x2, starting transfers between devices, gather_all(): lax.all_to_all(spread, ('gx', 'gy'), split_axis=0, concat_axis=0, tiled=T...  7.94 us
  transfers between devices with their start and end apart: 6, of which 6 were waited for; matrix products, arithmetic and copies ran while one was open for 6% of the time, Pallas kernels for 0%

profile of v3, /device:TPU:1, one launch (start us, length us, event | category | flops | bytes accessed | tf_op | source)
XLA Modules:
  0.0 247.9 jit_solution(13652585334275863338)
XLA Ops:
  0.6 0.0 copy-start
  0.6 0.6 compare_reduce_fusion
  1.3 1.3 convert_select_fusion
  2.6 0.2 reshape.211
  2.8 1.3 fusion.2
  4.1 33.5 %all_to_all.35 = bf16[128,8,640]{2,1,0:T(8,128)(2,1)S(1)} all-to-all(bf16[128,8,640]{2,1,0:T(8,128)(2,1)S(1)} %fusion.2), channel_id=1, replica_groups=mesh['gx'=16,'gy'=8] {'gx','gy'}, dimensions={0} | all-to-all | bytes 2621440 | tf_op jit(solution)/shard_map/all_to_all | solution.py:94
  37.7 0.7 convert_reduce_fusion.1
  38.4 0.2 convert_reduce_fusion
  38.6 0.4 fusion.19
  39.0 0.0 copy-done.7
  39.0 1.1 fusion.10.do_ref
  40.2 0.0 copy-done
  40.2 2.1 convolution_convert_fusion
  42.2 37.8 %shard_map.102 = (bf16[128,1024]{1,0:T(8,128)(2,1)}, bf16[3,128,1024]{2,1,0:T(8,128)(2,1)}) custom-call(bf16[3,256,1024]{2,1,0:T(8,128)(2,1)} %bitcast.62, bf16[256,1024]{1,0:T(8,128)(2,1)} %fusion.10.do_ref, f32[1,1024]{1,0:T(1,128)} %bitcast.60), custom_call_target="tpu_custom_call" | custom-call | flops 1610612736 | bytes 2097152 | tf_op jit(solution)/shard_map/pallas_call | solution.py:68
  80.0 37.8 %shard_map.101 = (bf16[128,1024]{1,0:T(8,128)(2,1)}, bf16[3,128,1024]{2,1,0:T(8,128)(2,1)}) custom-call(bf16[3,256,1024]{2,1,0:T(8,128)(2,1)} %bitcast.63, bf16[256,1024]{1,0:T(8,128)(2,1)} %fusion.10.do_ref, f32[1,1024]{1,0:T(1,128)} %bitcast.61), custom_call_target="tpu_custom_call" | custom-call | flops 1610612736 | bytes 2097152 | tf_op jit(solution)/shard_map/pallas_call | solution.py:68
  117.7 1.2 convolution_bitcast_fusion.1
  118.9 0.0 copy-done.5
  118.9 0.0 copy-start.3
  119.0 2.2 fusion.11
  121.1 0.1 copy.45
  121.2 4.0 %all-to-all-start.1 = ((bf16[128,8,256]{2,1,0:T(8,128)(2,1)}), bf16[128,8,256]{2,1,0:T(8,128)(2,1)S(1)}, u32[]{:S(2)}, u32[]{:S(2)}) async-start(bf16[128,8,256]{2,1,0:T(8,128)(2,1)} %fusion.11), calls=%async_computation.1 | async-start | bytes 1048576 | tf_op jit(solution)/shard_map/all_to_all | solution.py:94
  125.3 1.6 fusion.31
  126.8 1.0 reshape.198
  127.8 0.0 copy-start.2
  127.9 0.8 maximum_bitcast_fusion
  128.7 0.5 copy-done.2
  129.2 1.3 pad_maximum_fusion
  130.4 0.0 copy-start.6
  130.4 2.0 fusion.18
  132.4 6.8 %all-to-all-done.1 = bf16[128,8,256]{2,1,0:T(8,128)(2,1)S(1)} async-done(((bf16[128,8,256]{2,1,0:T(8,128)(2,1)}), bf16[128,8,256]{2,1,0:T(8,128)(2,1)S(1)}, u32[]{:S(2)}, u32[]{:S(2)}) %all-to-all-start.1) | async-done | bytes 524320 | tf_op jit(solution)/shard_map/all_to_all | solution.py:94
  139.3 4.0 %all-to-all-start.3 = ((f32[128,8,128]{2,1,0:T(8,128)}), f32[128,8,128]{2,1,0:T(8,128)S(1)}, u32[]{:S(2)}, u32[]{:S(2)}) async-start(f32[128,8,128]{2,1,0:T(8,128)} %maximum_bitcast_fusion), calls=%async_computation.3 | async-start | bytes 1048576 | tf_op jit(solution)/shard_map/all_to_all | solution.py:99
  143.3 0.2 convolution_bitcast_fusion
  143.6 0.1 copy.46
  143.6 0.9 copy-done.1
  144.5 1.5 fusion.20
  146.1 11.2 %all-to-all-done.3 = f32[128,8,128]{2,1,0:T(8,128)S(1)} async-done(((f32[128,8,128]{2,1,0:T(8,128)}), f32[128,8,128]{2,1,0:T(8,128)S(1)}, u32[]{:S(2)}, u32[]{:S(2)}) %all-to-all-start.3) | async-done | bytes 524320 | tf_op jit(solution)/shard_map/all_to_all | solution.py:99
  157.3 4.0 %all-to-all-start.2 = ((bf16[128,8,256]{2,1,0:T(8,128)(2,1)}), bf16[128,8,256]{2,1,0:T(8,128)(2,1)S(1)}, u32[]{:S(2)}, u32[]{:S(2)}) async-start(bf16[128,8,256]{2,1,0:T(8,128)(2,1)} %fusion.20), calls=%async_computation.2 | async-start | bytes 1048576 | tf_op jit(solution)/shard_map/all_to_all | solution.py:94
  161.3 2.7 %fusion.29 = f32[256,384]{1,0:T(8,128)} fusion(bf16[384,1024]{1,0:T(8,128)(2,1)} %bitcast.55, f32[256]{0:T(256)S(1)} %copy-done.8, f32[1024]{0:T(1024)S(1)} %add_rsqrt_fusion, f32[1024]{0:T(1024)S(1)} %broadcast_multiply_fusion.2, bf16[1024,640]{1,0:T(8,128)(2,1)S(1)} %bitcast.50), kind=kOutput, calls=%fused_computation.53 | convolution fusion | flops 202637312 | bytes 1713152 | tf_op jit(solution)/shard_map/dot_general | solution.py:109
  164.0 1.0 reshape.203
  165.1 0.1 reshape.206
  165.2 1.1 select_maximum_fusion
  166.3 9.0 %all-to-all-done.2 = bf16[128,8,256]{2,1,0:T(8,128)(2,1)S(1)} async-done(((bf16[128,8,256]{2,1,0:T(8,128)(2,1)}), bf16[128,8,256]{2,1,0:T(8,128)(2,1)S(1)}, u32[]{:S(2)}, u32[]{:S(2)}) %all-to-all-start.2) | async-done | bytes 524320 | tf_op jit(solution)/shard_map/all_to_all | solution.py:94
  175.3 4.0 %all-to-all-start.5 = ((f32[128,9,128]{2,1,0:T(8,128)}), f32[128,9,128]{2,1,0:T(8,128)S(1)}, u32[]{:S(2)}, u32[]{:S(2)}) async-start(f32[128,9,128]{2,1,0:T(8,128)} %select_maximum_fusion), calls=%async_computation.5 | async-start | bytes 2097152 | tf_op jit(solution)/shard_map/all_to_all | solution.py:99
  179.4 0.1 reduce_sum.67
  179.5 19.3 %all-to-all-done.5 = f32[128,9,128]{2,1,0:T(8,128)S(1)} async-done(((f32[128,9,128]{2,1,0:T(8,128)}), f32[128,9,128]{2,1,0:T(8,128)S(1)}, u32[]{:S(2)}, u32[]{:S(2)}) %all-to-all-start.5) | async-done | bytes 589856 | tf_op jit(solution)/shard_map/all_to_all | solution.py:99
  198.8 0.8 broadcast_in_dim.4
  199.7 3.9 %all-to-all-start.4 = ((f32[128,8,128]{2,1,0:T(8,128)}), f32[128,8,128]{2,1,0:T(8,128)S(1)}, u32[]{:S(2)}, u32[]{:S(2)}) async-start(f32[128,8,128]{2,1,0:T(8,128)} %broadcast_in_dim.4), calls=%async_computation.4 | async-start | bytes 1048576 | tf_op jit(solution)/shard_map/all_to_all | solution.py:105
  203.6 0.1 reduce_sum.69
  203.7 13.9 %all-to-all-done.4 = f32[128,8,128]{2,1,0:T(8,128)S(1)} async-done(((f32[128,8,128]{2,1,0:T(8,128)}), f32[128,8,128]{2,1,0:T(8,128)S(1)}, u32[]{:S(2)}, u32[]{:S(2)}) %all-to-all-start.4) | async-done | bytes 524320 | tf_op jit(solution)/shard_map/all_to_all | solution.py:105
  217.7 1.1 broadcast_in_dim.5
  218.7 4.0 %all-to-all-start.6 = ((f32[128,9,128]{2,1,0:T(8,128)}), f32[128,9,128]{2,1,0:T(8,128)S(1)}, u32[]{:S(2)}, u32[]{:S(2)}) async-start(f32[128,9,128]{2,1,0:T(8,128)} %broadcast_in_dim.5), calls=%async_computation.6 | async-start | bytes 2097152 | tf_op jit(solution)/shard_map/all_to_all | solution.py:105
  222.9 0.2 reshape.201
  223.1 19.2 %all-to-all-done.6 = f32[128,9,128]{2,1,0:T(8,128)S(1)} async-done(((f32[128,9,128]{2,1,0:T(8,128)}), f32[128,9,128]{2,1,0:T(8,128)S(1)}, u32[]{:S(2)}, u32[]{:S(2)}) %all-to-all-start.6) | async-done | bytes 589856 | tf_op jit(solution)/shard_map/all_to_all | solution.py:105
  242.2 0.2 fusion.27
  242.4 0.7 mul.87
  243.2 0.7 reshape.209
  243.9 0.2 reshape.207
  244.1 0.1 maximum_multiply_fusion
  244.2 0.0 copy-start.4
  244.2 0.3 copy.40
  244.5 1.1 copy.41
  245.6 0.7 maximum_multiply_fusion.1
  246.3 0.8 copy.49
  247.1 0.8 copy.50
  (19 shorter events, 0.2 us)
Async XLA Ops:
  0.6 39.5 %copy-start = (bf16[256,768]{1,0:T(8,128)(2,1)S(1)}, bf16[256,768]{1,0:T(8,128)(2,1)}, u32[]{:S(2)}) copy-start(bf16[256,768]{1,0:T(8,128)(2,1)} %param.14) | copy-start | bytes 1179652
  37.7 1.3 copy-start.7
  37.7 2.5 %copy-start.8 = (f32[256]{0:T(256)S(1)}, f32[256]{0:T(256)}, u32[]{:S(2)}) copy-start(f32[256]{0:T(256)} %param.13) | copy-start | bytes 3076
  80.0 39.0 %copy-start.5 = (bf16[128,1024]{1,0:T(8,128)(2,1)S(1)}, bf16[128,1024]{1,0:T(8,128)(2,1)}, u32[]{:S(2)}) copy-start(bf16[128,1024]{1,0:T(8,128)(2,1)} %get-tuple-element.34) | copy-start | bytes 786436
  118.9 6.3 %copy-start.3 = (bf16[3,128,1024]{2,1,0:T(8,128)(2,1)S(1)}, bf16[3,128,1024]{2,1,0:T(8,128)(2,1)}, u32[]{:S(2)}) copy-start(bf16[3,128,1024]{2,1,0:T(8,128)(2,1)} %get-tuple-element.35) | copy-start | bytes 2359300
  121.2 18.1 %all-to-all-start.1 = ((bf16[128,8,256]{2,1,0:T(8,128)(2,1)}), bf16[128,8,256]{2,1,0:T(8,128)(2,1)S(1)}, u32[]{:S(2)}, u32[]{:S(2)}) async-start(bf16[128,8,256]{2,1,0:T(8,128)(2,1)} %fusion.11), calls=%async_computation.1 | async-start | bytes 1048576 | tf_op jit(solution)/shard_map/all_to_all | solution.py:94
  127.8 1.3 copy-start.2
  130.4 12.9 %copy-start.6 = (bf16[128,1024]{1,0:T(8,128)(2,1)S(1)}, bf16[128,1024]{1,0:T(8,128)(2,1)}, u32[]{:S(2)}) copy-start(bf16[128,1024]{1,0:T(8,128)(2,1)} %get-tuple-element.34) | copy-start | bytes 786436
  139.3 18.0 %all-to-all-start.3 = ((f32[128,8,128]{2,1,0:T(8,128)}), f32[128,8,128]{2,1,0:T(8,128)S(1)}, u32[]{:S(2)}, u32[]{:S(2)}) async-start(f32[128,8,128]{2,1,0:T(8,128)} %maximum_bitcast_fusion), calls=%async_computation.3 | async-start | bytes 1048576 | tf_op jit(solution)/shard_map/all_to_all | solution.py:99
  143.3 1.2 copy-start.1
  157.3 18.0 %all-to-all-start.2 = ((bf16[128,8,256]{2,1,0:T(8,128)(2,1)}), bf16[128,8,256]{2,1,0:T(8,128)(2,1)S(1)}, u32[]{:S(2)}, u32[]{:S(2)}) async-start(bf16[128,8,256]{2,1,0:T(8,128)(2,1)} %fusion.20), calls=%async_computation.2 | async-start | bytes 1048576 | tf_op jit(solution)/shard_map/all_to_all | solution.py:94
  175.3 23.5 %all-to-all-start.5 = ((f32[128,9,128]{2,1,0:T(8,128)}), f32[128,9,128]{2,1,0:T(8,128)S(1)}, u32[]{:S(2)}, u32[]{:S(2)}) async-start(f32[128,9,128]{2,1,0:T(8,128)} %select_maximum_fusion), calls=%async_computation.5 | async-start | bytes 2097152 | tf_op jit(solution)/shard_map/all_to_all | solution.py:99
  199.7 18.0 %all-to-all-start.4 = ((f32[128,8,128]{2,1,0:T(8,128)}), f32[128,8,128]{2,1,0:T(8,128)S(1)}, u32[]{:S(2)}, u32[]{:S(2)}) async-start(f32[128,8,128]{2,1,0:T(8,128)} %broadcast_in_dim.4), calls=%async_computation.4 | async-start | bytes 1048576 | tf_op jit(solution)/shard_map/all_to_all | solution.py:105
  218.7 23.5 %all-to-all-start.6 = ((f32[128,9,128]{2,1,0:T(8,128)}), f32[128,9,128]{2,1,0:T(8,128)S(1)}, u32[]{:S(2)}, u32[]{:S(2)}) async-start(f32[128,9,128]{2,1,0:T(8,128)} %broadcast_in_dim.5), calls=%async_computation.6 | async-start | bytes 2097152 | tf_op jit(solution)/shard_map/all_to_all | solution.py:105
  244.2 1.4 copy-start.4

commit v4 on v3

--- a/solution.py
+++ b/solution.py
@@ -146,9 +146,10 @@
     attnT = jnp.concatenate([attn_a, attn_b], 0)
     y_val = (
         input_rows.astype(jnp.float32)
-        + lax.dot_general(attnT, w_out, (((0,), (0,)), ((), ())), preferred_element_type=jnp.float32)
+        + lax.dot_general(
+            attnT, w_out, (((0,), (0,)), ((), ())), preferred_element_type=jnp.float32
+        )
     ).astype(jnp.bfloat16)
-    y_plain = to_all(y_val)
     wq_b, wo_b = half_grads(hidden_state, dqkv_b, attn_b, gt)
     d_qkvT = jnp.concatenate([dqkv_a, dqkv_b], 1).reshape(3 * width, rows)
     hidden_gradient = lax.dot_general(
@@ -166,8 +167,19 @@
     per = width // size
     side = jnp.zeros((size, 1, 128), jnp.float32).at[:, 0, :per].set(shard_gamma.reshape(size, per))
     pay_b = jnp.concatenate([main_b, side], 1)
-    mine_b = scatter_sum(pay_b)
-    dx_plain = to_all(d_x)
+    lead = pay_b.astype(jnp.bfloat16)
+    rest = (pay_b - lead.astype(jnp.float32)).astype(jnp.bfloat16)
+    nb = pay_b.shape[1]
+    coded = jnp.concatenate([lead, rest], 1).reshape(size, nb, 2 * 128)
+    per_dev = rows // size
+    payload = jnp.concatenate(
+        [d_x.reshape(size, per_dev, width), y_val.reshape(size, per_dev, width), coded], 1
+    )
+    moved_b = lax.all_to_all(payload, ("gx", "gy"), split_axis=0, concat_axis=0, tiled=True)
+    dx_plain = moved_b[:, :per_dev].reshape(rows, width)
+    y_plain = moved_b[:, per_dev : 2 * per_dev].reshape(rows, width)
+    got = moved_b[:, 2 * per_dev :].reshape(size, 2 * nb, 128).astype(jnp.float32)
+    mine_b = jnp.sum(got[:, :nb] + got[:, nb:], 0, keepdims=True)
     total_b = gather_all(mine_b, size)
     gamma_total = total_b[:, -1, :per].reshape(width)
     flat_b = total_b[:, :-1, :].reshape(-1)

time: 249 us -> 236 us (0.948)
  waiting for transfers between devices: 79.5 us -> 49.9 us
  local copies, waits for them, and re-layouts: 10.7 us -> 25.3 us
  other arithmetic: 10.6 us -> 14.4 us
    all_to_all x2 -> x1, waiting for transfers between devices: 30.6 us -> 0.01 us  [scatter_sum(): lax.all_to_all(payload, ('gx', 'gy'), split_axis=0, concat_axis=0, tiled=...]
    all_to_all x2 -> x1, waiting for transfers between devices: 15.9 us -> 29.4 us  [block(): lax.all_to_all(payload, ('gx', 'gy'), split_axis=0, concat_axis=0, tiled=...]
    all_to_all x2, waiting for transfers between devices: 33.1 us -> 20.5 us  [gather_all(): lax.all_to_all(spread, ('gx', 'gy'), split_axis=0, concat_axis=0, tiled=T...]
    concatenate x0 -> x2, local copies, waits for them, and re-layouts: none -> 3.77 us  [the longest x1 3.31 us: block(): jnp.concatenate([d_x.reshape(size, per_dev, width), y_val.reshape(size, p...]
    reshape x0 -> x3, local copies, waits for them, and re-layouts: none -> 3.7 us  [the longest x1 1.47 us: block(): y_val.reshape(size, per_dev, width)]
    reshape x4, local copies, waits for them, and re-layouts: 0.39 us -> 3.96 us  [unpack(): wq = flat[:sizes_a[0]].reshape(width, 3, hw)]
    all_to_all x2 -> x1, starting transfers between devices: 8.05 us -> 5.1 us  [scatter_sum(): lax.all_to_all(payload, ('gx', 'gy'), split_axis=0, concat_axis=0, tiled=...]
    all_to_all x2 -> x1, starting transfers between devices: 8.06 us -> 9.9 us  [block(): lax.all_to_all(payload, ('gx', 'gy'), split_axis=0, concat_axis=0, tiled=...]
  transfers between devices with their start and end apart: 6 -> 4, of which waited for: 6 -> 3; matrix products, arithmetic and copies ran while one was open for 6% -> 13% of each run, Pallas kernels for 0% -> 0%
where the time goes in v4:
time: 236 us; the launch traced here: 235 us
  Pallas kernels  75.5 us (32%)
  waiting for transfers between devices  49.9 us (21%)
  blocking collectives  33.5 us (14%)
  local copies, waits for them, and re-layouts  25.3 us (11%)
  starting transfers between devices  24.2 us (10%)
  other arithmetic  14.4 us (6%)
  matrix products  11.5 us (5%)
    pallas_call x2, Pallas kernels, fused_attention(): pl.pallas_call(kernel, grid=(count,), in_specs=[pl.BlockSpec((3, d, n), l...  75.5 us
    all_to_all x1, blocking collectives, to_all(): lax.all_to_all(shaped, ('gx', 'gy'), split_axis=0, concat_axis=0, tiled=T...  33.5 us
    all_to_all x1, waiting for transfers between devices, block(): lax.all_to_all(payload, ('gx', 'gy'), split_axis=0, concat_axis=0, tiled=...  29.4 us
    all_to_all x2, waiting for transfers between devices, gather_all(): lax.all_to_all(spread, ('gx', 'gy'), split_axis=0, concat_axis=0, tiled=T...  20.5 us
    all_to_all x1, starting transfers between devices, block(): lax.all_to_all(payload, ('gx', 'gy'), split_axis=0, concat_axis=0, tiled=...  9.9 us
    all_to_all x2, starting transfers between devices, gather_all(): lax.all_to_all(spread, ('gx', 'gy'), split_axis=0, concat_axis=0, tiled=T...  9.19 us
    all_to_all x1, starting transfers between devices, scatter_sum(): lax.all_to_all(payload, ('gx', 'gy'), split_axis=0, concat_axis=0, tiled=...  5.1 us
  transfers between devices with their start and end apart: 4, of which 3 were waited for; matrix products, arithmetic and copies ran while one was open for 13% of the time, Pallas kernels for 0%

profile of v4, /device:TPU:1, one launch (start us, length us, event | category | flops | bytes accessed | tf_op | source)
XLA Modules:
  0.0 235.3 jit_solution(5984706825714399575)
XLA Ops:
  0.6 0.0 copy-start
  0.6 0.6 compare_reduce_fusion
  1.3 1.3 convert_select_fusion
  2.6 0.2 reshape.219
  2.8 1.3 fusion.2
  4.2 33.5 %all_to_all.25 = bf16[128,8,640]{2,1,0:T(8,128)(2,1)S(1)} all-to-all(bf16[128,8,640]{2,1,0:T(8,128)(2,1)S(1)} %fusion.2), channel_id=1, replica_groups=mesh['gx'=16,'gy'=8] {'gx','gy'}, dimensions={0} | all-to-all | bytes 2621440 | tf_op jit(solution)/shard_map/all_to_all | solution.py:94
  37.7 0.7 convert_reduce_fusion.1
  38.4 0.2 convert_reduce_fusion
  38.6 0.4 fusion.19
  39.0 1.1 fusion.10.do_ref
  40.2 2.1 convolution_convert_fusion
  42.2 37.8 %shard_map.102 = (bf16[128,1024]{1,0:T(8,128)(2,1)}, bf16[3,128,1024]{2,1,0:T(8,128)(2,1)}) custom-call(bf16[3,256,1024]{2,1,0:T(8,128)(2,1)} %bitcast.68, bf16[256,1024]{1,0:T(8,128)(2,1)} %fusion.10.do_ref, f32[1,1024]{1,0:T(1,128)} %bitcast.66), custom_call_target="tpu_custom_call" | custom-call | flops 1610612736 | bytes 2097152 | tf_op jit(solution)/shard_map/pallas_call | solution.py:68
  80.0 37.8 %shard_map.101 = (bf16[128,1024]{1,0:T(8,128)(2,1)}, bf16[3,128,1024]{2,1,0:T(8,128)(2,1)}) custom-call(bf16[3,256,1024]{2,1,0:T(8,128)(2,1)} %bitcast.69, bf16[256,1024]{1,0:T(8,128)(2,1)} %fusion.10.do_ref, f32[1,1024]{1,0:T(1,128)} %bitcast.67), custom_call_target="tpu_custom_call" | custom-call | flops 1610612736 | bytes 2097152 | tf_op jit(solution)/shard_map/pallas_call | solution.py:68
  117.8 0.2 convolution_bitcast_fusion.1
  118.0 1.2 convolution_bitcast_fusion
  119.2 1.2 fusion.11
  120.4 0.1 copy.68
  120.4 1.5 copy.58
  121.9 0.1 copy.69
  122.0 1.6 fusion.31
  123.6 1.0 reshape.210
  124.6 0.8 maximum_bitcast_fusion.1
  125.4 5.1 %all-to-all-start.2 = ((f32[128,8,128]{2,1,0:T(8,128)}), f32[128,8,128]{2,1,0:T(8,128)}, u32[]{:S(2)}, u32[]{:S(2)}) async-start(f32[128,8,128]{2,1,0:T(8,128)} %maximum_bitcast_fusion.1), calls=%async_computation.2 | async-start | bytes 1048576 | tf_op jit(solution)/shard_map/all_to_all | solution.py:99
  130.5 2.7 %pad_maximum_fusion.1 = bf16[3,256,1024]{2,1,0:T(8,128)(2,1)} fusion(bf16[3,128,1024]{2,1,0:T(8,128)(2,1)} %get-tuple-element.34, bf16[3,128,1024]{2,1,0:T(8,128)(2,1)} %get-tuple-element.33), kind=kLoop, calls=%fused_computation.4 | loop fusion | flops 3145728 | bytes 3145728 | tf_op jit(solution)/shard_map/concatenate | solution.py:154
  133.3 1.6 fusion.33
  134.8 1.0 reshape.202
  135.9 2.6 %fusion.13 = (f32[1024]{0:T(1024)S(1)}, f32[256]{0:T(256)S(1)}, f32[1024]{0:T(1024)S(1)}, f32[1024,256]{1,0:T(8,128)S(1)}) fusion(f32[256]{0:T(256)S(1)} %copy-done.9, f32[1024]{0:T(1024)S(1)} %add_rsqrt_fusion, f32[1024]{0:T(1024)S(1)} %broadcast_multiply_fusion.2, bf16[1024,640]{1,0:T(8,128)(2,1)S(1)} %bitcast.54, bf16[768,1024]{1,0:T(8,128)(2,1)} %bitcast.59, ...), kind=kOutput, calls=%fused_computation.23 | convolution fusion | flops 405010176 | bytes 3557376 | tf_op jit(solution)/shard_map/dot_general | solution.py:155
  138.5 0.9 fusion.22
  139.4 1.2 copy.57
  140.6 0.1 reshape.205
  140.8 0.1 subtract_convert_fusion
  140.9 0.1 fusion.20
  141.0 0.3 pad_maximum_fusion.2
  141.3 0.5 copy.56
  141.8 1.2 pad_maximum_fusion
  143.0 3.3 %copy.59 = bf16[128,25,256]{2,1,0:T(8,128)(2,1)} copy(bf16[128,25,256]{0,2,1:T(8,128)(2,1)S(1)} %pad_maximum_fusion) | data formatting | bytes 3276800 | tf_op jit(solution)/shard_map/concatenate | solution.py:175
  146.3 9.9 %all-to-all-start.1 = ((bf16[128,25,256]{2,1,0:T(8,128)(2,1)}), bf16[128,25,256]{2,1,0:T(8,128)(2,1)S(1)}, u32[]{:S(2)}, u32[]{:S(2)}) async-start(bf16[128,25,256]{2,1,0:T(8,128)(2,1)} %copy.59), calls=%async_computation.1 | async-start | bytes 4194304 | tf_op jit(solution)/shard_map/all_to_all | solution.py:178
  156.2 1.2 reduce_sum.68
  157.4 29.4 %all-to-all-done.1 = bf16[128,25,256]{2,1,0:T(8,128)(2,1)S(1)} async-done(((bf16[128,25,256]{2,1,0:T(8,128)(2,1)}), bf16[128,25,256]{2,1,0:T(8,128)(2,1)S(1)}, u32[]{:S(2)}, u32[]{:S(2)}) %all-to-all-start.1) | async-done | bytes 1638432 | tf_op jit(solution)/shard_map/all_to_all | solution.py:178
  186.8 0.8 broadcast_in_dim.4
  187.6 5.2 %all-to-all-start.3 = ((f32[128,8,128]{2,1,0:T(8,128)}), f32[128,8,128]{2,1,0:T(8,128)}, u32[]{:S(2)}, u32[]{:S(2)}) async-start(f32[128,8,128]{2,1,0:T(8,128)} %broadcast_in_dim.4), calls=%async_computation.3 | async-start | bytes 1048576 | tf_op jit(solution)/shard_map/all_to_all | solution.py:105
  192.8 0.1 slice.102
  192.9 1.5 copy.66
  194.4 1.2 convert.2
  195.6 0.2 fusion.21
  195.8 10.7 %all-to-all-done.3 = f32[128,8,128]{2,1,0:T(8,128)} async-done(((f32[128,8,128]{2,1,0:T(8,128)}), f32[128,8,128]{2,1,0:T(8,128)}, u32[]{:S(2)}, u32[]{:S(2)}) %all-to-all-start.3) | async-done | bytes 524320 | tf_op jit(solution)/shard_map/all_to_all | solution.py:105
  206.5 1.1 broadcast_in_dim.5
  207.6 4.0 %all-to-all-start.4 = ((f32[128,9,128]{2,1,0:T(8,128)}), f32[128,9,128]{2,1,0:T(8,128)S(1)}, u32[]{:S(2)}, u32[]{:S(2)}) async-start(f32[128,9,128]{2,1,0:T(8,128)} %broadcast_in_dim.5), calls=%async_computation.4 | async-start | bytes 2097152 | tf_op jit(solution)/shard_map/all_to_all | solution.py:105
  211.6 1.6 slice.106
  213.2 1.6 reshape.215
  214.8 1.8 slice.101
  216.6 2.0 reshape.213
  218.5 1.8 copy.61
  220.3 1.0 slice_bitcast_fusion
  221.4 9.8 %all-to-all-done.4 = f32[128,9,128]{2,1,0:T(8,128)S(1)} async-done(((f32[128,9,128]{2,1,0:T(8,128)}), f32[128,9,128]{2,1,0:T(8,128)S(1)}, u32[]{:S(2)}, u32[]{:S(2)}) %all-to-all-start.4) | async-done | bytes 589856 | tf_op jit(solution)/shard_map/all_to_all | solution.py:105
  231.1 0.2 fusion.29
  231.3 0.7 mul.87
  232.0 0.7 reshape.216
  232.8 0.2 reshape.214
  233.0 0.1 copy-done.1
  233.1 0.1 maximum_multiply_fusion
  233.2 0.3 copy.63
  233.4 1.1 copy.64
  234.6 0.7 maximum_multiply_fusion.1
  (26 shorter events, 0.2 us)
Async XLA Ops:
  0.6 39.5 %copy-start = (bf16[256,768]{1,0:T(8,128)(2,1)S(1)}, bf16[256,768]{1,0:T(8,128)(2,1)}, u32[]{:S(2)}) copy-start(bf16[256,768]{1,0:T(8,128)(2,1)} %param.14) | copy-start | bytes 1179652
  4.1 34.9 %copy-start.8 = (bf16[256,256]{1,0:T(8,128)(2,1)S(1)}, bf16[256,256]{1,0:T(8,128)(2,1)}, u32[]{:S(2)}) copy-start(bf16[256,256]{1,0:T(8,128)(2,1)} %param.15) | copy-start | bytes 393220
  37.7 2.5 %copy-start.9 = (f32[256]{0:T(256)S(1)}, f32[256]{0:T(256)}, u32[]{:S(2)}) copy-start(f32[256]{0:T(256)} %param.13) | copy-start | bytes 3076
  80.0 37.8 %copy-start.6 = (bf16[128,1024]{1,0:T(8,128)(2,1)S(1)}, bf16[128,1024]{1,0:T(8,128)(2,1)}, u32[]{:S(2)}) copy-start(bf16[128,1024]{1,0:T(8,128)(2,1)} %get-tuple-element.36) | copy-start | bytes 786436
  117.8 1.4 copy-start.7
  119.2 2.8 %copy-start.3 = (bf16[3,128,1024]{2,1,0:T(8,128)(2,1)S(1)}, bf16[3,128,1024]{2,1,0:T(8,128)(2,1)}, u32[]{:S(2)}) copy-start(bf16[3,128,1024]{2,1,0:T(8,128)(2,1)} %get-tuple-element.33) | copy-start | bytes 2359300
  125.4 20.9 %all-to-all-start.2 = ((f32[128,8,128]{2,1,0:T(8,128)}), f32[128,8,128]{2,1,0:T(8,128)}, u32[]{:S(2)}, u32[]{:S(2)}) async-start(f32[128,8,128]{2,1,0:T(8,128)} %maximum_bitcast_fusion.1), calls=%async_computation.2 | async-start | bytes 1048576 | tf_op jit(solution)/shard_map/all_to_all | solution.py:99
  130.5 2.7 %copy-start.2 = (bf16[3,128,1024]{2,1,0:T(8,128)(2,1)S(1)}, bf16[3,128,1024]{2,1,0:T(8,128)(2,1)}, u32[]{:S(2)}) copy-start(bf16[3,128,1024]{2,1,0:T(8,128)(2,1)} %get-tuple-element.34) | copy-start | bytes 2359300
  146.3 40.5 %all-to-all-start.1 = ((bf16[128,25,256]{2,1,0:T(8,128)(2,1)}), bf16[128,25,256]{2,1,0:T(8,128)(2,1)S(1)}, u32[]{:S(2)}, u32[]{:S(2)}) async-start(bf16[128,25,256]{2,1,0:T(8,128)(2,1)} %copy.59), calls=%async_computation.1 | async-start | bytes 4194304 | tf_op jit(solution)/shard_map/all_to_all | solution.py:178
  187.6 19.0 %all-to-all-start.3 = ((f32[128,8,128]{2,1,0:T(8,128)}), f32[128,8,128]{2,1,0:T(8,128)}, u32[]{:S(2)}, u32[]{:S(2)}) async-start(f32[128,8,128]{2,1,0:T(8,128)} %broadcast_in_dim.4), calls=%async_computation.3 | async-start | bytes 1048576 | tf_op jit(solution)/shard_map/all_to_all | solution.py:105
  207.6 23.5 %all-to-all-start.4 = ((f32[128,9,128]{2,1,0:T(8,128)}), f32[128,9,128]{2,1,0:T(8,128)S(1)}, u32[]{:S(2)}, u32[]{:S(2)}) async-start(f32[128,9,128]{2,1,0:T(8,128)} %broadcast_in_dim.5), calls=%async_computation.4 | async-start | bytes 2097152 | tf_op jit(solution)/shard_map/all_to_all | solution.py:105
  232.0 1.0 copy-start.1
  233.1 1.4 copy-start.4
  233.1 1.4 copy-start.5

commit v5 on v2

--- a/solution.py
+++ b/solution.py
@@ -102,10 +102,14 @@
     per = rows // size
     side = jnp.zeros((size, per, 128), jnp.float32).at[:, :, 0].set(vector.reshape(size, per))
     payload = jnp.concatenate([matrix.reshape(size, per, cols), side], 2)
-    moved = lax.all_to_all(payload, ("gx", "gy"), split_axis=0, concat_axis=0, tiled=True)
-    mine = jnp.sum(moved, 0, keepdims=True)
-    spread = jnp.broadcast_to(mine, payload.shape)
-    total = lax.all_to_all(spread, ("gx", "gy"), split_axis=0, concat_axis=0, tiled=True)
+    moved = lax.all_to_all(
+        payload.astype(jnp.bfloat16), ("gx", "gy"), split_axis=0, concat_axis=0, tiled=True
+    )
+    mine = jnp.sum(moved.astype(jnp.float32), 0, keepdims=True)
+    spread = jnp.broadcast_to(mine.astype(jnp.bfloat16), payload.shape)
+    total = lax.all_to_all(
+        spread, ("gx", "gy"), split_axis=0, concat_axis=0, tiled=True
+    ).astype(jnp.float32)
     return total[:, :, :cols].reshape(rows, cols), total[:, :, cols].reshape(rows)
 
 

time: 216 us -> 200 us (0.926)
  waiting for transfers between devices: 56.2 us -> 46.6 us
  local copies, waits for them, and re-layouts: 8.94 us -> 5.17 us
    all_to_all x1, waiting for transfers between devices: 20.9 us -> 14.7 us  [sum_all(): lax.all_to_all(spread, ('gx', 'gy'), split_axis=0, concat_axis=0, tiled=T...]
    all_to_all x1, waiting for transfers between devices: 18.2 us -> 12.1 us  [sum_all(): lax.all_to_all(payload.astype(jnp.bfloat16), ('gx', 'gy'), split_axis=0,...]
    all_to_all x2, waiting for transfers between devices: 17.1 us -> 19.9 us  [to_all(): lax.all_to_all(shaped, ('gx', 'gy'), split_axis=0, concat_axis=0, tiled=T...]
    all_to_all x1, starting transfers between devices: 6.22 us -> 4.02 us  [sum_all(): lax.all_to_all(payload.astype(jnp.bfloat16), ('gx', 'gy'), split_axis=0,...]
  transfers between devices with their start and end apart: 4 -> 4, of which waited for: 4 -> 4; matrix products, arithmetic and copies ran while one was open for 6% -> 5% of each run, Pallas kernels for 0% -> 0%
where the time goes in v5:
time: 200 us; the launch traced here: 199 us
  Pallas kernels  73.9 us (37%)
  waiting for transfers between devices  46.6 us (23%)
  blocking collectives  33.5 us (17%)
  starting transfers between devices  16.1 us (8%)
  other arithmetic  11.5 us (6%)
  matrix products  11.4 us (6%)
  local copies, waits for them, and re-layouts  5.17 us (3%)
    pallas_call x1, Pallas kernels, fused_attention(): pl.pallas_call(kernel, grid=(heads,), in_specs=[pl.BlockSpec((3, d, n), l...  73.9 us
    all_to_all x1, blocking collectives, to_all(): lax.all_to_all(shaped, ('gx', 'gy'), split_axis=0, concat_axis=0, tiled=T...  33.5 us
    all_to_all x2, waiting for transfers between devices, to_all(): lax.all_to_all(shaped, ('gx', 'gy'), split_axis=0, concat_axis=0, tiled=T...  19.9 us
    all_to_all x1, waiting for transfers between devices, sum_all(): lax.all_to_all(spread, ('gx', 'gy'), split_axis=0, concat_axis=0, tiled=T...  14.7 us
    all_to_all x1, waiting for transfers between devices, sum_all(): lax.all_to_all(payload.astype(jnp.bfloat16), ('gx', 'gy'), split_axis=0,...  12.1 us
    all_to_all x2, starting transfers between devices, to_all(): lax.all_to_all(shaped, ('gx', 'gy'), split_axis=0, concat_axis=0, tiled=T...  8.01 us
    all_to_all x1, starting transfers between devices, sum_all(): lax.all_to_all(payload.astype(jnp.bfloat16), ('gx', 'gy'), split_axis=0,...  4.02 us
    all_to_all x1, starting transfers between devices, sum_all(): lax.all_to_all(spread, ('gx', 'gy'), split_axis=0, concat_axis=0, tiled=T...  4.02 us
  transfers between devices with their start and end apart: 4, of which 4 were waited for; matrix products, arithmetic and copies ran while one was open for 5% of the time, Pallas kernels for 0%

profile of v5, /device:TPU:1, one launch (start us, length us, event | category | flops | bytes accessed | tf_op | source)
XLA Modules:
  0.0 199.1 jit_solution(10105105446185909809)
XLA Ops:
  0.6 0.0 copy-start
  0.6 0.6 compare_reduce_fusion
  1.3 1.3 convert_select_fusion
  2.6 0.2 reshape.158
  2.8 1.3 fusion.2
  4.1 33.5 %all_to_all.25 = bf16[128,8,640]{2,1,0:T(8,128)(2,1)S(1)} all-to-all(bf16[128,8,640]{2,1,0:T(8,128)(2,1)S(1)} %fusion.2), channel_id=1, replica_groups=mesh['gx'=16,'gy'=8] {'gx','gy'}, dimensions={0} | all-to-all | bytes 2621440 | tf_op jit(solution)/shard_map/all_to_all | solution.py:94
  37.7 0.0 copy-start.6
  37.7 0.0 copy-start.7
  37.7 0.7 convert_reduce_fusion.1
  38.4 0.2 convert_reduce_fusion
  38.6 0.4 fusion.19
  39.0 0.0 copy-done.6
  39.0 1.1 fusion.10.do_ref
  40.2 0.0 copy-done
  40.2 0.0 copy-done.7
  40.2 2.0 %convolution_convert_fusion = bf16[1024,768]{0,1:T(8,128)(2,1)} fusion(bf16[256,768]{1,0:T(8,128)(2,1)S(1)} %copy-done, f32[256]{0:T(256)S(1)} %copy-done.7, f32[1024]{0:T(1024)S(1)} %add_rsqrt_fusion, f32[1024]{0:T(1024)S(1)} %broadcast_multiply_fusion.2, bf16[1024,640]{1,0:T(8,128)(2,1)S(1)} %bitcast.28), kind=kOutput, calls=%fused_computation.3 | convolution fusion | flops 404750336 | bytes 2499584 | tf_op jit(solution)/shard_map/dot_general | solution.py:126
  42.2 73.9 %shard_map.101 = (bf16[256,1024]{1,0:T(8,128)(2,1)}, bf16[3,256,1024]{2,1,0:T(8,128)(2,1)}) custom-call(bf16[3,256,1024]{2,1,0:T(8,128)(2,1)} %bitcast.39, bf16[256,1024]{1,0:T(8,128)(2,1)} %fusion.10.do_ref, f32[1,1024]{1,0:T(1,128)} %bitcast.36), custom_call_target="tpu_custom_call" | custom-call | flops 3221225472 | bytes 4194304 | tf_op jit(solution)/shard_map/pallas_call | solution.py:68
  116.1 0.0 copy-start.5
  116.1 1.4 convolution_convert_fusion.3
  117.6 0.0 copy-done.5
  117.6 1.2 fusion.11
  118.7 4.0 %all-to-all-start.1 = ((bf16[128,8,256]{2,1,0:T(8,128)(2,1)}), bf16[128,8,256]{2,1,0:T(8,128)(2,1)S(1)}, u32[]{:S(2)}, u32[]{:S(2)}) async-start(bf16[128,8,256]{2,1,0:T(8,128)(2,1)} %fusion.11), calls=%async_computation.1 | async-start | bytes 1048576 | tf_op jit(solution)/shard_map/all_to_all | solution.py:94
  122.7 2.3 %convolution_convert_fusion.2 = bf16[256,768]{1,0:T(8,128)(2,1)S(1)} fusion(bf16[768,1024]{1,0:T(8,128)(2,1)} %bitcast.37, f32[256]{0:T(256)S(1)} %copy-done.7, f32[1024]{0:T(1024)S(1)} %add_rsqrt_fusion, f32[1024]{0:T(1024)S(1)} %broadcast_multiply_fusion.2, bf16[1024,640]{1,0:T(8,128)(2,1)S(1)} %bitcast.31), kind=kOutput, calls=%fused_computation.11 | convolution fusion | flops 404160512 | bytes 2499584 | tf_op jit(solution)/shard_map/dot_general | solution.py:141
  125.1 0.1 pad_maximum_fusion
  125.1 0.2 reshape.154
  125.4 3.4 %fusion.18 = (bf16[256]{0:T(256)(128)(2,1)S(1)}, f32[1024]{0:T(1024)S(1)}, f32[1024]{0:T(1024)S(1)}, f32[1024,256]{1,0:T(8,128)}) fusion(f32[1024]{0:T(1024)S(1)} %add_rsqrt_fusion, f32[1024]{0:T(1024)S(1)} %broadcast_multiply_fusion.2, bf16[1024,640]{1,0:T(8,128)(2,1)S(1)} %bitcast.32, f32[256]{0:T(256)S(1)} %copy-done.7, bf16[768,1024]{1,0:T(8,128)(2,1)} %bitcast.38, ...), kind=kOutput, calls=%fused_computation.27 | convolution fusion | flops 405010176 | bytes 3556864 | tf_op jit(solution)/shard_map/dot_general | solution.py:144
  128.7 0.2 reshape.160
  129.0 1.4 fusion.20
  130.3 6.4 %all-to-all-done.1 = bf16[128,8,256]{2,1,0:T(8,128)(2,1)S(1)} async-done(((bf16[128,8,256]{2,1,0:T(8,128)(2,1)}), bf16[128,8,256]{2,1,0:T(8,128)(2,1)S(1)}, u32[]{:S(2)}, u32[]{:S(2)}) %all-to-all-start.1) | async-done | bytes 524320 | tf_op jit(solution)/shard_map/all_to_all | solution.py:94
  136.8 0.0 copy-start.1
  136.8 4.0 %all-to-all-start.3 = ((bf16[128,2,1152]{2,1,0:T(2,128)(2,1)}), bf16[128,2,1152]{2,1,0:T(2,128)(2,1)S(1)}, u32[]{:S(2)}, u32[]{:S(2)}) async-start(bf16[128,2,1152]{2,1,0:T(2,128)(2,1)} %fusion.20), calls=%async_computation.3 | async-start | bytes 1179648 | tf_op jit(solution)/shard_map/all_to_all | solution.py:105
  140.8 2.6 %fusion.21 = bf16[128,8,256]{2,1,0:T(8,128)(2,1)} fusion(f32[1024,256]{1,0:T(8,128)} %get-tuple-element.36, f32[1024]{0:T(1024)S(1)} %get-tuple-element.37, f32[1024]{0:T(1024)S(1)} %get-tuple-element.38, f32[256]{0:T(256)S(1)} %copy-done.7, f32[1024]{0:T(1024)S(1)} %add_rsqrt_fusion, f32[1024]{0:T(1024)S(1)} %broadcast_multiply_fusion.2, ...), kind=kLoop, calls=%fused_computation.32 | loop fusion | flops 2883584 | bytes 2638848 | tf_op jit(solution)/shard_map/reshape | solution.py:93
  143.4 0.0 copy-done.1
  143.4 12.1 %all-to-all-done.3 = bf16[128,2,1152]{2,1,0:T(2,128)(2,1)S(1)} async-done(((bf16[128,2,1152]{2,1,0:T(2,128)(2,1)}), bf16[128,2,1152]{2,1,0:T(2,128)(2,1)S(1)}, u32[]{:S(2)}, u32[]{:S(2)}) %all-to-all-start.3) | async-done | bytes 589856 | tf_op jit(solution)/shard_map/all_to_all | solution.py:105
  155.5 4.0 %all-to-all-start.2 = ((bf16[128,8,256]{2,1,0:T(8,128)(2,1)}), bf16[128,8,256]{2,1,0:T(8,128)(2,1)S(1)}, u32[]{:S(2)}, u32[]{:S(2)}) async-start(bf16[128,8,256]{2,1,0:T(8,128)(2,1)} %fusion.21), calls=%async_computation.2 | async-start | bytes 1048576 | tf_op jit(solution)/shard_map/all_to_all | solution.py:94
  159.5 0.6 reduce_sum.62
  160.0 13.5 %all-to-all-done.2 = bf16[128,8,256]{2,1,0:T(8,128)(2,1)S(1)} async-done(((bf16[128,8,256]{2,1,0:T(8,128)(2,1)}), bf16[128,8,256]{2,1,0:T(8,128)(2,1)S(1)}, u32[]{:S(2)}, u32[]{:S(2)}) %all-to-all-start.2) | async-done | bytes 524320 | tf_op jit(solution)/shard_map/all_to_all | solution.py:94
  173.5 0.0 copy-start.3
  173.5 1.1 broadcast_in_dim.2
  174.6 4.0 %all-to-all-start.4 = ((bf16[128,2,1152]{2,1,0:T(2,128)(2,1)}), bf16[128,2,1152]{2,1,0:T(2,128)(2,1)S(1)}, u32[]{:S(2)}, u32[]{:S(2)}) async-start(bf16[128,2,1152]{2,1,0:T(2,128)(2,1)} %broadcast_in_dim.2), calls=%async_computation.4 | async-start | bytes 1179648 | tf_op jit(solution)/shard_map/all_to_all | solution.py:110
  178.7 14.7 %all-to-all-done.4 = bf16[128,2,1152]{2,1,0:T(2,128)(2,1)S(1)} async-done(((bf16[128,2,1152]{2,1,0:T(2,128)(2,1)}), bf16[128,2,1152]{2,1,0:T(2,128)(2,1)S(1)}, u32[]{:S(2)}, u32[]{:S(2)}) %all-to-all-start.4) | async-done | bytes 589856 | tf_op jit(solution)/shard_map/all_to_all | solution.py:110
  193.4 0.0 copy-done.3
  193.4 0.4 slice.64
  193.7 0.7 reshape.156
  194.4 0.7 slice_multiply_fusion.1
  195.2 1.0 slice_multiply_fusion
  196.1 0.0 copy-start.2
  196.1 0.0 copy-start.4
  196.1 0.4 convert_element_type.66
  196.6 0.2 fusion.24
  196.8 0.7 mul.83
  197.5 0.0 copy-done.2
  197.5 0.8 copy.28
  198.3 0.0 copy-done.4
  198.3 0.8 copy.29
  (3 shorter events, 0.0 us)
Async XLA Ops:
  0.6 39.5 %copy-start = (bf16[256,768]{1,0:T(8,128)(2,1)S(1)}, bf16[256,768]{1,0:T(8,128)(2,1)}, u32[]{:S(2)}) copy-start(bf16[256,768]{1,0:T(8,128)(2,1)} %param.14) | copy-start | bytes 1179652
  37.7 1.3 copy-start.6
  37.7 2.5 %copy-start.7 = (f32[256]{0:T(256)S(1)}, f32[256]{0:T(256)}, u32[]{:S(2)}) copy-start(f32[256]{0:T(256)} %param.13) | copy-start | bytes 3076
  116.1 1.4 copy-start.5
  118.7 18.0 %all-to-all-start.1 = ((bf16[128,8,256]{2,1,0:T(8,128)(2,1)}), bf16[128,8,256]{2,1,0:T(8,128)(2,1)S(1)}, u32[]{:S(2)}, u32[]{:S(2)}) async-start(bf16[128,8,256]{2,1,0:T(8,128)(2,1)} %fusion.11), calls=%async_computation.1 | async-start | bytes 1048576 | tf_op jit(solution)/shard_map/all_to_all | solution.py:94
  136.8 6.6 %copy-start.1 = (bf16[128,8,256]{2,1,0:T(8,128)(2,1)}, bf16[128,8,256]{2,1,0:T(8,128)(2,1)S(1)}, u32[]{:S(2)}) copy-start(bf16[128,8,256]{2,1,0:T(8,128)(2,1)S(1)} %all-to-all-done.1) | copy-start | bytes 1572868
  136.8 18.7 %all-to-all-start.3 = ((bf16[128,2,1152]{2,1,0:T(2,128)(2,1)}), bf16[128,2,1152]{2,1,0:T(2,128)(2,1)S(1)}, u32[]{:S(2)}, u32[]{:S(2)}) async-start(bf16[128,2,1152]{2,1,0:T(2,128)(2,1)} %fusion.20), calls=%async_computation.3 | async-start | bytes 1179648 | tf_op jit(solution)/shard_map/all_to_all | solution.py:105
  155.5 18.0 %all-to-all-start.2 = ((bf16[128,8,256]{2,1,0:T(8,128)(2,1)}), bf16[128,8,256]{2,1,0:T(8,128)(2,1)S(1)}, u32[]{:S(2)}, u32[]{:S(2)}) async-start(bf16[128,8,256]{2,1,0:T(8,128)(2,1)} %fusion.21), calls=%async_computation.2 | async-start | bytes 1048576 | tf_op jit(solution)/shard_map/all_to_all | solution.py:94
  173.5 19.8 %copy-start.3 = (bf16[128,8,256]{2,1,0:T(8,128)(2,1)}, bf16[128,8,256]{2,1,0:T(8,128)(2,1)S(1)}, u32[]{:S(2)}) copy-start(bf16[128,8,256]{2,1,0:T(8,128)(2,1)S(1)} %all-to-all-done.2) | copy-start | bytes 1572868
  174.6 18.7 %all-to-all-start.4 = ((bf16[128,2,1152]{2,1,0:T(2,128)(2,1)}), bf16[128,2,1152]{2,1,0:T(2,128)(2,1)S(1)}, u32[]{:S(2)}, u32[]{:S(2)}) async-start(bf16[128,2,1152]{2,1,0:T(2,128)(2,1)} %broadcast_in_dim.2), calls=%async_computation.4 | async-start | bytes 1179648 | tf_op jit(solution)/shard_map/all_to_all | solution.py:110
  196.1 1.3 copy-start.2
  196.1 2.1 %copy-start.4 = (bf16[128,8,256]{2,1,0:T(8,128)(2,1)S(1)}, bf16[128,8,256]{2,1,0:T(8,128)(2,1)}, u32[]{:S(2)}) copy-start(bf16[128,8,256]{2,1,0:T(8,128)(2,1)} %copy-done.3) | copy-start | bytes 1572868

commit v6 on v5

--- a/solution.py
+++ b/solution.py
@@ -9,7 +9,7 @@
 
 HEADS = 16
 K = 1024
-TQ = 256
+TQ = 512
 
 
 def layer_norm_apply(input_rows, gamma):
@@ -31,6 +31,8 @@
     d = qT.shape[0]
     dk_acc = jnp.zeros((d, n), jnp.float32)
     dv_acc = jnp.zeros((d, n), jnp.float32)
+    k_rows = kT.T
+    v_rows = vT.T
     for b in range(n // tq):
         cols = slice(b * tq, (b + 1) * tq)
         qT_b = qT[:, cols]
@@ -44,16 +46,16 @@
         l = jnp.sum(e, -1, keepdims=True)
         p = e * (1.0 / l)
         pb = p.astype(jnp.bfloat16)
-        o_ref[:, cols] = lax.dot_general(
-            vT, pb, (((1,), (1,)), ((), ())), preferred_element_type=jnp.float32
-        ).astype(o_ref.dtype)
+        o_ref[:, cols] = (
+            jnp.dot(pb, v_rows, preferred_element_type=jnp.float32).T.astype(o_ref.dtype)
+        )
         dv_acc = dv_acc + jnp.dot(doT_b, pb, preferred_element_type=jnp.float32)
         dp = jnp.dot(do_b, vT, preferred_element_type=jnp.float32)
         rs = jnp.sum(dp * p, -1, keepdims=True)
         ds = (p * (dp - rs) * scale).astype(jnp.bfloat16)
-        dqkv_ref[0, :, cols] = lax.dot_general(
-            kT, ds, (((1,), (1,)), ((), ())), preferred_element_type=jnp.float32
-        ).astype(dqkv_ref.dtype)
+        dqkv_ref[0, :, cols] = (
+            jnp.dot(ds, k_rows, preferred_element_type=jnp.float32).T.astype(dqkv_ref.dtype)
+        )
         dk_acc = dk_acc + jnp.dot(qT_b, ds, preferred_element_type=jnp.float32)
     dqkv_ref[1] = dk_acc.astype(dqkv_ref.dtype)
     dqkv_ref[2] = dv_acc.astype(dqkv_ref.dtype)

time: 200 us -> 189 us (0.945)
  Pallas kernels: 73.9 us -> 62.9 us
    pallas_call x1, Pallas kernels: 73.9 us -> 62.9 us  [fused_attention(): pl.pallas_call(kernel, grid=(heads,), in_specs=[pl.BlockSpec((3, d, n), l...]
  transfers between devices with their start and end apart: 4 -> 4, of which waited for: 4 -> 4; matrix products, arithmetic and copies ran while one was open for 5% -> 6% of each run, Pallas kernels for 0% -> 0%
where the time goes in v6:
time: 189 us; the launch traced here: 188 us
  Pallas kernels  62.9 us (33%)
  waiting for transfers between devices  46.7 us (25%)
  blocking collectives  33.5 us (18%)
  starting transfers between devices  16 us (8%)
  other arithmetic  11.5 us (6%)
  matrix products  11.4 us (6%)
  local copies, waits for them, and re-layouts  5.17 us (3%)
    pallas_call x1, Pallas kernels, fused_attention(): pl.pallas_call(kernel, grid=(heads,), in_specs=[pl.BlockSpec((3, d, n), l...  62.9 us
    all_to_all x1, blocking collectives, to_all(): lax.all_to_all(shaped, ('gx', 'gy'), split_axis=0, concat_axis=0, tiled=T...  33.5 us
    all_to_all x2, waiting for transfers between devices, to_all(): lax.all_to_all(shaped, ('gx', 'gy'), split_axis=0, concat_axis=0, tiled=T...  19.9 us
    all_to_all x1, waiting for transfers between devices, sum_all(): lax.all_to_all(spread, ('gx', 'gy'), split_axis=0, concat_axis=0, tiled=T...  14.7 us
    all_to_all x1, waiting for transfers between devices, sum_all(): lax.all_to_all(payload.astype(jnp.bfloat16), ('gx', 'gy'), split_axis=0,...  12.1 us
    all_to_all x2, starting transfers between devices, to_all(): lax.all_to_all(shaped, ('gx', 'gy'), split_axis=0, concat_axis=0, tiled=T...  7.97 us
    all_to_all x1, starting transfers between devices, sum_all(): lax.all_to_all(payload.astype(jnp.bfloat16), ('gx', 'gy'), split_axis=0,...  4.02 us
    all_to_all x1, starting transfers between devices, sum_all(): lax.all_to_all(spread, ('gx', 'gy'), split_axis=0, concat_axis=0, tiled=T...  4.02 us
  transfers between devices with their start and end apart: 4, of which 4 were waited for; matrix products, arithmetic and copies ran while one was open for 6% of the time, Pallas kernels for 0%

profile of v6, /device:TPU:1, one launch (start us, length us, event | category | flops | bytes accessed | tf_op | source)
XLA Modules:
  0.0 188.0 jit_solution(13307644606566668906)
XLA Ops:
  0.6 0.0 copy-start
  0.6 0.6 compare_reduce_fusion
  1.3 1.3 convert_select_fusion
  2.6 0.2 reshape.158
  2.8 1.3 fusion.2
  4.1 33.5 %all_to_all.25 = bf16[128,8,640]{2,1,0:T(8,128)(2,1)S(1)} all-to-all(bf16[128,8,640]{2,1,0:T(8,128)(2,1)S(1)} %fusion.2), channel_id=1, replica_groups=mesh['gx'=16,'gy'=8] {'gx','gy'}, dimensions={0} | all-to-all | bytes 2621440 | tf_op jit(solution)/shard_map/all_to_all | solution.py:96
  37.7 0.0 copy-start.6
  37.7 0.0 copy-start.7
  37.7 0.7 convert_reduce_fusion.1
  38.4 0.2 convert_reduce_fusion
  38.6 0.4 fusion.19
  39.0 0.0 copy-done.6
  39.0 1.1 fusion.10.do_ref
  40.2 0.0 copy-done
  40.2 0.0 copy-done.7
  40.2 2.0 %convolution_convert_fusion = bf16[1024,768]{0,1:T(8,128)(2,1)} fusion(bf16[256,768]{1,0:T(8,128)(2,1)S(1)} %copy-done, f32[256]{0:T(256)S(1)} %copy-done.7, f32[1024]{0:T(1024)S(1)} %add_rsqrt_fusion, f32[1024]{0:T(1024)S(1)} %broadcast_multiply_fusion.2, bf16[1024,640]{1,0:T(8,128)(2,1)S(1)} %bitcast.28), kind=kOutput, calls=%fused_computation.3 | convolution fusion | flops 404750336 | bytes 2499584 | tf_op jit(solution)/shard_map/dot_general | solution.py:128
  42.2 62.9 %shard_map.101 = (bf16[256,1024]{1,0:T(8,128)(2,1)}, bf16[3,256,1024]{2,1,0:T(8,128)(2,1)}) custom-call(bf16[3,256,1024]{2,1,0:T(8,128)(2,1)} %bitcast.39, bf16[256,1024]{1,0:T(8,128)(2,1)} %fusion.10.do_ref, f32[1,1024]{1,0:T(1,128)} %bitcast.36), custom_call_target="tpu_custom_call" | custom-call | flops 3221225472 | bytes 4194304 | tf_op jit(solution)/shard_map/pallas_call | solution.py:70
  105.1 0.0 copy-start.5
  105.1 1.4 convolution_convert_fusion.3
  106.5 0.0 copy-done.5
  106.5 1.2 fusion.11
  107.7 4.0 %all-to-all-start.1 = ((bf16[128,8,256]{2,1,0:T(8,128)(2,1)}), bf16[128,8,256]{2,1,0:T(8,128)(2,1)S(1)}, u32[]{:S(2)}, u32[]{:S(2)}) async-start(bf16[128,8,256]{2,1,0:T(8,128)(2,1)} %fusion.11), calls=%async_computation.1 | async-start | bytes 1048576 | tf_op jit(solution)/shard_map/all_to_all | solution.py:96
  111.7 2.3 %convolution_convert_fusion.2 = bf16[256,768]{1,0:T(8,128)(2,1)S(1)} fusion(bf16[768,1024]{1,0:T(8,128)(2,1)} %bitcast.37, f32[256]{0:T(256)S(1)} %copy-done.7, f32[1024]{0:T(1024)S(1)} %add_rsqrt_fusion, f32[1024]{0:T(1024)S(1)} %broadcast_multiply_fusion.2, bf16[1024,640]{1,0:T(8,128)(2,1)S(1)} %bitcast.31), kind=kOutput, calls=%fused_computation.11 | convolution fusion | flops 404160512 | bytes 2499584 | tf_op jit(solution)/shard_map/dot_general | solution.py:143
  114.0 0.1 pad_maximum_fusion
  114.1 0.2 reshape.154
  114.3 3.4 %fusion.18 = (bf16[256]{0:T(256)(128)(2,1)S(1)}, f32[1024]{0:T(1024)S(1)}, f32[1024]{0:T(1024)S(1)}, f32[1024,256]{1,0:T(8,128)}) fusion(f32[1024]{0:T(1024)S(1)} %add_rsqrt_fusion, f32[1024]{0:T(1024)S(1)} %broadcast_multiply_fusion.2, bf16[1024,640]{1,0:T(8,128)(2,1)S(1)} %bitcast.32, f32[256]{0:T(256)S(1)} %copy-done.7, bf16[768,1024]{1,0:T(8,128)(2,1)} %bitcast.38, ...), kind=kOutput, calls=%fused_computation.27 | convolution fusion | flops 405010176 | bytes 3556864 | tf_op jit(solution)/shard_map/dot_general | solution.py:146
  117.6 0.2 reshape.160
  117.9 1.4 fusion.20
  119.3 6.4 %all-to-all-done.1 = bf16[128,8,256]{2,1,0:T(8,128)(2,1)S(1)} async-done(((bf16[128,8,256]{2,1,0:T(8,128)(2,1)}), bf16[128,8,256]{2,1,0:T(8,128)(2,1)S(1)}, u32[]{:S(2)}, u32[]{:S(2)}) %all-to-all-start.1) | async-done | bytes 524320 | tf_op jit(solution)/shard_map/all_to_all | solution.py:96
  125.7 0.0 copy-start.1
  125.7 4.0 %all-to-all-start.3 = ((bf16[128,2,1152]{2,1,0:T(2,128)(2,1)}), bf16[128,2,1152]{2,1,0:T(2,128)(2,1)S(1)}, u32[]{:S(2)}, u32[]{:S(2)}) async-start(bf16[128,2,1152]{2,1,0:T(2,128)(2,1)} %fusion.20), calls=%async_computation.3 | async-start | bytes 1179648 | tf_op jit(solution)/shard_map/all_to_all | solution.py:107
  129.7 2.6 %fusion.21 = bf16[128,8,256]{2,1,0:T(8,128)(2,1)} fusion(f32[1024,256]{1,0:T(8,128)} %get-tuple-element.36, f32[1024]{0:T(1024)S(1)} %get-tuple-element.37, f32[1024]{0:T(1024)S(1)} %get-tuple-element.38, f32[256]{0:T(256)S(1)} %copy-done.7, f32[1024]{0:T(1024)S(1)} %add_rsqrt_fusion, f32[1024]{0:T(1024)S(1)} %broadcast_multiply_fusion.2, ...), kind=kLoop, calls=%fused_computation.32 | loop fusion | flops 2883584 | bytes 2638848 | tf_op jit(solution)/shard_map/reshape | solution.py:95
  132.3 0.0 copy-done.1
  132.3 12.1 %all-to-all-done.3 = bf16[128,2,1152]{2,1,0:T(2,128)(2,1)S(1)} async-done(((bf16[128,2,1152]{2,1,0:T(2,128)(2,1)}), bf16[128,2,1152]{2,1,0:T(2,128)(2,1)S(1)}, u32[]{:S(2)}, u32[]{:S(2)}) %all-to-all-start.3) | async-done | bytes 589856 | tf_op jit(solution)/shard_map/all_to_all | solution.py:107
  144.4 4.0 %all-to-all-start.2 = ((bf16[128,8,256]{2,1,0:T(8,128)(2,1)}), bf16[128,8,256]{2,1,0:T(8,128)(2,1)S(1)}, u32[]{:S(2)}, u32[]{:S(2)}) async-start(bf16[128,8,256]{2,1,0:T(8,128)(2,1)} %fusion.21), calls=%async_computation.2 | async-start | bytes 1048576 | tf_op jit(solution)/shard_map/all_to_all | solution.py:96
  148.4 0.6 reduce_sum.62
  149.0 13.5 %all-to-all-done.2 = bf16[128,8,256]{2,1,0:T(8,128)(2,1)S(1)} async-done(((bf16[128,8,256]{2,1,0:T(8,128)(2,1)}), bf16[128,8,256]{2,1,0:T(8,128)(2,1)S(1)}, u32[]{:S(2)}, u32[]{:S(2)}) %all-to-all-start.2) | async-done | bytes 524320 | tf_op jit(solution)/shard_map/all_to_all | solution.py:96
  162.4 0.0 copy-start.3
  162.4 1.1 broadcast_in_dim.2
  163.6 4.0 %all-to-all-start.4 = ((bf16[128,2,1152]{2,1,0:T(2,128)(2,1)}), bf16[128,2,1152]{2,1,0:T(2,128)(2,1)S(1)}, u32[]{:S(2)}, u32[]{:S(2)}) async-start(bf16[128,2,1152]{2,1,0:T(2,128)(2,1)} %broadcast_in_dim.2), calls=%async_computation.4 | async-start | bytes 1179648 | tf_op jit(solution)/shard_map/all_to_all | solution.py:112
  167.6 14.7 %all-to-all-done.4 = bf16[128,2,1152]{2,1,0:T(2,128)(2,1)S(1)} async-done(((bf16[128,2,1152]{2,1,0:T(2,128)(2,1)}), bf16[128,2,1152]{2,1,0:T(2,128)(2,1)S(1)}, u32[]{:S(2)}, u32[]{:S(2)}) %all-to-all-start.4) | async-done | bytes 589856 | tf_op jit(solution)/shard_map/all_to_all | solution.py:112
  182.3 0.0 copy-done.3
  182.3 0.4 slice.64
  182.7 0.7 reshape.156
  183.4 0.7 slice_multiply_fusion.1
  184.1 1.0 slice_multiply_fusion
  185.1 0.0 copy-start.2
  185.1 0.0 copy-start.4
  185.1 0.4 convert_element_type.66
  185.5 0.2 fusion.24
  185.7 0.7 mul.83
  186.4 0.0 copy-done.2
  186.4 0.8 copy.28
  187.2 0.0 copy-done.4
  187.2 0.8 copy.29
  (3 shorter events, 0.0 us)
Async XLA Ops:
  0.6 39.5 %copy-start = (bf16[256,768]{1,0:T(8,128)(2,1)S(1)}, bf16[256,768]{1,0:T(8,128)(2,1)}, u32[]{:S(2)}) copy-start(bf16[256,768]{1,0:T(8,128)(2,1)} %param.14) | copy-start | bytes 1179652
  37.7 1.3 copy-start.6
  37.7 2.5 %copy-start.7 = (f32[256]{0:T(256)S(1)}, f32[256]{0:T(256)}, u32[]{:S(2)}) copy-start(f32[256]{0:T(256)} %param.13) | copy-start | bytes 3076
  105.1 1.4 copy-start.5
  107.7 18.0 %all-to-all-start.1 = ((bf16[128,8,256]{2,1,0:T(8,128)(2,1)}), bf16[128,8,256]{2,1,0:T(8,128)(2,1)S(1)}, u32[]{:S(2)}, u32[]{:S(2)}) async-start(bf16[128,8,256]{2,1,0:T(8,128)(2,1)} %fusion.11), calls=%async_computation.1 | async-start | bytes 1048576 | tf_op jit(solution)/shard_map/all_to_all | solution.py:96
  125.7 6.6 %copy-start.1 = (bf16[128,8,256]{2,1,0:T(8,128)(2,1)}, bf16[128,8,256]{2,1,0:T(8,128)(2,1)S(1)}, u32[]{:S(2)}) copy-start(bf16[128,8,256]{2,1,0:T(8,128)(2,1)S(1)} %all-to-all-done.1) | copy-start | bytes 1572868
  125.7 18.7 %all-to-all-start.3 = ((bf16[128,2,1152]{2,1,0:T(2,128)(2,1)}), bf16[128,2,1152]{2,1,0:T(2,128)(2,1)S(1)}, u32[]{:S(2)}, u32[]{:S(2)}) async-start(bf16[128,2,1152]{2,1,0:T(2,128)(2,1)} %fusion.20), calls=%async_computation.3 | async-start | bytes 1179648 | tf_op jit(solution)/shard_map/all_to_all | solution.py:107
  144.4 18.0 %all-to-all-start.2 = ((bf16[128,8,256]{2,1,0:T(8,128)(2,1)}), bf16[128,8,256]{2,1,0:T(8,128)(2,1)S(1)}, u32[]{:S(2)}, u32[]{:S(2)}) async-start(bf16[128,8,256]{2,1,0:T(8,128)(2,1)} %fusion.21), calls=%async_computation.2 | async-start | bytes 1048576 | tf_op jit(solution)/shard_map/all_to_all | solution.py:96
  162.4 19.8 %copy-start.3 = (bf16[128,8,256]{2,1,0:T(8,128)(2,1)}, bf16[128,8,256]{2,1,0:T(8,128)(2,1)S(1)}, u32[]{:S(2)}) copy-start(bf16[128,8,256]{2,1,0:T(8,128)(2,1)S(1)} %all-to-all-done.2) | copy-start | bytes 1572868
  163.6 18.7 %all-to-all-start.4 = ((bf16[128,2,1152]{2,1,0:T(2,128)(2,1)}), bf16[128,2,1152]{2,1,0:T(2,128)(2,1)S(1)}, u32[]{:S(2)}, u32[]{:S(2)}) async-start(bf16[128,2,1152]{2,1,0:T(2,128)(2,1)} %broadcast_in_dim.2), calls=%async_computation.4 | async-start | bytes 1179648 | tf_op jit(solution)/shard_map/all_to_all | solution.py:112
  185.1 1.3 copy-start.2
  185.1 2.1 %copy-start.4 = (bf16[128,8,256]{2,1,0:T(8,128)(2,1)S(1)}, bf16[128,8,256]{2,1,0:T(8,128)(2,1)}, u32[]{:S(2)}) copy-start(bf16[128,8,256]{2,1,0:T(8,128)(2,1)} %copy-done.3) | copy-start | bytes 1572868

commit v7 on v3

--- a/solution.py
+++ b/solution.py
@@ -9,7 +9,7 @@
 
 
 HEADS = 16
-TQ = 256
+TQ = 512
 
 
 def layer_norm_apply(input_rows, gamma):
@@ -31,6 +31,8 @@
     d = qT.shape[0]
     dk_acc = jnp.zeros((d, n), jnp.float32)
     dv_acc = jnp.zeros((d, n), jnp.float32)
+    k_rows = kT.T
+    v_rows = vT.T
     for b in range(n // tq):
         cols = slice(b * tq, (b + 1) * tq)
         qT_b = qT[:, cols]
@@ -44,16 +46,16 @@
         l = jnp.sum(e, -1, keepdims=True)
         p = e * (1.0 / l)
         pb = p.astype(jnp.bfloat16)
-        o_ref[:, cols] = lax.dot_general(
-            vT, pb, (((1,), (1,)), ((), ())), preferred_element_type=jnp.float32
-        ).astype(o_ref.dtype)
+        o_ref[:, cols] = (
+            jnp.dot(pb, v_rows, preferred_element_type=jnp.float32).T.astype(o_ref.dtype)
+        )
         dv_acc = dv_acc + jnp.dot(doT_b, pb, preferred_element_type=jnp.float32)
         dp = jnp.dot(do_b, vT, preferred_element_type=jnp.float32)
         rs = jnp.sum(dp * p, -1, keepdims=True)
         ds = (p * (dp - rs) * scale).astype(jnp.bfloat16)
-        dqkv_ref[0, :, cols] = lax.dot_general(
-            kT, ds, (((1,), (1,)), ((), ())), preferred_element_type=jnp.float32
-        ).astype(dqkv_ref.dtype)
+        dqkv_ref[0, :, cols] = (
+            jnp.dot(ds, k_rows, preferred_element_type=jnp.float32).T.astype(dqkv_ref.dtype)
+        )
         dk_acc = dk_acc + jnp.dot(qT_b, ds, preferred_element_type=jnp.float32)
     dqkv_ref[1] = dk_acc.astype(dqkv_ref.dtype)
     dqkv_ref[2] = dv_acc.astype(dqkv_ref.dtype)
@@ -95,14 +97,14 @@
     return moved.reshape(array.shape)
 
 
-def scatter_sum(payload):
-    moved = lax.all_to_all(payload, ("gx", "gy"), split_axis=0, concat_axis=0, tiled=True)
-    return jnp.sum(moved, 0, keepdims=True)
-
-
-def gather_all(chunk, size):
-    spread = jnp.broadcast_to(chunk, (size,) + chunk.shape[1:])
-    return lax.all_to_all(spread, ("gx", "gy"), split_axis=0, concat_axis=0, tiled=True)
+def device_sum(got):
+    ones = jnp.ones((1, got.shape[0]), got.dtype)
+    flat = jnp.dot(ones, got.reshape(got.shape[0], -1), preferred_element_type=jnp.float32)
+    return flat.reshape((1,) + got.shape[1:])
+
+
+def exchange(payload):
+    return lax.all_to_all(payload, ("gx", "gy"), split_axis=0, concat_axis=0, tiled=True)
 
 
 def half_grads(hidden_state, d_qkvT_half, attnT_half, gt):
@@ -121,6 +123,7 @@
     inverse_root = float(nodes) ** (-0.5)
     half = HEADS // 2
     hw = width // 2
+    per_dev = rows // size
     flag = jnp.zeros((rows, 128), jnp.bfloat16).at[:, 0].set(valid.astype(jnp.bfloat16))
     moved = to_all(jnp.concatenate([features, cotangent, flag], 1))
     input_rows = moved[:, :width]
@@ -137,24 +140,35 @@
 
     attn_a, dqkv_a = fused_attention(qkvT, d_attnT, keep_row, HEADS, 0, half)
     wq_a, wo_a = half_grads(hidden_state, dqkv_a, attn_a, gt)
-    sizes_a = (wq_a.size, wo_a.size)
-    pay_a = jnp.concatenate([wq_a.reshape(-1), wo_a.reshape(-1)]).reshape(size, -1, 128)
-    mine_a = scatter_sum(pay_a)
+    n_wq = wq_a.size
+    pay_a = jnp.concatenate([wq_a.reshape(-1), wo_a.reshape(-1)]).reshape(size, -1, width)
+    got_a = exchange(pay_a.astype(jnp.bfloat16))
     attn_b, dqkv_b = fused_attention(qkvT, d_attnT, keep_row, HEADS, half, half)
-    total_a = gather_all(mine_a, size).reshape(-1)
-
+    mine_a = device_sum(got_a)
     attnT = jnp.concatenate([attn_a, attn_b], 0)
     y_val = (
         input_rows.astype(jnp.float32)
         + lax.dot_general(attnT, w_out, (((0,), (0,)), ((), ())), preferred_element_type=jnp.float32)
     ).astype(jnp.bfloat16)
-    y_plain = to_all(y_val)
+    na = pay_a.shape[1]
+    spread_a = jnp.broadcast_to(mine_a.astype(jnp.bfloat16), (size, na, width))
+    back_a = exchange(
+        jnp.concatenate([spread_a, y_val.reshape(size, per_dev, width)], 1)
+    )
+    total_a = back_a[:, :na].astype(jnp.float32).reshape(-1)
+    y_plain = back_a[:, na:].reshape(rows, width)
+
     wq_b, wo_b = half_grads(hidden_state, dqkv_b, attn_b, gt)
     d_qkvT = jnp.concatenate([dqkv_a, dqkv_b], 1).reshape(3 * width, rows)
     hidden_gradient = lax.dot_general(
         d_qkvT, w_qkv, (((0,), (1,)), ((), ())), preferred_element_type=jnp.float32
     )
-    shard_gamma = jnp.sum(hidden_gradient * normalized_input, 0)
+    shard_gamma = jnp.dot(
+        jnp.ones((1, rows), jnp.float32),
+        hidden_gradient * normalized_input,
+        precision=lax.Precision.HIGHEST,
+        preferred_element_type=jnp.float32,
+    )[0]
     scaled_output = hidden_gradient * gamma
     norm_gradient = reciprocal_deviation * (
         scaled_output
@@ -162,19 +176,25 @@
         - normalized_input * jnp.mean(scaled_output * normalized_input, -1, keepdims=True)
     )
     d_x = (gt.astype(jnp.float32) + norm_gradient).astype(jnp.bfloat16)
-    main_b = jnp.concatenate([wq_b.reshape(-1), wo_b.reshape(-1)]).reshape(size, -1, 128)
+    main_b = jnp.concatenate([wq_b.reshape(-1), wo_b.reshape(-1)]).reshape(size, -1, width)
     per = width // size
-    side = jnp.zeros((size, 1, 128), jnp.float32).at[:, 0, :per].set(shard_gamma.reshape(size, per))
+    side = jnp.zeros((size, 1, width), jnp.float32).at[:, 0, :per].set(
+        shard_gamma.reshape(size, per)
+    )
     pay_b = jnp.concatenate([main_b, side], 1)
-    mine_b = scatter_sum(pay_b)
-    dx_plain = to_all(d_x)
-    total_b = gather_all(mine_b, size)
+    nb = pay_b.shape[1]
+    payload = jnp.concatenate([d_x.reshape(size, per_dev, width), pay_b.astype(jnp.bfloat16)], 1)
+    moved_b = exchange(payload)
+    dx_plain = moved_b[:, :per_dev].reshape(rows, width)
+    mine_b = device_sum(moved_b[:, per_dev:])
+    total_b = exchange(jnp.broadcast_to(mine_b.astype(jnp.bfloat16), (size, nb, width)))
+    total_b = total_b.astype(jnp.float32)
     gamma_total = total_b[:, -1, :per].reshape(width)
     flat_b = total_b[:, :-1, :].reshape(-1)
 
     def unpack(flat):
-        wq = flat[: sizes_a[0]].reshape(width, 3, hw)
-        wo = flat[sizes_a[0] :].reshape(hw, width)
+        wq = flat[:n_wq].reshape(width, 3, hw)
+        wo = flat[n_wq:].reshape(hw, width)
         return wq, wo
 
     wq_ta, wo_ta = unpack(total_a)

time: 249 us -> 206 us (0.83)
  waiting for transfers between devices: 79.5 us -> 43.7 us
  Pallas kernels: 75.5 us -> 64.4 us
  other arithmetic: 10.6 us -> 15.4 us
  local copies, waits for them, and re-layouts: 10.7 us -> 14.9 us
  matrix products: 13 us -> 10 us
    all_to_all x6 -> x4, waiting for transfers between devices: 79.5 us -> 43.7 us  [exchange(): lax.all_to_all(payload, ('gx', 'gy'), split_axis=0, concat_axis=0, tiled=...]
    pallas_call x2, Pallas kernels: 75.5 us -> 64.4 us  [fused_attention(): pl.pallas_call(kernel, grid=(count,), in_specs=[pl.BlockSpec((3, d, n), l...]
    dot_general x0 -> x4, local copies, waits for them, and re-layouts: none -> 3.16 us  [the longest x2 3.15 us: block(): jnp.dot(jnp.ones((1, rows), jnp.float32), hidden_gradient * normalized_in...]
    concatenate x1 -> x4, other arithmetic: 1.07 us -> 3.76 us  [the longest x1 1.45 us: block(): jnp.concatenate([spread_a, y_val.reshape(size, per_dev, width)], 1)]
    dot_general x2, matrix products: 4.26 us -> 1.62 us  [half_grads(): lax.dot_general(hidden_state, d_qkvT_half.reshape(-1, d_qkvT_half.shape[-...]
    all_to_all x6 -> x4, starting transfers between devices: 24 us -> 22.6 us  [exchange(): lax.all_to_all(payload, ('gx', 'gy'), split_axis=0, concat_axis=0, tiled=...]
  transfers between devices with their start and end apart: 6 -> 4, of which waited for: 6 -> 3; matrix products, arithmetic and copies ran while one was open for 6% -> 11% of each run, Pallas kernels for 0% -> 0%
where the time goes in v7:
time: 206 us
  Pallas kernels  64.4 us (31%)
  waiting for transfers between devices  43.7 us (21%)
  blocking collectives  33.5 us (16%)
  starting transfers between devices  22.6 us (11%)
  other arithmetic  15.4 us (7%)
  local copies, waits for them, and re-layouts  14.9 us (7%)
  matrix products  10 us (5%)
    pallas_call x2, Pallas kernels, fused_attention(): pl.pallas_call(kernel, grid=(count,), in_specs=[pl.BlockSpec((3, d, n), l...  64.4 us
    all_to_all x4, waiting for transfers between devices, exchange(): lax.all_to_all(payload, ('gx', 'gy'), split_axis=0, concat_axis=0, tiled=...  43.7 us
    all_to_all x1, blocking collectives, to_all(): lax.all_to_all(shaped, ('gx', 'gy'), split_axis=0, concat_axis=0, tiled=T...  33.5 us
    all_to_all x4, starting transfers between devices, exchange(): lax.all_to_all(payload, ('gx', 'gy'), split_axis=0, concat_axis=0, tiled=...  22.6 us
  transfers between devices with their start and end apart: 4, of which 3 were waited for; matrix products, arithmetic and copies ran while one was open for 11% of the time, Pallas kernels for 0%

profile of v7, /device:TPU:1, one launch (start us, length us, event | category | flops | bytes accessed | tf_op | source)
XLA Modules:
  0.0 205.6 jit_solution(16690592603572007026)
XLA Ops:
  0.6 0.0 copy-start
  0.6 0.6 compare_reduce_fusion
  1.3 1.3 convert_select_fusion
  2.6 0.2 reshape.245
  2.8 1.3 fusion.3
  4.1 0.0 copy-start.6
  4.2 33.5 %all_to_all.25 = bf16[128,8,640]{2,1,0:T(8,128)(2,1)S(1)} all-to-all(bf16[128,8,640]{2,1,0:T(8,128)(2,1)S(1)} %fusion.3), channel_id=1, replica_groups=mesh['gx'=16,'gy'=8] {'gx','gy'}, dimensions={0} | all-to-all | bytes 2621440 | tf_op jit(solution)/shard_map/all_to_all | solution.py:96
  37.7 0.7 convert_reduce_fusion.1
  38.4 0.2 convert_reduce_fusion
  38.6 0.4 fusion.22
  39.0 1.1 fusion.11.do_ref
  40.2 2.1 %convolution_convert_fusion = bf16[1024,768]{0,1:T(8,128)(2,1)} fusion(bf16[256,768]{1,0:T(8,128)(2,1)S(1)} %copy-done, f32[256]{0:T(256)S(1)} %copy-done.8, f32[1024]{0:T(1024)S(1)} %add_rsqrt_fusion, f32[1024]{0:T(1024)S(1)} %broadcast_multiply_fusion.2, bf16[1024,640]{1,0:T(8,128)(2,1)S(1)} %bitcast.69), kind=kOutput, calls=%fused_computation.4 | convolution fusion | flops 404750336 | bytes 2499584 | tf_op jit(solution)/shard_map/dot_general | solution.py:133
  42.2 32.2 %shard_map.102 = (bf16[128,1024]{1,0:T(8,128)(2,1)}, bf16[3,128,1024]{2,1,0:T(8,128)(2,1)}) custom-call(bf16[3,256,1024]{2,1,0:T(8,128)(2,1)} %bitcast.88, bf16[256,1024]{1,0:T(8,128)(2,1)} %fusion.11.do_ref, f32[1,1024]{1,0:T(1,128)} %bitcast.85), custom_call_target="tpu_custom_call" | custom-call | flops 1610612736 | bytes 2097152 | tf_op jit(solution)/shard_map/pallas_call | solution.py:70
  74.4 32.2 %shard_map.101 = (bf16[128,1024]{1,0:T(8,128)(2,1)}, bf16[3,128,1024]{2,1,0:T(8,128)(2,1)}) custom-call(bf16[3,256,1024]{2,1,0:T(8,128)(2,1)} %bitcast.89, bf16[256,1024]{1,0:T(8,128)(2,1)} %fusion.11.do_ref, f32[1,1024]{1,0:T(1,128)} %bitcast.86), custom_call_target="tpu_custom_call" | custom-call | flops 1610612736 | bytes 2097152 | tf_op jit(solution)/shard_map/pallas_call | solution.py:70
  106.7 0.2 fusion.14
  106.9 0.7 copy.70
  107.6 1.2 fusion.13
  108.8 0.1 copy.68
  108.9 0.8 convolution_convert_fusion.3
  109.7 0.1 reshape.220
  109.8 0.9 convert_element_type.71
  110.7 4.9 %all-to-all-start.1 = ((bf16[128,4,256]{2,1,0:T(4,128)(2,1)}), bf16[128,4,256]{2,1,0:T(4,128)(2,1)}, u32[]{:S(2)}, u32[]{:S(2)}) async-start(bf16[128,4,256]{2,1,0:T(4,128)(2,1)} %convert_element_type.71), calls=%async_computation.1 | async-start | bytes 524288 | tf_op jit(solution)/shard_map/all_to_all | solution.py:107
  115.6 1.6 pad_maximum_fusion
  117.1 0.0 copy-done.4
  117.2 0.8 convolution_convert_fusion.2
  118.0 0.8 reshape.228
  118.7 1.0 pad_maximum_fusion.3
  119.7 0.9 reshape.230
  120.6 1.2 multiply_reduce_fusion
  121.8 1.7 fusion.24
  123.5 1.6 copy.48
  125.1 1.6 dot_general.57
  126.7 1.5 bitcast_reduce_fusion
  128.2 0.1 copy.71
  128.3 0.2 copy.66
  128.5 1.3 fusion.23
  129.8 9.9 %all-to-all-start.3 = ((bf16[128,13,256]{2,1,0:T(8,128)(2,1)}), bf16[128,13,256]{2,1,0:T(8,128)(2,1)S(1)}, u32[]{:S(2)}, u32[]{:S(2)}) async-start(bf16[128,13,256]{2,1,0:T(8,128)(2,1)} %fusion.23), calls=%async_computation.3 | async-start | bytes 2097152 | tf_op jit(solution)/shard_map/all_to_all | solution.py:107
  139.7 0.4 fusion.12
  140.1 1.1 fusion.33
  141.2 0.1 broadcast_in_dim.6
  141.2 1.5 pad_maximum_fusion.1
  142.7 16.5 %all-to-all-done.3 = bf16[128,13,256]{2,1,0:T(8,128)(2,1)S(1)} async-done(((bf16[128,13,256]{2,1,0:T(8,128)(2,1)}), bf16[128,13,256]{2,1,0:T(8,128)(2,1)S(1)}, u32[]{:S(2)}, u32[]{:S(2)}) %all-to-all-start.3) | async-done | bytes 852000 | tf_op jit(solution)/shard_map/all_to_all | solution.py:107
  159.2 3.9 %all-to-all-start.2 = ((bf16[128,12,256]{2,1,0:T(8,128)(2,1)}), bf16[128,12,256]{2,1,0:T(8,128)(2,1)S(1)}, u32[]{:S(2)}, u32[]{:S(2)}) async-start(bf16[128,12,256]{2,1,0:T(8,128)(2,1)} %pad_maximum_fusion.1), calls=%async_computation.2 | async-start | bytes 2097152 | tf_op jit(solution)/shard_map/all_to_all | solution.py:107
  163.1 1.0 copy.50
  164.2 1.2 fusion.31
  165.3 0.9 slice_bitcast_fusion
  166.2 16.5 %all-to-all-done.2 = bf16[128,12,256]{2,1,0:T(8,128)(2,1)S(1)} async-done(((bf16[128,12,256]{2,1,0:T(8,128)(2,1)}), bf16[128,12,256]{2,1,0:T(8,128)(2,1)S(1)}, u32[]{:S(2)}, u32[]{:S(2)}) %all-to-all-start.2) | async-done | bytes 786464 | tf_op jit(solution)/shard_map/all_to_all | solution.py:107
  182.7 0.9 broadcast_in_dim.8
  183.5 0.3 copy-done.1
  183.8 3.9 %all-to-all-start.4 = ((bf16[128,5,256]{2,1,0:T(8,128)(2,1)}), bf16[128,5,256]{2,1,0:T(8,128)(2,1)S(1)}, u32[]{:S(2)}, u32[]{:S(2)}) async-start(bf16[128,5,256]{2,1,0:T(8,128)(2,1)} %broadcast_in_dim.8), calls=%async_computation.4 | async-start | bytes 1048576 | tf_op jit(solution)/shard_map/all_to_all | solution.py:107
  187.7 1.1 slice_convert_fusion
  189.0 0.3 reshape.233
  189.3 0.8 copy-done.2
  190.1 0.9 slice_bitcast_fusion.1
  191.0 10.8 %all-to-all-done.4 = bf16[128,5,256]{2,1,0:T(8,128)(2,1)S(1)} async-done(((bf16[128,5,256]{2,1,0:T(8,128)(2,1)}), bf16[128,5,256]{2,1,0:T(8,128)(2,1)S(1)}, u32[]{:S(2)}, u32[]{:S(2)}) %all-to-all-start.4) | async-done | bytes 327712 | tf_op jit(solution)/shard_map/all_to_all | solution.py:107
  201.9 0.1 slice.100
  202.0 0.3 reshape.235
  202.3 0.1 maximum_multiply_fusion
  202.4 0.3 copy.53
  202.7 1.1 copy.54
  203.8 0.1 convert_element_type.78
  203.9 0.2 fusion.36
  204.1 0.7 mul.87
  204.8 0.7 maximum_multiply_fusion.1
  (34 shorter events, 0.3 us)
Async XLA Ops:
  0.6 39.5 %copy-start = (bf16[256,768]{1,0:T(8,128)(2,1)S(1)}, bf16[256,768]{1,0:T(8,128)(2,1)}, u32[]{:S(2)}) copy-start(bf16[256,768]{1,0:T(8,128)(2,1)} %param.14) | copy-start | bytes 1179652
  4.1 34.9 %copy-start.6 = (bf16[256,256]{1,0:T(8,128)(2,1)S(1)}, bf16[256,256]{1,0:T(8,128)(2,1)}, u32[]{:S(2)}) copy-start(bf16[256,256]{1,0:T(8,128)(2,1)} %param.15) | copy-start | bytes 393220
  37.7 2.5 %copy-start.8 = (f32[256]{0:T(256)S(1)}, f32[256]{0:T(256)}, u32[]{:S(2)}) copy-start(f32[256]{0:T(256)} %param.13) | copy-start | bytes 3076
  74.4 32.2 %copy-start.9 = (bf16[128,1024]{1,0:T(8,128)(2,1)S(1)}, bf16[128,1024]{1,0:T(8,128)(2,1)}, u32[]{:S(2)}) copy-start(bf16[128,1024]{1,0:T(8,128)(2,1)} %get-tuple-element.35) | copy-start | bytes 786436
  106.7 2.2 %copy-start.5 = (bf16[3,128,1024]{2,1,0:T(8,128)(2,1)S(1)}, bf16[3,128,1024]{2,1,0:T(8,128)(2,1)}, u32[]{:S(2)}) copy-start(bf16[3,128,1024]{2,1,0:T(8,128)(2,1)} %get-tuple-element.33) | copy-start | bytes 2359300
  110.7 19.1 %all-to-all-start.1 = ((bf16[128,4,256]{2,1,0:T(4,128)(2,1)}), bf16[128,4,256]{2,1,0:T(4,128)(2,1)}, u32[]{:S(2)}, u32[]{:S(2)}) async-start(bf16[128,4,256]{2,1,0:T(4,128)(2,1)} %convert_element_type.71), calls=%async_computation.1 | async-start | bytes 524288 | tf_op jit(solution)/shard_map/all_to_all | solution.py:107
  115.5 1.6 copy-start.4
  125.1 3.4 %copy-start.3 = (bf16[128,4,256]{2,1,0:T(4,128)(2,1)S(1)}, bf16[128,4,256]{2,1,0:T(4,128)(2,1)}, u32[]{:S(2)}) copy-start(bf16[128,4,256]{2,1,0:T(4,128)(2,1)} %reshape.230) | copy-start | bytes 786436
  129.8 9.9 %copy-start.7 = (bf16[256,256]{1,0:T(8,128)(2,1)S(1)}, bf16[256,256]{1,0:T(8,128)(2,1)}, u32[]{:S(2)}) copy-start(bf16[256,256]{1,0:T(8,128)(2,1)} %param.15) | copy-start | bytes 393220
  129.8 9.9 %copy-start.10 = (bf16[128,1024]{1,0:T(8,128)(2,1)S(1)}, bf16[128,1024]{1,0:T(8,128)(2,1)}, u32[]{:S(2)}) copy-start(bf16[128,1024]{1,0:T(8,128)(2,1)} %get-tuple-element.35) | copy-start | bytes 786436
  129.8 9.9 %copy-start.11 = (bf16[128,1024]{1,0:T(8,128)(2,1)S(1)}, bf16[128,1024]{1,0:T(8,128)(2,1)}, u32[]{:S(2)}) copy-start(bf16[128,1024]{1,0:T(8,128)(2,1)} %get-tuple-element.34) | copy-start | bytes 786436
  129.8 29.4 %all-to-all-start.3 = ((bf16[128,13,256]{2,1,0:T(8,128)(2,1)}), bf16[128,13,256]{2,1,0:T(8,128)(2,1)S(1)}, u32[]{:S(2)}, u32[]{:S(2)}) async-start(bf16[128,13,256]{2,1,0:T(8,128)(2,1)} %fusion.23), calls=%async_computation.3 | async-start | bytes 2097152 | tf_op jit(solution)/shard_map/all_to_all | solution.py:107
  159.2 23.5 %all-to-all-start.2 = ((bf16[128,12,256]{2,1,0:T(8,128)(2,1)}), bf16[128,12,256]{2,1,0:T(8,128)(2,1)S(1)}, u32[]{:S(2)}, u32[]{:S(2)}) async-start(bf16[128,12,256]{2,1,0:T(8,128)(2,1)} %pad_maximum_fusion.1), calls=%async_computation.2 | async-start | bytes 2097152 | tf_op jit(solution)/shard_map/all_to_all | solution.py:107
  182.7 1.2 copy-start.1
  183.8 18.0 %all-to-all-start.4 = ((bf16[128,5,256]{2,1,0:T(8,128)(2,1)}), bf16[128,5,256]{2,1,0:T(8,128)(2,1)S(1)}, u32[]{:S(2)}, u32[]{:S(2)}) async-start(bf16[128,5,256]{2,1,0:T(8,128)(2,1)} %broadcast_in_dim.8), calls=%async_computation.4 | async-start | bytes 1048576 | tf_op jit(solution)/shard_map/all_to_all | solution.py:107
  188.8 1.2 copy-start.2

commit v8 on v6

--- a/solution.py
+++ b/solution.py
@@ -22,62 +22,64 @@
     return (normalized_input, reciprocal_deviation, (normalized_input * gamma).astype(jnp.bfloat16))
 
 
-def _attn_kernel(qkv_ref, do_ref, keep_ref, o_ref, dqkv_ref, *, scale, n, tq):
-    qT = qkv_ref[0]
-    kT = qkv_ref[1]
-    vT = qkv_ref[2]
-    doT = do_ref[...]
+def _attn_kernel(qkv_ref, do_ref, keep_ref, o_ref, dqkv_ref, *, scale, n, tq, d, group):
     keep = keep_ref[...] > 0.5
-    d = qT.shape[0]
-    dk_acc = jnp.zeros((d, n), jnp.float32)
-    dv_acc = jnp.zeros((d, n), jnp.float32)
-    k_rows = kT.T
-    v_rows = vT.T
-    for b in range(n // tq):
-        cols = slice(b * tq, (b + 1) * tq)
-        qT_b = qT[:, cols]
-        doT_b = doT[:, cols]
-        q_b = qT_b.T
-        do_b = doT_b.T
-        s = jnp.dot(q_b, kT, preferred_element_type=jnp.float32) * scale
-        s = jnp.where(keep, s, -1e30)
-        m = jnp.max(s, -1, keepdims=True)
-        e = jnp.exp(s - m)
-        l = jnp.sum(e, -1, keepdims=True)
-        p = e * (1.0 / l)
-        pb = p.astype(jnp.bfloat16)
-        o_ref[:, cols] = (
-            jnp.dot(pb, v_rows, preferred_element_type=jnp.float32).T.astype(o_ref.dtype)
-        )
-        dv_acc = dv_acc + jnp.dot(doT_b, pb, preferred_element_type=jnp.float32)
-        dp = jnp.dot(do_b, vT, preferred_element_type=jnp.float32)
-        rs = jnp.sum(dp * p, -1, keepdims=True)
-        ds = (p * (dp - rs) * scale).astype(jnp.bfloat16)
-        dqkv_ref[0, :, cols] = (
-            jnp.dot(ds, k_rows, preferred_element_type=jnp.float32).T.astype(dqkv_ref.dtype)
-        )
-        dk_acc = dk_acc + jnp.dot(qT_b, ds, preferred_element_type=jnp.float32)
-    dqkv_ref[1] = dk_acc.astype(dqkv_ref.dtype)
-    dqkv_ref[2] = dv_acc.astype(dqkv_ref.dtype)
+    for g in range(group):
+        rows = slice(g * d, (g + 1) * d)
+        qT = qkv_ref[0, rows, :]
+        kT = qkv_ref[1, rows, :]
+        vT = qkv_ref[2, rows, :]
+        doT = do_ref[rows, :]
+        dk_acc = jnp.zeros((d, n), jnp.float32)
+        dv_acc = jnp.zeros((d, n), jnp.float32)
+        k_rows = kT.T
+        v_rows = vT.T
+        for b in range(n // tq):
+            cols = slice(b * tq, (b + 1) * tq)
+            qT_b = qT[:, cols]
+            doT_b = doT[:, cols]
+            q_b = qT_b.T
+            do_b = doT_b.T
+            s = jnp.dot(q_b, kT, preferred_element_type=jnp.float32) * scale
+            s = jnp.where(keep, s, -1e30)
+            m = jnp.max(s, -1, keepdims=True)
+            e = jnp.exp(s - m)
+            l = jnp.sum(e, -1, keepdims=True)
+            p = e * (1.0 / l)
+            pb = p.astype(jnp.bfloat16)
+            o_ref[rows, cols] = (
+                jnp.dot(pb, v_rows, preferred_element_type=jnp.float32).T.astype(o_ref.dtype)
+            )
+            dv_acc = dv_acc + jnp.dot(doT_b, pb, preferred_element_type=jnp.float32)
+            dp = jnp.dot(do_b, vT, preferred_element_type=jnp.float32)
+            rs = jnp.sum(dp * p, -1, keepdims=True)
+            ds = (p * (dp - rs) * scale).astype(jnp.bfloat16)
+            dqkv_ref[0, rows, cols] = (
+                jnp.dot(ds, k_rows, preferred_element_type=jnp.float32).T.astype(dqkv_ref.dtype)
+            )
+            dk_acc = dk_acc + jnp.dot(qT_b, ds, preferred_element_type=jnp.float32)
+        dqkv_ref[1, rows, :] = dk_acc.astype(dqkv_ref.dtype)
+        dqkv_ref[2, rows, :] = dv_acc.astype(dqkv_ref.dtype)
 
 
 def fused_attention(qkvT, doT, keep_row, heads):
     _, c, n = qkvT.shape
     d = c // heads
     scale = d ** (-0.5)
-    kernel = functools.partial(_attn_kernel, scale=scale, n=n, tq=TQ)
+    group = 2
+    kernel = functools.partial(_attn_kernel, scale=scale, n=n, tq=TQ, d=d, group=group)
     flops = heads * 6 * 2 * n * n * d
     return pl.pallas_call(
         kernel,
-        grid=(heads,),
+        grid=(heads // group,),
         in_specs=[
-            pl.BlockSpec((3, d, n), lambda h: (0, h, 0)),
-            pl.BlockSpec((d, n), lambda h: (h, 0)),
+            pl.BlockSpec((3, group * d, n), lambda h: (0, h, 0)),
+            pl.BlockSpec((group * d, n), lambda h: (h, 0)),
             pl.BlockSpec((1, n), lambda h: (0, 0)),
         ],
         out_specs=[
-            pl.BlockSpec((d, n), lambda h: (h, 0)),
-            pl.BlockSpec((3, d, n), lambda h: (0, h, 0)),
+            pl.BlockSpec((group * d, n), lambda h: (h, 0)),
+            pl.BlockSpec((3, group * d, n), lambda h: (0, h, 0)),
         ],
         out_shape=[
             jax.ShapeDtypeStruct((c, n), jnp.bfloat16),
@@ -97,7 +99,7 @@
     return moved.reshape(array.shape)
 
 
-def sum_all(parts):
+def sum_all(parts, scale):
     size = lax.axis_size("gx") * lax.axis_size("gy")
     matrix, vector = parts
     rows, cols = matrix.shape
@@ -107,8 +109,9 @@
     moved = lax.all_to_all(
         payload.astype(jnp.bfloat16), ("gx", "gy"), split_axis=0, concat_axis=0, tiled=True
     )
-    mine = jnp.sum(moved.astype(jnp.float32), 0, keepdims=True)
-    spread = jnp.broadcast_to(mine.astype(jnp.bfloat16), payload.shape)
+    ones = jnp.ones((1, size), jnp.bfloat16)
+    mine = jnp.dot(ones, moved.reshape(size, -1), preferred_element_type=jnp.float32) * scale
+    spread = jnp.broadcast_to(mine.astype(jnp.bfloat16).reshape((1,) + payload.shape[1:]), payload.shape)
     total = lax.all_to_all(
         spread, ("gx", "gy"), split_axis=0, concat_axis=0, tiled=True
     ).astype(jnp.float32)
@@ -146,7 +149,12 @@
     hidden_gradient = lax.dot_general(
         d_qkvT, w_qkv, (((0,), (1,)), ((), ())), preferred_element_type=jnp.float32
     )
-    shard_gamma = jnp.sum(hidden_gradient * normalized_input, 0)
+    shard_gamma = jnp.dot(
+        jnp.ones((1, rows), jnp.float32),
+        hidden_gradient * normalized_input,
+        precision=lax.Precision.HIGHEST,
+        preferred_element_type=jnp.float32,
+    )[0]
     scaled_output = hidden_gradient * gamma
     norm_gradient = reciprocal_deviation * (
         scaled_output
@@ -155,15 +163,15 @@
     )
     d_x = (gt.astype(jnp.float32) + norm_gradient).astype(jnp.bfloat16)
     total_w, total_gamma = sum_all(
-        (jnp.concatenate([local_wqkv, local_wout], 1), shard_gamma)
+        (jnp.concatenate([local_wqkv, local_wout], 1), shard_gamma), inverse_root
     )
     dx_plain = to_all(d_x)
     return (
         y_plain,
         dx_plain,
-        total_w[:, : 3 * width] * inverse_root,
-        total_w[:, 3 * width :] * inverse_root,
-        total_gamma * inverse_root,
+        total_w[:, : 3 * width],
+        total_w[:, 3 * width :],
+        total_gamma,
     )
 
 

time: 189 us -> 190 us (level)
  blocking collectives: 33.5 us -> 52 us
  waiting for transfers between devices: 46.7 us -> 35.5 us
  starting transfers between devices: 16 us -> 12 us
  local copies, waits for them, and re-layouts: 5.17 us -> 8.87 us
    all_to_all x0 -> x1, blocking collectives: none -> 18.5 us  [sum_all(): lax.all_to_all(payload.astype(jnp.bfloat16), ('gx', 'gy'), split_axis=0,...]
    all_to_all x1 -> x0, waiting for transfers between devices: 12.1 us -> none  [sum_all(): lax.all_to_all(payload.astype(jnp.bfloat16), ('gx', 'gy'), split_axis=0,...]
    all_to_all x1 -> x0, starting transfers between devices: 4.02 us -> none  [sum_all(): lax.all_to_all(payload.astype(jnp.bfloat16), ('gx', 'gy'), split_axis=0,...]
    dot_general x0 -> x1, other arithmetic: none -> 2.65 us  [shards(): jnp.dot(jnp.ones((1, rows), jnp.float32), hidden_gradient * normalized_in...]
    reshape x2 -> x1, other arithmetic: 3.91 us -> 1.31 us  [to_all(): shaped = array.reshape(size, -1, array.shape[-1])]
  transfers between devices with their start and end apart: 4 -> 3, of which waited for: 4 -> 3; matrix products, arithmetic and copies ran while one was open for 6% -> 4% of each run, Pallas kernels for 0% -> 0%
where the time goes in v8:
time: 190 us
  Pallas kernels  61.4 us (32%)
  blocking collectives  52 us (27%)
  waiting for transfers between devices  35.5 us (19%)
  starting transfers between devices  12 us (6%)
  matrix products  9.7 us (5%)
  other arithmetic  9.63 us (5%)
  local copies, waits for them, and re-layouts  8.87 us (5%)
    pallas_call x1, Pallas kernels, fused_attention(): pl.pallas_call(kernel, grid=(heads // group,), in_specs=[pl.BlockSpec((3,...  61.4 us
    all_to_all x1, blocking collectives, to_all(): lax.all_to_all(shaped, ('gx', 'gy'), split_axis=0, concat_axis=0, tiled=T...  33.5 us
    all_to_all x2, waiting for transfers between devices, to_all(): lax.all_to_all(shaped, ('gx', 'gy'), split_axis=0, concat_axis=0, tiled=T...  20.8 us
    all_to_all x1, blocking collectives, sum_all(): lax.all_to_all(payload.astype(jnp.bfloat16), ('gx', 'gy'), split_axis=0,...  18.5 us
    all_to_all x1, waiting for transfers between devices, sum_all(): lax.all_to_all(spread, ('gx', 'gy'), split_axis=0, concat_axis=0, tiled=T...  14.7 us
    all_to_all x2, starting transfers between devices, to_all(): lax.all_to_all(shaped, ('gx', 'gy'), split_axis=0, concat_axis=0, tiled=T...  8 us
    all_to_all x1, starting transfers between devices, sum_all(): lax.all_to_all(spread, ('gx', 'gy'), split_axis=0, concat_axis=0, tiled=T...  4.02 us
  transfers between devices with their start and end apart: 3, of which 3 were waited for; matrix products, arithmetic and copies ran while one was open for 4% of the time, Pallas kernels for 0%

profile of v8, /device:TPU:1, one launch (start us, length us, event | category | flops | bytes accessed | tf_op | source)
XLA Modules:
  0.0 190.0 jit_solution(1188081337678859156)
XLA Ops:
  0.6 0.0 copy-start
  0.6 0.6 compare_reduce_fusion
  1.3 1.3 convert_select_fusion
  2.6 0.2 reshape.169
  2.8 1.3 fusion.2
  4.1 33.5 %all_to_all.25 = bf16[128,8,640]{2,1,0:T(8,128)(2,1)S(1)} all-to-all(bf16[128,8,640]{2,1,0:T(8,128)(2,1)S(1)} %fusion.2), channel_id=1, replica_groups=mesh['gx'=16,'gy'=8] {'gx','gy'}, dimensions={0} | all-to-all | bytes 2621440 | tf_op jit(solution)/shard_map/all_to_all | solution.py:98
  37.7 0.0 copy-start.6
  37.7 0.0 copy-start.8
  37.7 0.7 convert_reduce_fusion.1
  38.4 0.2 convert_reduce_fusion
  38.6 0.4 fusion.19
  39.0 0.0 copy-done.6
  39.0 1.1 fusion.10.do_ref
  40.2 0.0 copy-done
  40.2 0.0 copy-done.8
  40.2 2.1 %convolution_convert_fusion = bf16[1024,768]{0,1:T(8,128)(2,1)} fusion(bf16[256,768]{1,0:T(8,128)(2,1)S(1)} %copy-done, f32[256]{0:T(256)S(1)} %copy-done.8, f32[1024]{0:T(1024)S(1)} %add_rsqrt_fusion, f32[1024]{0:T(1024)S(1)} %broadcast_multiply_fusion.2, bf16[1024,640]{1,0:T(8,128)(2,1)S(1)} %bitcast.36), kind=kOutput, calls=%fused_computation.3 | convolution fusion | flops 404750336 | bytes 2499584 | tf_op jit(solution)/shard_map/dot_general | solution.py:131
  42.2 61.4 %shard_map.101 = (bf16[256,1024]{1,0:T(8,128)(2,1)}, bf16[3,256,1024]{2,1,0:T(8,128)(2,1)}) custom-call(bf16[3,256,1024]{2,1,0:T(8,128)(2,1)} %bitcast.50, bf16[256,1024]{1,0:T(8,128)(2,1)} %fusion.10.do_ref, f32[1,1024]{1,0:T(1,128)} %bitcast.46), custom_call_target="tpu_custom_call" | custom-call | flops 3221225472 | bytes 4194304 | tf_op jit(solution)/shard_map/pallas_call | solution.py:72
  103.6 0.0 copy-start.5
  103.6 0.0 copy-start.9
  103.6 1.5 convolution_convert_fusion.3
  105.1 0.0 copy-done.5
  105.1 1.2 fusion.11
  106.3 0.0 copy-done.9
  106.3 1.7 convolution_convert_fusion.2
  108.0 2.0 %multiply_reduce_fusion = (f32[1024]{0:T(1024)S(1)}, f32[1024]{0:T(1024)S(1)}, f32[1024,256]{1,0:T(8,128)}) fusion(f32[256]{0:T(256)S(1)} %copy-done.8, f32[1024]{0:T(1024)S(1)} %add_rsqrt_fusion, f32[1024]{0:T(1024)S(1)} %broadcast_multiply_fusion.2, bf16[1024,640]{1,0:T(8,128)(2,1)S(1)} %bitcast.40, bf16[768,1024]{1,0:T(8,128)(2,1)S(1)} %bitcast.49, ...), kind=kOutput, calls=%fused_computation.31 | convolution fusion | flops 404486144 | bytes 3556352 | tf_op jit(solution)/shard_map/dot_general | solution.py:149
  109.9 4.0 %all-to-all-start.1 = ((bf16[128,8,256]{2,1,0:T(8,128)(2,1)}), bf16[128,8,256]{2,1,0:T(8,128)(2,1)S(1)}, u32[]{:S(2)}, u32[]{:S(2)}) async-start(bf16[128,8,256]{2,1,0:T(8,128)(2,1)} %fusion.11), calls=%async_computation.1 | async-start | bytes 1048576 | tf_op jit(solution)/shard_map/all_to_all | solution.py:98
  114.0 0.0 copy-start.7
  114.0 2.7 %fusion.18 = (f32[256,1024]{0,1:T(8,128)S(1)}, bf16[128,8,256]{2,1,0:T(8,128)(2,1)}) fusion(f32[1024,256]{1,0:T(8,128)} %get-tuple-element.37, f32[1024]{0:T(1024)S(1)} %add_rsqrt_fusion, f32[1024]{0:T(1024)S(1)} %broadcast_multiply_fusion.2, bf16[1024,640]{1,0:T(8,128)(2,1)S(1)} %bitcast.41, f32[1024]{0:T(1024)S(1)} %get-tuple-element.38, ...), kind=kLoop, calls=%fused_computation.28 | loop fusion | flops 3145728 | bytes 3687424 | tf_op jit(solution)/shard_map/dot_general | solution.py:152
  116.6 0.0 copy-done.7
  116.6 0.1 pad_maximum_fusion
  116.7 1.0 reshape.160
  117.7 0.3 copy.37
  118.0 0.6 dot_general.35
  118.7 0.3 bitcast_reduce_fusion
  119.0 0.1 copy.50
  119.0 0.2 copy.48
  119.2 1.6 fusion.20
  120.8 7.1 %all-to-all-done.1 = bf16[128,8,256]{2,1,0:T(8,128)(2,1)S(1)} async-done(((bf16[128,8,256]{2,1,0:T(8,128)(2,1)}), bf16[128,8,256]{2,1,0:T(8,128)(2,1)S(1)}, u32[]{:S(2)}, u32[]{:S(2)}) %all-to-all-start.1) | async-done | bytes 524320 | tf_op jit(solution)/shard_map/all_to_all | solution.py:98
  128.0 0.0 copy-start.1
  128.0 18.5 %all_to_all.26 = bf16[128,2,1152]{2,1,0:T(2,128)(2,1)S(1)} all-to-all(bf16[128,2,1152]{2,1,0:T(2,128)(2,1)S(1)} %fusion.20), channel_id=1, replica_groups=mesh['gx'=16,'gy'=8] {'gx','gy'}, dimensions={0} | all-to-all | bytes 1179648 | tf_op jit(solution)/shard_map/all_to_all | solution.py:109
  146.5 4.0 %all-to-all-start.2 = ((bf16[128,8,256]{2,1,0:T(8,128)(2,1)}), bf16[128,8,256]{2,1,0:T(8,128)(2,1)S(1)}, u32[]{:S(2)}, u32[]{:S(2)}) async-start(bf16[128,8,256]{2,1,0:T(8,128)(2,1)} %get-tuple-element.36), calls=%async_computation.2 | async-start | bytes 1048576 | tf_op jit(solution)/shard_map/all_to_all | solution.py:98
  150.5 0.1 copy.49
  150.5 0.0 copy-done.1
  150.5 0.2 convolution_reduce_fusion
  150.8 13.7 %all-to-all-done.2 = bf16[128,8,256]{2,1,0:T(8,128)(2,1)S(1)} async-done(((bf16[128,8,256]{2,1,0:T(8,128)(2,1)}), bf16[128,8,256]{2,1,0:T(8,128)(2,1)S(1)}, u32[]{:S(2)}, u32[]{:S(2)}) %all-to-all-start.2) | async-done | bytes 524320 | tf_op jit(solution)/shard_map/all_to_all | solution.py:98
  164.5 0.0 copy-start.3
  164.5 1.1 broadcast_in_dim.11
  165.6 4.0 %all-to-all-start.4 = ((bf16[128,2,1152]{2,1,0:T(2,128)(2,1)}), bf16[128,2,1152]{2,1,0:T(2,128)(2,1)S(1)}, u32[]{:S(2)}, u32[]{:S(2)}) async-start(bf16[128,2,1152]{2,1,0:T(2,128)(2,1)} %broadcast_in_dim.11), calls=%async_computation.4 | async-start | bytes 1179648 | tf_op jit(solution)/shard_map/all_to_all | solution.py:115
  169.6 0.0 copy-done.3
  169.6 14.7 %all-to-all-done.4 = bf16[128,2,1152]{2,1,0:T(2,128)(2,1)S(1)} async-done(((bf16[128,2,1152]{2,1,0:T(2,128)(2,1)}), bf16[128,2,1152]{2,1,0:T(2,128)(2,1)S(1)}, u32[]{:S(2)}, u32[]{:S(2)}) %all-to-all-start.4) | async-done | bytes 589856 | tf_op jit(solution)/shard_map/all_to_all | solution.py:115
  184.3 0.4 slice.64
  184.7 0.7 reshape.163
  185.4 0.7 slice.66
  186.1 0.9 slice.65
  187.1 0.0 copy-start.2
  187.1 0.0 copy-start.4
  187.1 0.4 convert_element_type.64
  187.5 0.2 slice_reduce_fusion
  187.7 0.7 reshape_squeeze.4
  188.4 0.0 copy-done.2
  188.4 0.8 copy.53
  189.2 0.0 copy-done.4
  189.2 0.8 copy.54
  (5 shorter events, 0.0 us)
Async XLA Ops:
  0.6 39.5 %copy-start = (bf16[256,768]{1,0:T(8,128)(2,1)S(1)}, bf16[256,768]{1,0:T(8,128)(2,1)}, u32[]{:S(2)}) copy-start(bf16[256,768]{1,0:T(8,128)(2,1)} %param.14) | copy-start | bytes 1179652
  37.7 1.3 copy-start.6
  37.7 2.5 %copy-start.8 = (f32[256]{0:T(256)S(1)}, f32[256]{0:T(256)}, u32[]{:S(2)}) copy-start(f32[256]{0:T(256)} %param.13) | copy-start | bytes 3076
  103.6 1.5 copy-start.5
  103.6 2.7 %copy-start.9 = (bf16[3,256,1024]{2,1,0:T(8,128)(2,1)S(1)}, bf16[3,256,1024]{2,1,0:T(8,128)(2,1)}, u32[]{:S(2)}) copy-start(bf16[3,256,1024]{2,1,0:T(8,128)(2,1)} %get-tuple-element.32) | copy-start | bytes 4718596
  109.9 18.0 %all-to-all-start.1 = ((bf16[128,8,256]{2,1,0:T(8,128)(2,1)}), bf16[128,8,256]{2,1,0:T(8,128)(2,1)S(1)}, u32[]{:S(2)}, u32[]{:S(2)}) async-start(bf16[128,8,256]{2,1,0:T(8,128)(2,1)} %fusion.11), calls=%async_computation.1 | async-start | bytes 1048576 | tf_op jit(solution)/shard_map/all_to_all | solution.py:98
  114.0 2.7 %copy-start.7 = (bf16[256,768]{1,0:T(8,128)(2,1)S(1)}, bf16[256,768]{1,0:T(8,128)(2,1)}, u32[]{:S(2)}) copy-start(bf16[256,768]{1,0:T(8,128)(2,1)} %convolution_convert_fusion.2) | copy-start | bytes 1179652
  128.0 22.6 %copy-start.1 = (bf16[128,8,256]{2,1,0:T(8,128)(2,1)}, bf16[128,8,256]{2,1,0:T(8,128)(2,1)S(1)}, u32[]{:S(2)}) copy-start(bf16[128,8,256]{2,1,0:T(8,128)(2,1)S(1)} %all-to-all-done.1) | copy-start | bytes 1572868
  146.5 18.0 %all-to-all-start.2 = ((bf16[128,8,256]{2,1,0:T(8,128)(2,1)}), bf16[128,8,256]{2,1,0:T(8,128)(2,1)S(1)}, u32[]{:S(2)}, u32[]{:S(2)}) async-start(bf16[128,8,256]{2,1,0:T(8,128)(2,1)} %get-tuple-element.36), calls=%async_computation.2 | async-start | bytes 1048576 | tf_op jit(solution)/shard_map/all_to_all | solution.py:98
  164.5 5.2 %copy-start.3 = (bf16[128,8,256]{2,1,0:T(8,128)(2,1)}, bf16[128,8,256]{2,1,0:T(8,128)(2,1)S(1)}, u32[]{:S(2)}) copy-start(bf16[128,8,256]{2,1,0:T(8,128)(2,1)S(1)} %all-to-all-done.2) | copy-start | bytes 1572868
  165.6 18.7 %all-to-all-start.4 = ((bf16[128,2,1152]{2,1,0:T(2,128)(2,1)}), bf16[128,2,1152]{2,1,0:T(2,128)(2,1)S(1)}, u32[]{:S(2)}, u32[]{:S(2)}) async-start(bf16[128,2,1152]{2,1,0:T(2,128)(2,1)} %broadcast_in_dim.11), calls=%async_computation.4 | async-start | bytes 1179648 | tf_op jit(solution)/shard_map/all_to_all | solution.py:115
  187.1 1.3 copy-start.2
  187.1 2.1 %copy-start.4 = (bf16[128,8,256]{2,1,0:T(8,128)(2,1)S(1)}, bf16[128,8,256]{2,1,0:T(8,128)(2,1)}, u32[]{:S(2)}) copy-start(bf16[128,8,256]{2,1,0:T(8,128)(2,1)} %copy-done.3) | copy-start | bytes 1572868

commit v9 on v8

--- a/solution.py
+++ b/solution.py
@@ -7,8 +7,8 @@
 from jax.experimental.pallas import tpu as pltpu
 from jax.sharding import PartitionSpec as P
 
+
 HEADS = 16
-K = 1024
 TQ = 512
 
 
@@ -99,26 +99,7 @@
     return moved.reshape(array.shape)
 
 
-def sum_all(parts, scale):
-    size = lax.axis_size("gx") * lax.axis_size("gy")
-    matrix, vector = parts
-    rows, cols = matrix.shape
-    per = rows // size
-    side = jnp.zeros((size, per, 128), jnp.float32).at[:, :, 0].set(vector.reshape(size, per))
-    payload = jnp.concatenate([matrix.reshape(size, per, cols), side], 2)
-    moved = lax.all_to_all(
-        payload.astype(jnp.bfloat16), ("gx", "gy"), split_axis=0, concat_axis=0, tiled=True
-    )
-    ones = jnp.ones((1, size), jnp.bfloat16)
-    mine = jnp.dot(ones, moved.reshape(size, -1), preferred_element_type=jnp.float32) * scale
-    spread = jnp.broadcast_to(mine.astype(jnp.bfloat16).reshape((1,) + payload.shape[1:]), payload.shape)
-    total = lax.all_to_all(
-        spread, ("gx", "gy"), split_axis=0, concat_axis=0, tiled=True
-    ).astype(jnp.float32)
-    return total[:, :, :cols].reshape(rows, cols), total[:, :, cols].reshape(rows)
-
-
-def shards(features, valid, cotangent, gamma, w_qkv, w_out):
+def block(features, valid, cotangent, gamma, w_qkv, w_out):
     rows, width = features.shape
     nodes = rows * lax.axis_size("gx") * lax.axis_size("gy")
     inverse_root = float(nodes) ** (-0.5)
@@ -137,11 +118,18 @@
     ).astype(jnp.bfloat16)
     attnT, d_qkvT = fused_attention(qkvT.reshape(3, width, rows), d_attnT, keep_row, HEADS)
     d_qkvT = d_qkvT.reshape(3 * width, rows)
+    size = lax.axis_size("gx") * lax.axis_size("gy")
+    per_dev = rows // size
     y_val = (
         input_rows.astype(jnp.float32)
-        + lax.dot_general(attnT, w_out, (((0,), (0,)), ((), ())), preferred_element_type=jnp.float32)
+        + lax.dot_general(
+            attnT, w_out, (((0,), (0,)), ((), ())), preferred_element_type=jnp.float32
+        )
     ).astype(jnp.bfloat16)
-    y_plain = to_all(y_val)
+    y_plain = lax.all_to_all(
+        y_val.reshape(size, per_dev, width), ("gx", "gy"), split_axis=0, concat_axis=0,
+        tiled=True,
+    ).reshape(rows, width)
     local_wout = jnp.dot(attnT, gt, preferred_element_type=jnp.float32)
     local_wqkv = lax.dot_general(
         hidden_state, d_qkvT, (((0,), (1,)), ((), ())), preferred_element_type=jnp.float32
@@ -155,6 +143,14 @@
         precision=lax.Precision.HIGHEST,
         preferred_element_type=jnp.float32,
     )[0]
+    matrix = jnp.concatenate([local_wqkv, local_wout], 1)
+    cols = matrix.shape[1]
+    per = width // size
+    side = jnp.zeros((size, per, 128), jnp.float32).at[:, :, 0].set(shard_gamma.reshape(size, per))
+    payload = jnp.concatenate([matrix.reshape(size, per, cols), side], 2)
+    moved = lax.all_to_all(
+        payload.astype(jnp.bfloat16), ("gx", "gy"), split_axis=0, concat_axis=0, tiled=True
+    )
     scaled_output = hidden_gradient * gamma
     norm_gradient = reciprocal_deviation * (
         scaled_output
@@ -162,10 +158,22 @@
         - normalized_input * jnp.mean(scaled_output * normalized_input, -1, keepdims=True)
     )
     d_x = (gt.astype(jnp.float32) + norm_gradient).astype(jnp.bfloat16)
-    total_w, total_gamma = sum_all(
-        (jnp.concatenate([local_wqkv, local_wout], 1), shard_gamma), inverse_root
+    back = lax.all_to_all(
+        d_x.reshape(size, per_dev, width), ("gx", "gy"), split_axis=0, concat_axis=0,
+        tiled=True,
     )
-    dx_plain = to_all(d_x)
+    dx_plain = back.reshape(rows, width)
+    ones = jnp.ones((1, size), jnp.bfloat16)
+    mine = jnp.dot(ones, moved.reshape(size, -1), preferred_element_type=jnp.float32)
+    mine = mine * inverse_root
+    spread = jnp.broadcast_to(
+        mine.astype(jnp.bfloat16).reshape((1,) + payload.shape[1:]), payload.shape
+    )
+    total = lax.all_to_all(
+        spread, ("gx", "gy"), split_axis=0, concat_axis=0, tiled=True
+    ).astype(jnp.float32)
+    total_w = total[:, :, :cols].reshape(width, cols)
+    total_gamma = total[:, :, cols].reshape(width)
     return (
         y_plain,
         dx_plain,
@@ -178,7 +186,7 @@
 def solution(mesh):
     placed = (P(("gx", "gy"), None), P(("gx", "gy")), P(("gx", "gy"), None), P(), P(), P())
     return jax.shard_map(
-        shards,
+        block,
         mesh=mesh,
         in_specs=placed,
         out_specs=(P(("gx", "gy"), None), P(("gx", "gy"), None), P(), P(), P()),

time: 190 us -> 190 us (level)
  no operation moved by 1% of the time
where the time goes in v9:
time: 190 us
  Pallas kernels  61.4 us (32%)
  blocking collectives  52 us (27%)
  waiting for transfers between devices  35.5 us (19%)
  starting transfers between devices  12 us (6%)
  matrix products  9.7 us (5%)
  other arithmetic  9.63 us (5%)
  local copies, waits for them, and re-layouts  8.87 us (5%)
    pallas_call x1, Pallas kernels, fused_attention(): pl.pallas_call(kernel, grid=(heads // group,), in_specs=[pl.BlockSpec((3,...  61.4 us
    all_to_all x1, blocking collectives, to_all(): lax.all_to_all(shaped, ('gx', 'gy'), split_axis=0, concat_axis=0, tiled=T...  33.5 us
    all_to_all x1, blocking collectives, block(): lax.all_to_all(payload.astype(jnp.bfloat16), ('gx', 'gy'), split_axis=0,...  18.5 us
    all_to_all x1, waiting for transfers between devices, block(): lax.all_to_all(spread, ('gx', 'gy'), split_axis=0, concat_axis=0, tiled=T...  14.7 us
    all_to_all x1, waiting for transfers between devices, block(): lax.all_to_all(d_x.reshape(size, per_dev, width), ('gx', 'gy'), split_axi...  13.7 us
    all_to_all x1, waiting for transfers between devices, block(): lax.all_to_all(y_val.reshape(size, per_dev, width), ('gx', 'gy'), split_a...  7.14 us
    all_to_all x1, starting transfers between devices, block(): lax.all_to_all(spread, ('gx', 'gy'), split_axis=0, concat_axis=0, tiled=T...  4.02 us
    all_to_all x1, starting transfers between devices, block(): lax.all_to_all(y_val.reshape(size, per_dev, width), ('gx', 'gy'), split_a...  4.01 us
  transfers between devices with their start and end apart: 3, of which 3 were waited for; matrix products, arithmetic and copies ran while one was open for 4% of the time, Pallas kernels for 0%

profile of v9, /device:TPU:1, one launch (start us, length us, event | category | flops | bytes accessed | tf_op | source)
XLA Modules:
  0.0 190.0 jit_solution(1188081337678859156)
XLA Ops:
  0.6 0.0 copy-start
  0.6 0.6 compare_reduce_fusion
  1.3 1.3 convert_select_fusion
  2.6 0.2 reshape.169
  2.8 1.3 fusion.2
  4.1 33.5 %all_to_all.25 = bf16[128,8,640]{2,1,0:T(8,128)(2,1)S(1)} all-to-all(bf16[128,8,640]{2,1,0:T(8,128)(2,1)S(1)} %fusion.2), channel_id=1, replica_groups=mesh['gx'=16,'gy'=8] {'gx','gy'}, dimensions={0} | all-to-all | bytes 2621440 | tf_op jit(solution)/shard_map/all_to_all | solution.py:98
  37.7 0.0 copy-start.6
  37.7 0.0 copy-start.8
  37.7 0.7 convert_reduce_fusion.1
  38.4 0.2 convert_reduce_fusion
  38.6 0.4 fusion.19
  39.0 0.0 copy-done.6
  39.0 1.1 fusion.10.do_ref
  40.2 0.0 copy-done
  40.2 0.0 copy-done.8
  40.2 2.1 %convolution_convert_fusion = bf16[1024,768]{0,1:T(8,128)(2,1)} fusion(bf16[256,768]{1,0:T(8,128)(2,1)S(1)} %copy-done, f32[256]{0:T(256)S(1)} %copy-done.8, f32[1024]{0:T(1024)S(1)} %add_rsqrt_fusion, f32[1024]{0:T(1024)S(1)} %broadcast_multiply_fusion.2, bf16[1024,640]{1,0:T(8,128)(2,1)S(1)} %bitcast.36), kind=kOutput, calls=%fused_computation.3 | convolution fusion | flops 404750336 | bytes 2499584 | tf_op jit(solution)/shard_map/dot_general | solution.py:112
  42.2 61.4 %shard_map.101 = (bf16[256,1024]{1,0:T(8,128)(2,1)}, bf16[3,256,1024]{2,1,0:T(8,128)(2,1)}) custom-call(bf16[3,256,1024]{2,1,0:T(8,128)(2,1)} %bitcast.50, bf16[256,1024]{1,0:T(8,128)(2,1)} %fusion.10.do_ref, f32[1,1024]{1,0:T(1,128)} %bitcast.46), custom_call_target="tpu_custom_call" | custom-call | flops 3221225472 | bytes 4194304 | tf_op jit(solution)/shard_map/pallas_call | solution.py:72
  103.6 0.0 copy-start.5
  103.6 0.0 copy-start.9
  103.6 1.5 convolution_convert_fusion.3
  105.1 0.0 copy-done.5
  105.1 1.2 fusion.11
  106.3 0.0 copy-done.9
  106.3 1.7 convolution_convert_fusion.2
  108.0 2.0 %multiply_reduce_fusion = (f32[1024]{0:T(1024)S(1)}, f32[1024]{0:T(1024)S(1)}, f32[1024,256]{1,0:T(8,128)}) fusion(f32[256]{0:T(256)S(1)} %copy-done.8, f32[1024]{0:T(1024)S(1)} %add_rsqrt_fusion, f32[1024]{0:T(1024)S(1)} %broadcast_multiply_fusion.2, bf16[1024,640]{1,0:T(8,128)(2,1)S(1)} %bitcast.40, bf16[768,1024]{1,0:T(8,128)(2,1)S(1)} %bitcast.49, ...), kind=kOutput, calls=%fused_computation.31 | convolution fusion | flops 404486144 | bytes 3556352 | tf_op jit(solution)/shard_map/dot_general | solution.py:137
  109.9 4.0 %all-to-all-start.1 = ((bf16[128,8,256]{2,1,0:T(8,128)(2,1)}), bf16[128,8,256]{2,1,0:T(8,128)(2,1)S(1)}, u32[]{:S(2)}, u32[]{:S(2)}) async-start(bf16[128,8,256]{2,1,0:T(8,128)(2,1)} %fusion.11), calls=%async_computation.1 | async-start | bytes 1048576 | tf_op jit(solution)/shard_map/all_to_all | solution.py:129
  114.0 0.0 copy-start.7
  114.0 2.7 %fusion.18 = (f32[256,1024]{0,1:T(8,128)S(1)}, bf16[128,8,256]{2,1,0:T(8,128)(2,1)}) fusion(f32[1024,256]{1,0:T(8,128)} %get-tuple-element.37, f32[1024]{0:T(1024)S(1)} %add_rsqrt_fusion, f32[1024]{0:T(1024)S(1)} %broadcast_multiply_fusion.2, bf16[1024,640]{1,0:T(8,128)(2,1)S(1)} %bitcast.41, f32[1024]{0:T(1024)S(1)} %get-tuple-element.38, ...), kind=kLoop, calls=%fused_computation.28 | loop fusion | flops 3145728 | bytes 3687424 | tf_op jit(solution)/shard_map/dot_general | solution.py:140
  116.6 0.0 copy-done.7
  116.6 0.1 pad_maximum_fusion
  116.7 1.0 reshape.160
  117.7 0.3 copy.37
  118.0 0.6 dot_general.35
  118.7 0.3 bitcast_reduce_fusion
  119.0 0.1 copy.50
  119.0 0.2 copy.48
  119.2 1.6 fusion.20
  120.8 7.1 %all-to-all-done.1 = bf16[128,8,256]{2,1,0:T(8,128)(2,1)S(1)} async-done(((bf16[128,8,256]{2,1,0:T(8,128)(2,1)}), bf16[128,8,256]{2,1,0:T(8,128)(2,1)S(1)}, u32[]{:S(2)}, u32[]{:S(2)}) %all-to-all-start.1) | async-done | bytes 524320 | tf_op jit(solution)/shard_map/all_to_all | solution.py:129
  128.0 0.0 copy-start.1
  128.0 18.5 %all_to_all.26 = bf16[128,2,1152]{2,1,0:T(2,128)(2,1)S(1)} all-to-all(bf16[128,2,1152]{2,1,0:T(2,128)(2,1)S(1)} %fusion.20), channel_id=1, replica_groups=mesh['gx'=16,'gy'=8] {'gx','gy'}, dimensions={0} | all-to-all | bytes 1179648 | tf_op jit(solution)/shard_map/all_to_all | solution.py:151
  146.5 4.0 %all-to-all-start.2 = ((bf16[128,8,256]{2,1,0:T(8,128)(2,1)}), bf16[128,8,256]{2,1,0:T(8,128)(2,1)S(1)}, u32[]{:S(2)}, u32[]{:S(2)}) async-start(bf16[128,8,256]{2,1,0:T(8,128)(2,1)} %get-tuple-element.36), calls=%async_computation.2 | async-start | bytes 1048576 | tf_op jit(solution)/shard_map/all_to_all | solution.py:161
  150.5 0.1 copy.49
  150.5 0.0 copy-done.1
  150.5 0.2 convolution_reduce_fusion
  150.8 13.7 %all-to-all-done.2 = bf16[128,8,256]{2,1,0:T(8,128)(2,1)S(1)} async-done(((bf16[128,8,256]{2,1,0:T(8,128)(2,1)}), bf16[128,8,256]{2,1,0:T(8,128)(2,1)S(1)}, u32[]{:S(2)}, u32[]{:S(2)}) %all-to-all-start.2) | async-done | bytes 524320 | tf_op jit(solution)/shard_map/all_to_all | solution.py:161
  164.5 0.0 copy-start.3
  164.5 1.1 broadcast_in_dim.11
  165.6 4.0 %all-to-all-start.4 = ((bf16[128,2,1152]{2,1,0:T(2,128)(2,1)}), bf16[128,2,1152]{2,1,0:T(2,128)(2,1)S(1)}, u32[]{:S(2)}, u32[]{:S(2)}) async-start(bf16[128,2,1152]{2,1,0:T(2,128)(2,1)} %broadcast_in_dim.11), calls=%async_computation.4 | async-start | bytes 1179648 | tf_op jit(solution)/shard_map/all_to_all | solution.py:172
  169.6 0.0 copy-done.3
  169.6 14.7 %all-to-all-done.4 = bf16[128,2,1152]{2,1,0:T(2,128)(2,1)S(1)} async-done(((bf16[128,2,1152]{2,1,0:T(2,128)(2,1)}), bf16[128,2,1152]{2,1,0:T(2,128)(2,1)S(1)}, u32[]{:S(2)}, u32[]{:S(2)}) %all-to-all-start.4) | async-done | bytes 589856 | tf_op jit(solution)/shard_map/all_to_all | solution.py:172
  184.3 0.4 slice.64
  184.7 0.7 reshape.163
  185.4 0.7 slice.66
  186.1 0.9 slice.65
  187.1 0.0 copy-start.2
  187.1 0.0 copy-start.4
  187.1 0.4 convert_element_type.64
  187.5 0.2 slice_reduce_fusion
  187.7 0.7 reshape_squeeze.4
  188.4 0.0 copy-done.2
  188.4 0.8 copy.53
  189.2 0.0 copy-done.4
  189.2 0.8 copy.54
  (5 shorter events, 0.0 us)
Async XLA Ops:
  0.6 39.5 %copy-start = (bf16[256,768]{1,0:T(8,128)(2,1)S(1)}, bf16[256,768]{1,0:T(8,128)(2,1)}, u32[]{:S(2)}) copy-start(bf16[256,768]{1,0:T(8,128)(2,1)} %param.14) | copy-start | bytes 1179652
  37.7 1.3 copy-start.6
  37.7 2.5 %copy-start.8 = (f32[256]{0:T(256)S(1)}, f32[256]{0:T(256)}, u32[]{:S(2)}) copy-start(f32[256]{0:T(256)} %param.13) | copy-start | bytes 3076
  103.6 1.5 copy-start.5
  103.6 2.7 %copy-start.9 = (bf16[3,256,1024]{2,1,0:T(8,128)(2,1)S(1)}, bf16[3,256,1024]{2,1,0:T(8,128)(2,1)}, u32[]{:S(2)}) copy-start(bf16[3,256,1024]{2,1,0:T(8,128)(2,1)} %get-tuple-element.32) | copy-start | bytes 4718596
  109.9 18.0 %all-to-all-start.1 = ((bf16[128,8,256]{2,1,0:T(8,128)(2,1)}), bf16[128,8,256]{2,1,0:T(8,128)(2,1)S(1)}, u32[]{:S(2)}, u32[]{:S(2)}) async-start(bf16[128,8,256]{2,1,0:T(8,128)(2,1)} %fusion.11), calls=%async_computation.1 | async-start | bytes 1048576 | tf_op jit(solution)/shard_map/all_to_all | solution.py:129
  114.0 2.7 %copy-start.7 = (bf16[256,768]{1,0:T(8,128)(2,1)S(1)}, bf16[256,768]{1,0:T(8,128)(2,1)}, u32[]{:S(2)}) copy-start(bf16[256,768]{1,0:T(8,128)(2,1)} %convolution_convert_fusion.2) | copy-start | bytes 1179652
  128.0 22.6 %copy-start.1 = (bf16[128,8,256]{2,1,0:T(8,128)(2,1)}, bf16[128,8,256]{2,1,0:T(8,128)(2,1)S(1)}, u32[]{:S(2)}) copy-start(bf16[128,8,256]{2,1,0:T(8,128)(2,1)S(1)} %all-to-all-done.1) | copy-start | bytes 1572868
  146.5 18.0 %all-to-all-start.2 = ((bf16[128,8,256]{2,1,0:T(8,128)(2,1)}), bf16[128,8,256]{2,1,0:T(8,128)(2,1)S(1)}, u32[]{:S(2)}, u32[]{:S(2)}) async-start(bf16[128,8,256]{2,1,0:T(8,128)(2,1)} %get-tuple-element.36), calls=%async_computation.2 | async-start | bytes 1048576 | tf_op jit(solution)/shard_map/all_to_all | solution.py:161
  164.5 5.2 %copy-start.3 = (bf16[128,8,256]{2,1,0:T(8,128)(2,1)}, bf16[128,8,256]{2,1,0:T(8,128)(2,1)S(1)}, u32[]{:S(2)}) copy-start(bf16[128,8,256]{2,1,0:T(8,128)(2,1)S(1)} %all-to-all-done.2) | copy-start | bytes 1572868
  165.6 18.7 %all-to-all-start.4 = ((bf16[128,2,1152]{2,1,0:T(2,128)(2,1)}), bf16[128,2,1152]{2,1,0:T(2,128)(2,1)S(1)}, u32[]{:S(2)}, u32[]{:S(2)}) async-start(bf16[128,2,1152]{2,1,0:T(2,128)(2,1)} %broadcast_in_dim.11), calls=%async_computation.4 | async-start | bytes 1179648 | tf_op jit(solution)/shard_map/all_to_all | solution.py:172
  187.1 1.3 copy-start.2
  187.1 2.1 %copy-start.4 = (bf16[128,8,256]{2,1,0:T(8,128)(2,1)S(1)}, bf16[128,8,256]{2,1,0:T(8,128)(2,1)}, u32[]{:S(2)}) copy-start(bf16[128,8,256]{2,1,0:T(8,128)(2,1)} %copy-done.3) | copy-start | bytes 1572868

commit v10 on v9

--- a/solution.py
+++ b/solution.py
@@ -66,7 +66,7 @@
     _, c, n = qkvT.shape
     d = c // heads
     scale = d ** (-0.5)
-    group = 2
+    group = 4
     kernel = functools.partial(_attn_kernel, scale=scale, n=n, tq=TQ, d=d, group=group)
     flops = heads * 6 * 2 * n * n * d
     return pl.pallas_call(
@@ -118,18 +118,6 @@
     ).astype(jnp.bfloat16)
     attnT, d_qkvT = fused_attention(qkvT.reshape(3, width, rows), d_attnT, keep_row, HEADS)
     d_qkvT = d_qkvT.reshape(3 * width, rows)
-    size = lax.axis_size("gx") * lax.axis_size("gy")
-    per_dev = rows // size
-    y_val = (
-        input_rows.astype(jnp.float32)
-        + lax.dot_general(
-            attnT, w_out, (((0,), (0,)), ((), ())), preferred_element_type=jnp.float32
-        )
-    ).astype(jnp.bfloat16)
-    y_plain = lax.all_to_all(
-        y_val.reshape(size, per_dev, width), ("gx", "gy"), split_axis=0, concat_axis=0,
-        tiled=True,
-    ).reshape(rows, width)
     local_wout = jnp.dot(attnT, gt, preferred_element_type=jnp.float32)
     local_wqkv = lax.dot_general(
         hidden_state, d_qkvT, (((0,), (1,)), ((), ())), preferred_element_type=jnp.float32
@@ -143,6 +131,7 @@
         precision=lax.Precision.HIGHEST,
         preferred_element_type=jnp.float32,
     )[0]
+    size = lax.axis_size("gx") * lax.axis_size("gy")
     matrix = jnp.concatenate([local_wqkv, local_wout], 1)
     cols = matrix.shape[1]
     per = width // size
@@ -151,6 +140,12 @@
     moved = lax.all_to_all(
         payload.astype(jnp.bfloat16), ("gx", "gy"), split_axis=0, concat_axis=0, tiled=True
     )
+    y_val = (
+        input_rows.astype(jnp.float32)
+        + lax.dot_general(
+            attnT, w_out, (((0,), (0,)), ((), ())), preferred_element_type=jnp.float32
+        )
+    ).astype(jnp.bfloat16)
     scaled_output = hidden_gradient * gamma
     norm_gradient = reciprocal_deviation * (
         scaled_output
@@ -158,11 +153,13 @@
         - normalized_input * jnp.mean(scaled_output * normalized_input, -1, keepdims=True)
     )
     d_x = (gt.astype(jnp.float32) + norm_gradient).astype(jnp.bfloat16)
-    back = lax.all_to_all(
-        d_x.reshape(size, per_dev, width), ("gx", "gy"), split_axis=0, concat_axis=0,
-        tiled=True,
+    per_dev = rows // size
+    both = jnp.concatenate(
+        [d_x.reshape(size, per_dev, width), y_val.reshape(size, per_dev, width)], 1
     )
-    dx_plain = back.reshape(rows, width)
+    back = lax.all_to_all(both, ("gx", "gy"), split_axis=0, concat_axis=0, tiled=True)
+    dx_plain = back[:, :per_dev].reshape(rows, width)
+    y_plain = back[:, per_dev:].reshape(rows, width)
     ones = jnp.ones((1, size), jnp.bfloat16)
     mine = jnp.dot(ones, moved.reshape(size, -1), preferred_element_type=jnp.float32)
     mine = mine * inverse_root

time: 190 us -> 182 us (0.958)
  blocking collectives: 52 us -> 33.5 us
  waiting for transfers between devices: 35.5 us -> 44.6 us
    all_to_all x1 -> x0, blocking collectives: 18.5 us -> none  [block(): lax.all_to_all(payload.astype(jnp.bfloat16), ('gx', 'gy'), split_axis=0,...]
    all_to_all x2, waiting for transfers between devices: 20.8 us -> 30.9 us  [the longest x1 19.2 us: block(): lax.all_to_all(both, ('gx', 'gy'), split_axis=0, concat_axis=0, tiled=True)]
  transfers between devices with their start and end apart: 3 -> 3, of which waited for: 3 -> 3; matrix products, arithmetic and copies ran while one was open for 4% -> 2% of each run, Pallas kernels for 0% -> 0%
where the time goes in v10:
time: 182 us; the launch traced here: 181 us
  Pallas kernels  60.5 us (33%)
  waiting for transfers between devices  44.6 us (25%)
  blocking collectives  33.5 us (18%)
  starting transfers between devices  11.9 us (7%)
  local copies, waits for them, and re-layouts  10.6 us (6%)
  other arithmetic  10 us (5%)
  matrix products  9.46 us (5%)
    pallas_call x1, Pallas kernels, fused_attention(): pl.pallas_call(kernel, grid=(heads // group,), in_specs=[pl.BlockSpec((3,...  60.5 us
    all_to_all x1, blocking collectives, to_all(): lax.all_to_all(shaped, ('gx', 'gy'), split_axis=0, concat_axis=0, tiled=T...  33.5 us
    all_to_all x1, waiting for transfers between devices, block(): lax.all_to_all(both, ('gx', 'gy'), split_axis=0, concat_axis=0, tiled=True)  19.2 us
    all_to_all x1, waiting for transfers between devices, block(): lax.all_to_all(spread, ('gx', 'gy'), split_axis=0, concat_axis=0, tiled=T...  13.7 us
    all_to_all x1, waiting for transfers between devices, block(): lax.all_to_all(payload.astype(jnp.bfloat16), ('gx', 'gy'), split_axis=0,...  11.7 us
    all_to_all x1, starting transfers between devices, block(): lax.all_to_all(payload.astype(jnp.bfloat16), ('gx', 'gy'), split_axis=0,...  4.01 us
    all_to_all x1, starting transfers between devices, block(): lax.all_to_all(both, ('gx', 'gy'), split_axis=0, concat_axis=0, tiled=True)  3.99 us
    all_to_all x1, starting transfers between devices, block(): lax.all_to_all(spread, ('gx', 'gy'), split_axis=0, concat_axis=0, tiled=T...  3.91 us
  transfers between devices with their start and end apart: 3, of which 3 were waited for; matrix products, arithmetic and copies ran while one was open for 2% of the time, Pallas kernels for 0%

profile of v10, /device:TPU:1, one launch (start us, length us, event | category | flops | bytes accessed | tf_op | source)
XLA Modules:
  0.0 181.4 jit_solution(15161768529763459474)
XLA Ops:
  0.6 0.0 copy-start
  0.6 0.6 compare_reduce_fusion
  1.3 1.3 convert_select_fusion
  2.6 0.2 reshape.169
  2.8 1.3 fusion.2
  4.1 33.5 %all_to_all.20 = bf16[128,8,640]{2,1,0:T(8,128)(2,1)S(1)} all-to-all(bf16[128,8,640]{2,1,0:T(8,128)(2,1)S(1)} %fusion.2), channel_id=1, replica_groups=mesh['gx'=16,'gy'=8] {'gx','gy'}, dimensions={0} | all-to-all | bytes 2621440 | tf_op jit(solution)/shard_map/all_to_all | solution.py:98
  37.7 0.0 copy-start.4
  37.7 0.7 convert_reduce_fusion.1
  38.4 0.1 fusion.26
  38.5 0.1 copy-done.4
  38.6 1.1 fusion.10.do_ref
  39.7 0.0 copy-start.7
  39.7 0.2 copy.56
  39.9 0.1 convert_reduce_fusion
  40.0 0.2 fusion.18
  40.2 0.0 copy-done
  40.2 0.2 copy-done.7
  40.4 1.8 %convolution_convert_fusion = bf16[1024,768]{0,1:T(8,128)(2,1)} fusion(bf16[256,768]{1,0:T(8,128)(2,1)S(1)} %copy-done, bf16[1024,256]{0,1:T(8,128)(2,1)S(1)} %copy.56, f32[256]{0:T(256)S(1)} %copy-done.7, f32[1024]{0:T(1024)S(1)} %add_rsqrt_fusion, f32[1024]{0:T(1024)S(1)} %broadcast_multiply_fusion.2), kind=kOutput, calls=%fused_computation.3 | convolution fusion | flops 404750336 | bytes 2499584 | tf_op jit(solution)/shard_map/dot_general | solution.py:112
  42.2 60.5 %shard_map.101 = (bf16[256,1024]{1,0:T(8,128)(2,1)}, bf16[3,256,1024]{2,1,0:T(8,128)(2,1)}) custom-call(bf16[3,256,1024]{2,1,0:T(8,128)(2,1)} %bitcast.40, bf16[256,1024]{1,0:T(8,128)(2,1)} %fusion.10.do_ref, f32[1,1024]{1,0:T(1,128)} %bitcast.41), custom_call_target="tpu_custom_call" | custom-call | flops 3221225472 | bytes 4194304 | tf_op jit(solution)/shard_map/pallas_call | solution.py:72
  102.7 0.0 copy-start.8
  102.7 2.9 %convolution_convert_fusion.2 = bf16[256,768]{1,0:T(8,128)(2,1)} fusion(bf16[768,1024]{1,0:T(8,128)(2,1)} %bitcast.43, bf16[1024,256]{0,1:T(8,128)(2,1)S(1)} %copy.56, f32[256]{0:T(256)S(1)} %copy-done.7, f32[1024]{0:T(1024)S(1)} %add_rsqrt_fusion, f32[1024]{0:T(1024)S(1)} %broadcast_multiply_fusion.2), kind=kOutput, calls=%fused_computation.11 | convolution fusion | flops 404160512 | bytes 2499584 | tf_op jit(solution)/shard_map/dot_general | solution.py:122
  105.6 0.0 copy-done.8
  105.6 0.0 copy-start.3
  105.6 1.6 multiply_reduce_fusion
  107.3 1.0 copy.55
  108.3 0.0 copy-start.6
  108.3 0.0 copy-done.3
  108.3 0.3 convolution_convert_fusion.3
  108.6 0.7 copy-done.6
  109.3 0.0 copy-start.2
  109.3 0.1 pad_maximum_fusion.1
  109.3 0.2 reshape.160
  109.6 0.8 copy-done.2
  110.3 2.5 %fusion.17 = (f32[256,1024]{1,0:T(8,128)S(1)}, bf16[1024,256]{0,1:T(8,128)(2,1)}) fusion(f32[1024,256]{0,1:T(8,128)} %get-tuple-element.41, bf16[1024,256]{0,1:T(8,128)(2,1)S(1)} %copy.56, f32[1024]{0:T(1024)S(1)} %add_rsqrt_fusion, f32[1024]{0:T(1024)S(1)} %broadcast_multiply_fusion.2, f32[1024]{0:T(1024)S(1)} %get-tuple-element.42, ...), kind=kLoop, calls=%fused_computation.27 | loop fusion | flops 3145728 | bytes 3687424 | tf_op jit(solution)/shard_map/dot_general | solution.py:128
  112.8 0.6 dot_general.35
  113.4 0.3 bitcast_reduce_fusion
  113.7 0.0 copy-start.5
  113.7 0.1 copy.60
  113.8 0.2 copy.58
  114.0 1.4 fusion.19
  115.4 4.0 %all-to-all-start.2 = ((bf16[128,2,1152]{2,1,0:T(2,128)(2,1)}), bf16[128,2,1152]{2,1,0:T(2,128)(2,1)S(1)}, u32[]{:S(2)}, u32[]{:S(2)}) async-start(bf16[128,2,1152]{2,1,0:T(2,128)(2,1)} %fusion.19), calls=%async_computation.2 | async-start | bytes 1179648 | tf_op jit(solution)/shard_map/all_to_all | solution.py:140
  119.4 0.0 copy-done.5
  119.4 0.0 copy-start.1
  119.4 1.4 fusion.3
  120.8 0.2 copy.44
  121.0 0.0 copy-done.1
  121.1 0.2 copy.42
  121.3 1.1 pad_maximum_fusion
  122.3 11.7 %all-to-all-done.2 = bf16[128,2,1152]{2,1,0:T(2,128)(2,1)S(1)} async-done(((bf16[128,2,1152]{2,1,0:T(2,128)(2,1)}), bf16[128,2,1152]{2,1,0:T(2,128)(2,1)S(1)}, u32[]{:S(2)}, u32[]{:S(2)}) %all-to-all-start.2) | async-done | bytes 589856 | tf_op jit(solution)/shard_map/all_to_all | solution.py:140
  134.1 4.0 %all-to-all-start.1 = ((bf16[128,16,256]{2,1,0:T(8,128)(2,1)}), bf16[128,16,256]{2,1,0:T(8,128)(2,1)S(1)}, u32[]{:S(2)}, u32[]{:S(2)}) async-start(bf16[128,16,256]{2,1,0:T(8,128)(2,1)} %pad_maximum_fusion), calls=%async_computation.1 | async-start | bytes 2097152 | tf_op jit(solution)/shard_map/all_to_all | solution.py:160
  138.1 0.1 copy.59
  138.1 0.2 convolution_reduce_fusion
  138.4 19.2 %all-to-all-done.1 = bf16[128,16,256]{2,1,0:T(8,128)(2,1)S(1)} async-done(((bf16[128,16,256]{2,1,0:T(8,128)(2,1)}), bf16[128,16,256]{2,1,0:T(8,128)(2,1)S(1)}, u32[]{:S(2)}, u32[]{:S(2)}) %all-to-all-start.1) | async-done | bytes 1048608 | tf_op jit(solution)/shard_map/all_to_all | solution.py:160
  157.6 1.1 broadcast_in_dim.11
  158.7 3.9 %all-to-all-start.3 = ((bf16[128,2,1152]{2,1,0:T(2,128)(2,1)}), bf16[128,2,1152]{2,1,0:T(2,128)(2,1)S(1)}, u32[]{:S(2)}, u32[]{:S(2)}) async-start(bf16[128,2,1152]{2,1,0:T(2,128)(2,1)} %broadcast_in_dim.11), calls=%async_computation.3 | async-start | bytes 1179648 | tf_op jit(solution)/shard_map/all_to_all | solution.py:169
  162.6 1.0 slice_bitcast_fusion
  163.6 13.7 %all-to-all-done.3 = bf16[128,2,1152]{2,1,0:T(2,128)(2,1)S(1)} async-done(((bf16[128,2,1152]{2,1,0:T(2,128)(2,1)}), bf16[128,2,1152]{2,1,0:T(2,128)(2,1)S(1)}, u32[]{:S(2)}, u32[]{:S(2)}) %all-to-all-start.3) | async-done | bytes 589856 | tf_op jit(solution)/shard_map/all_to_all | solution.py:169
  177.4 0.4 slice.74
  177.7 0.7 reshape.163
  178.4 0.7 slice.76
  179.2 0.9 slice.75
  180.1 0.4 convert_element_type.64
  180.5 0.2 slice_reduce_fusion
  180.7 0.7 reshape_squeeze.4
  (5 shorter events, 0.0 us)
Async XLA Ops:
  0.6 39.6 %copy-start = (bf16[256,768]{1,0:T(8,128)(2,1)S(1)}, bf16[256,768]{1,0:T(8,128)(2,1)}, u32[]{:S(2)}) copy-start(bf16[256,768]{1,0:T(8,128)(2,1)} %param.14) | copy-start | bytes 1179652
  37.7 0.9 copy-start.4
  39.7 0.7 copy-start.7
  102.7 2.9 %copy-start.8 = (bf16[3,256,1024]{2,1,0:T(8,128)(2,1)S(1)}, bf16[3,256,1024]{2,1,0:T(8,128)(2,1)}, u32[]{:S(2)}) copy-start(bf16[3,256,1024]{2,1,0:T(8,128)(2,1)} %get-tuple-element.31) | copy-start | bytes 4718596
  105.6 2.6 %copy-start.3 = (bf16[256,1024]{1,0:T(8,128)(2,1)S(1)}, bf16[256,1024]{1,0:T(8,128)(2,1)}, u32[]{:S(2)}) copy-start(bf16[256,1024]{1,0:T(8,128)(2,1)} %get-tuple-element.32) | copy-start | bytes 1572868
  108.3 1.0 copy-start.6
  109.3 1.0 copy-start.2
  113.7 5.7 %copy-start.5 = (bf16[256,256]{1,0:T(8,128)(2,1)S(1)}, bf16[256,256]{1,0:T(8,128)(2,1)}, u32[]{:S(2)}) copy-start(bf16[256,256]{1,0:T(8,128)(2,1)} %param.15) | copy-start | bytes 393220
  115.4 18.7 %all-to-all-start.2 = ((bf16[128,2,1152]{2,1,0:T(2,128)(2,1)}), bf16[128,2,1152]{2,1,0:T(2,128)(2,1)S(1)}, u32[]{:S(2)}, u32[]{:S(2)}) async-start(bf16[128,2,1152]{2,1,0:T(2,128)(2,1)} %fusion.19), calls=%async_computation.2 | async-start | bytes 1179648 | tf_op jit(solution)/shard_map/all_to_all | solution.py:140
  119.4 1.7 copy-start.1
  134.1 23.5 %all-to-all-start.1 = ((bf16[128,16,256]{2,1,0:T(8,128)(2,1)}), bf16[128,16,256]{2,1,0:T(8,128)(2,1)S(1)}, u32[]{:S(2)}, u32[]{:S(2)}) async-start(bf16[128,16,256]{2,1,0:T(8,128)(2,1)} %pad_maximum_fusion), calls=%async_computation.1 | async-start | bytes 2097152 | tf_op jit(solution)/shard_map/all_to_all | solution.py:160
  158.7 18.7 %all-to-all-start.3 = ((bf16[128,2,1152]{2,1,0:T(2,128)(2,1)}), bf16[128,2,1152]{2,1,0:T(2,128)(2,1)S(1)}, u32[]{:S(2)}, u32[]{:S(2)}) async-start(bf16[128,2,1152]{2,1,0:T(2,128)(2,1)} %broadcast_in_dim.11), calls=%async_computation.3 | async-start | bytes 1179648 | tf_op jit(solution)/shard_map/all_to_all | solution.py:169
